TPU v7x, 256 devices: a whole 4x4x8 slice. The times are simulated.
256 devices in a mesh: dp: 64 (over y, z, core), mp: 4 (over x).
Axes of the slice: x: 4, y: 4, z: 8, core: 2. Of those that a mesh axis runs over, the one named last changes fastest.
Arguments:
- queries: bfloat16 [32768, 1024], P('dp', 'mp'), may hold values from -20 to 20
- passages: bfloat16 [262144, 1024], P('dp', 'mp'), may hold values from -6 to 6
- positives: int32 [32768], P('dp'), may hold values from 0 to 4095, as said below
- negatives: int32 [64, 64], replicated, may hold values from -1 to 31, as said below
Outputs:
- losses: float32 [32768], P('dp')
- query_grad: float32 [32768, 1024], P('dp', 'mp')
- passage_grad: float32 [262144, 1024], P('dp', 'mp')
Inputs may be any that keep to these rules, and one draw needn't show every extreme that they name: Within each dp index the 512 positives of its query block are distinct. `negatives`: each row names between 16 and 64 blocks (entries >= 0); some row names 64.
All inputs are finite; a program needn't handle non-finite values.
Results may differ from a plain program's by a relative error of at most 0.0075.
Values may be sent and summed in bfloat16 or wider, within the bound.
No kernel may reach another device: no remote copies, remote signals or barrier semaphores. Data moves between devices by JAX's collectives and lax.ppermute only.
A program may use at most 128 MiB of HBM per device.

v0:
```python
import jax
import jax.numpy as jnp
from jax import lax
from jax.sharding import PartitionSpec as P

PBS = 128


def combined_all(part, axis, combine):
    gathered = jax.tree.map(lambda a: lax.all_gather(a, axis), part)

    def take(source):
        return jax.tree.map(lambda a: lax.dynamic_index_in_dim(a, source, 0, False), gathered)

    return lax.fori_loop(
        1, lax.axis_size(axis), lambda source, state: combine(state, take(source)), take(0)
    )


def combine_stats(first, second):
    top = jnp.maximum(first[0], second[0])
    total = first[1] * jnp.exp(first[0] - top) + second[1] * jnp.exp(second[0] - top)
    return (top, total, first[2] + second[2])


def body(queries, passages, positives, negatives):
    dp_count = lax.axis_size("dp")
    mp_count = lax.axis_size("mp")
    own_index = lax.axis_index("dp")
    shard_width = queries.shape[1]
    factor = (shard_width * mp_count) ** (-0.5)
    query_rows = queries.shape[0]
    block_count = passages.shape[0] // PBS
    blocks = passages.reshape(block_count, PBS, shard_width)
    asked = lax.dynamic_index_in_dim(negatives, own_index, 1, keepdims=False)
    outgoing = jnp.take(blocks, jnp.maximum(asked, 0), axis=0)
    outgoing = jnp.where((asked >= 0)[:, None, None], outgoing, jnp.zeros_like(outgoing))
    fetched = lax.all_to_all(outgoing, "dp", split_axis=0, concat_axis=0, tiled=True)
    wanted = lax.dynamic_index_in_dim(negatives, own_index, 0, keepdims=False)
    positive_rows = jnp.take(passages, positives, axis=0)
    cands = jnp.concatenate([positive_rows, fetched.reshape(dp_count * PBS, shard_width)], 0)
    share = cands.shape[0] // mp_count
    width_index = lax.axis_index("mp")
    row_ids = width_index * share + jnp.arange(share, dtype=jnp.int32)
    slot_ids = (row_ids - query_rows) // PBS
    present = jnp.any(
        (slot_ids[:, None] == jnp.arange(dp_count, dtype=jnp.int32)[None, :])
        & (wanted >= 0)[None, :],
        axis=1,
    )
    valid = (row_ids < query_rows) | present
    target = row_ids[:, None] == jnp.arange(query_rows, dtype=jnp.int32)[None, :]
    scores = factor * lax.psum_scatter(
        lax.dot_general(
            cands, queries, (((1,), (1,)), ((), ())), preferred_element_type=jnp.float32
        ),
        "mp",
        scatter_dimension=0,
        tiled=True,
    )
    masked = jnp.where(valid[:, None], scores, jnp.float32(-1e30))
    local_top = jnp.max(masked, axis=0)
    local_total = jnp.sum(
        jnp.where(valid[:, None], jnp.exp(masked - local_top), jnp.float32(0.0)), axis=0
    )
    local_own = jnp.sum(jnp.where(target, scores, jnp.float32(0.0)), axis=0)
    top, total, own_score = combined_all((local_top, local_total, local_own), "mp", combine_stats)
    lse = top + jnp.log(total)
    losses = lse - own_score
    prob = jnp.where(valid[:, None], jnp.exp(masked - lse), jnp.float32(0.0))
    grad_scores = (prob - target.astype(jnp.float32)).astype(jnp.bfloat16)
    all_grads = lax.all_gather(grad_scores, "mp", axis=0, tiled=True)
    query_grad = factor * lax.dot_general(
        all_grads, cands, (((0,), (0,)), ((), ())), preferred_element_type=jnp.float32
    )
    cand_grad = factor * jnp.dot(all_grads, queries, preferred_element_type=jnp.float32)
    sending = cand_grad[query_rows:].reshape(dp_count, PBS, shard_width)
    returned = lax.all_to_all(
        sending.astype(jnp.bfloat16), "dp", split_axis=0, concat_axis=0, tiled=True
    ).astype(sending.dtype)
    selector = (asked[None, :] == jnp.arange(block_count, dtype=jnp.int32)[:, None]).astype(
        jnp.float32
    )
    block_grad = jnp.einsum("kr,rpd->kpd", selector, returned, precision=lax.Precision.HIGHEST)
    passage_grad = (
        block_grad.reshape(block_count * PBS, shard_width).at[positives].add(cand_grad[:query_rows])
    )
    return (losses, query_grad, passage_grad)


def solution(mesh):
    in_specs = (P("dp", "mp"), P("dp", "mp"), P("dp"), P())
    out_specs = (P("dp"), P("dp", "mp"), P("dp", "mp"))
    return jax.shard_map(body, mesh=mesh, in_specs=in_specs, out_specs=out_specs, check_vma=False)
```

profile of v0, /device:TPU:1, one launch (start us, length us, event | category | flops | bytes accessed | tf_op | source)
XLA Modules:
  0.0 568.6 jit_solution(12152360371149172275)
XLA Ops:
  7.2 1.1 dynamic-slice_reduce_fusion
  8.3 0.9 compare_reduce_fusion
  9.3 2.8 gather_fusion.1
  12.1 4.0 select_select_fusion
  16.1 13.5 %all-to-all-start = ((bf16[64,128,256]{2,1,0:T(8,128)(2,1)}), bf16[64,128,256]{2,1,0:T(8,128)(2,1)}, u32[]{:S(2)}, u32[]{:S(2)}) async-start(bf16[64,128,256]{2,1,0:T(8,128)(2,1)} %select_select_fusion), calls=%async_computation | async-start | bytes 8388608 | tf_op jit(solution)/shard_map/all_to_all | solution.py:38
  29.6 0.0 reduce-scatter.2.cloned.1.call-start
  29.7 2.0 gather_fusion
  31.7 0.1 broadcast_select_fusion
  31.8 93.7 %all-to-all-done = bf16[64,128,256]{2,1,0:T(8,128)(2,1)} async-done(((bf16[64,128,256]{2,1,0:T(8,128)(2,1)}), bf16[64,128,256]{2,1,0:T(8,128)(2,1)}, u32[]{:S(2)}, u32[]{:S(2)}) %all-to-all-start) | async-done | bytes 4194336 | tf_op jit(solution)/shard_map/all_to_all | solution.py:38
  125.5 10.8 %fusion.4 = f32[8704,512]{1,0:T(8,128)} fusion(bf16[512,256]{1,0:T(8,128)(2,1)S(1)} %copy-done.4, bf16[8192,256]{1,0:T(8,128)(2,1)} %bitcast.5, bf16[512,256]{1,0:T(8,128)(2,1)S(1)} %broadcast_select_fusion), kind=kOutput, calls=%fused_computation.20 | convolution fusion | flops 2290614272 | bytes 22544384 | tf_op jit(solution)/shard_map/dot_general | solution.py:54
  136.3 0.0 all-gather.8.cloned.1.call-start
  136.4 0.7 compare_bitcast_fusion
  137.1 0.1 fusion.7
  137.3 154.6 %reduce-scatter.2.cloned.1.call-done = f32[2176,512]{1,0:T(8,128)} async-done(((f32[8704,512]{1,0:T(8,128)}), f32[2176,512]{1,0:T(8,128)}) %reduce-scatter.2.cloned.1.call-update) | async-done | bytes 4456464 | tf_op jit(solution)/shard_map/reduce_scatter | solution.py:53
  291.9 3.0 fusion.2
  294.9 8.1 %all-gather.3 = f32[4,1,512]{2,1,0:T(1,128)S(1)} all-gather(f32[1,1,512]{2,1,0:T(1,128)S(1)} %bitcast.49), channel_id=2, replica_groups=mesh['dp'=64,'mp'=4] {'mp'}, dimensions={0}, use_global_device_ids=true | all-gather | bytes 10240 | tf_op jit(solution)/shard_map/all_gather | solution.py:10
  303.0 2.5 select_reduce_fusion
  305.5 8.1 %all-gather.4 = f32[4,1,512]{2,1,0:T(1,128)S(1)} all-gather(f32[1,1,512]{2,1,0:T(1,128)S(1)} %bitcast.51), channel_id=3, replica_groups=mesh['dp'=64,'mp'=4] {'mp'}, dimensions={0}, use_global_device_ids=true | all-gather | bytes 10240 | tf_op jit(solution)/shard_map/all_gather | solution.py:10
  313.6 8.1 %all-gather.5 = f32[4,1,512]{2,1,0:T(1,128)S(1)} all-gather(f32[1,1,512]{2,1,0:T(1,128)S(1)} %bitcast.50), channel_id=4, replica_groups=mesh['dp'=64,'mp'=4] {'mp'}, dimensions={0}, use_global_device_ids=true | all-gather | bytes 10240 | tf_op jit(solution)/shard_map/all_gather | solution.py:10
  321.7 0.3 while.19
  322.0 0.6 fusion.17
  322.6 5.3 subtract_convert_fusion
  327.9 97.9 %all-gather.8.cloned.1.call-done = bf16[8704,512]{1,0:T(8,128)(2,1)} async-done(((bf16[2176,512]{1,0:T(8,128)(2,1)}), bf16[8704,512]{1,0:T(8,128)(2,1)}) %all-gather.8.cloned.1.call-update) | async-done | bytes 8912912 | tf_op jit(solution)/shard_map/all_gather | solution.py:72
  425.8 6.0 %convolution_multiply_fusion = f32[8704,256]{1,0:T(8,128)S(1)} fusion(bf16[8704,512]{1,0:T(8,128)(2,1)} %all-gather.8.cloned.1.call-done, bf16[512,256]{1,0:T(8,128)(2,1)S(1)} %copy-done.4), kind=kOutput, calls=%fused_computation.7 | convolution fusion | flops 2283929600 | bytes 18087936 | tf_op jit(solution)/shard_map/dot_general | solution.py:76
  431.8 3.4 copy-done.3
  435.2 2.4 slice.30
  437.6 10.9 %all-to-all-start.1 = ((bf16[64,128,256]{2,1,0:T(8,128)(2,1)}), bf16[64,128,256]{2,1,0:T(8,128)(2,1)}, u32[]{:S(2)}, u32[]{:S(2)}) async-start(bf16[64,128,256]{2,1,0:T(8,128)(2,1)} %bitcast.38), calls=%async_computation.2 | async-start | bytes 8388608 | tf_op jit(solution)/shard_map/all_to_all | solution.py:78
  448.5 8.0 %fusion.5 = f32[512,256]{1,0:T(8,128)} fusion(bf16[8704,512]{1,0:T(8,128)(2,1)} %all-gather.8.cloned.1.call-done, bf16[8192,256]{1,0:T(8,128)(2,1)} %bitcast.5, bf16[512,256]{1,0:T(8,128)(2,1)S(1)} %broadcast_select_fusion), kind=kOutput, calls=%fused_computation.21 | convolution fusion | flops 2290745344 | bytes 13893632 | tf_op jit(solution)/shard_map/dot_general | solution.py:73
  456.5 87.9 %all-to-all-done.1 = bf16[64,128,256]{2,1,0:T(8,128)(2,1)} async-done(((bf16[64,128,256]{2,1,0:T(8,128)(2,1)}), bf16[64,128,256]{2,1,0:T(8,128)(2,1)}, u32[]{:S(2)}, u32[]{:S(2)}) %all-to-all-start.1) | async-done | bytes 4194336 | tf_op jit(solution)/shard_map/all_to_all | solution.py:78
  544.4 5.2 fusion
  549.6 4.4 copy.13
  554.0 7.7 %scatter_custom_fusion = f32[4096,256]{1,0:T(8,128)} fusion(f32[4096,256]{1,0:T(8,128)} %bitcast.39, s32[512]{0:T(512)S(1)} %compare_select_fusion, f32[8704,256]{1,0:T(8,128)} %copy-done.3), kind=kCustom, calls=%fused_computation.25 | custom fusion | flops 131072 | bytes 4718592 | tf_op jit(solution)/shard_map/scatter-add | solution.py:86
  (39 shorter events, 0.3 us)
Async XLA Ops:
  7.2 2.1 copy-start
  16.1 13.5 %copy-start.5 = (s32[512]{0:T(512)S(1)}, s32[512]{0:T(512)}, u32[]{:S(2)}) copy-start(s32[512]{0:T(512)} %param.8) | copy-start | bytes 6148
  16.1 109.4 %copy-start.4 = (bf16[512,256]{1,0:T(8,128)(2,1)S(1)}, bf16[512,256]{1,0:T(8,128)(2,1)}, u32[]{:S(2)}) copy-start(bf16[512,256]{1,0:T(8,128)(2,1)} %param.6) | copy-start | bytes 786436
  16.1 109.4 %all-to-all-start = ((bf16[64,128,256]{2,1,0:T(8,128)(2,1)}), bf16[64,128,256]{2,1,0:T(8,128)(2,1)}, u32[]{:S(2)}, u32[]{:S(2)}) async-start(bf16[64,128,256]{2,1,0:T(8,128)(2,1)} %select_select_fusion), calls=%async_computation | async-start | bytes 8388608 | tf_op jit(solution)/shard_map/all_to_all | solution.py:38
  29.6 262.3 %reduce-scatter.2.cloned.1.call-start = ((), (), s32[]{:S(2)}) async-start(), calls=%async_computation.3 | async-start | bytes 22282240 | tf_op jit(solution)/shard_map/reduce_scatter | solution.py:53
  136.3 289.4 %all-gather.8.cloned.1.call-start = ((), (), s32[]{:S(2)}) async-start(), calls=%async_computation.4 | async-start | bytes 11141120 | tf_op jit(solution)/shard_map/all_gather | solution.py:72
  291.9 11.1 %copy-start.2 = (f32[2176,512]{1,0:T(8,128)S(1)}, f32[2176,512]{1,0:T(8,128)}, u32[]{:S(2)}) copy-start(f32[2176,512]{1,0:T(8,128)} %reduce-scatter.2.cloned.1.call-done) | copy-start | bytes 13369348
  431.8 3.4 copy-start.3
  437.6 106.8 %all-to-all-start.1 = ((bf16[64,128,256]{2,1,0:T(8,128)(2,1)}), bf16[64,128,256]{2,1,0:T(8,128)(2,1)}, u32[]{:S(2)}, u32[]{:S(2)}) async-start(bf16[64,128,256]{2,1,0:T(8,128)(2,1)} %bitcast.38), calls=%async_computation.2 | async-start | bytes 8388608 | tf_op jit(solution)/shard_map/all_to_all | solution.py:78
  549.6 12.2 %copy-start.1 = (bf16[4096,256]{1,0:T(8,128)(2,1)S(1)}, bf16[4096,256]{1,0:T(8,128)(2,1)}, u32[]{:S(2)}) copy-start(bf16[4096,256]{1,0:T(8,128)(2,1)} %param.7) | copy-start | bytes 6291460
Sparse Core Ops, SparseCore 0:
  136.5 155.3 reduce-scatter.1
  328.0 97.6 all-gather.7
where the time goes:
time: 569 us
  waiting for transfers between devices  434 us (76%)
  matrix products  30.1 us (5%)
  other arithmetic  26.3 us (5%)
  starting transfers between devices  24.4 us (4%)
  blocking collectives  24.2 us (4%)
  local copies, waits for them, and re-layouts  15.2 us (3%)
  between operations  14.2 us (2%)
    reduce_scatter x1, waiting for transfers between devices, body(): lax.psum_scatter(lax.dot_general(cands, queries, (((1,), (1,)), ((), ()))...  155 us
    all_gather x1, waiting for transfers between devices, body(): all_grads = lax.all_gather(grad_scores, 'mp', axis=0, tiled=True)  97.9 us
    all_to_all x1, waiting for transfers between devices, body(): lax.all_to_all(outgoing, 'dp', split_axis=0, concat_axis=0, tiled=True)  93.7 us
    all_to_all x1, waiting for transfers between devices, body(): lax.all_to_all(sending.astype(jnp.bfloat16), 'dp', split_axis=0, concat_a...  87.9 us
    all_gather x3, blocking collectives, combined_all(): gathered = jax.tree.map(lambda a: lax.all_gather(a, axis), part)  24.2 us
    all_to_all x1, starting transfers between devices, body(): lax.all_to_all(outgoing, 'dp', split_axis=0, concat_axis=0, tiled=True)  13.5 us
  transfers between devices with their start and end apart: 4, of which 4 were waited for; matrix products, arithmetic and copies ran while one was open for 2% of the time, Pallas kernels for 0%

commit v1 on v0

v1 whole, which is shorter than its diff:
```python
import jax
import jax.numpy as jnp
from jax import lax
from jax.sharding import PartitionSpec as P

PBS = 128


def body(queries, passages, positives, negatives):
    dp_count = lax.axis_size("dp")
    mp_count = lax.axis_size("mp")
    own_index = lax.axis_index("dp")
    width_index = lax.axis_index("mp")
    query_rows, shard_width = queries.shape
    factor = (shard_width * mp_count) ** (-0.5)
    block_count = passages.shape[0] // PBS
    slots_per = dp_count // mp_count
    pos_per = query_rows // mp_count
    blocks = passages.reshape(block_count, PBS, shard_width)

    asked = lax.dynamic_index_in_dim(negatives, own_index, 1, keepdims=False)
    outgoing = jnp.take(blocks, jnp.maximum(asked, 0), axis=0)
    outgoing = jnp.where((asked >= 0)[:, None, None], outgoing, jnp.zeros_like(outgoing))
    fetched = lax.all_to_all(outgoing, "dp", split_axis=0, concat_axis=0, tiled=True)
    wanted = lax.dynamic_index_in_dim(negatives, own_index, 0, keepdims=False)

    positive_rows = jnp.take(passages, positives, axis=0)
    send = jnp.concatenate(
        [
            positive_rows.reshape(mp_count, pos_per, shard_width),
            fetched.reshape(mp_count, slots_per * PBS, shard_width),
        ],
        axis=1,
    )
    mine = lax.all_to_all(send, "mp", split_axis=0, concat_axis=0, tiled=True)
    row_count = mine.shape[1]
    q_full = lax.all_gather(queries, "mp", axis=1, tiled=True)
    q4 = q_full.reshape(query_rows, mp_count, shard_width)

    scores = factor * lax.dot_general(
        mine, q4, (((0, 2), (1, 2)), ((), ())), preferred_element_type=jnp.float32
    )

    rows = jnp.arange(row_count, dtype=jnp.int32)
    slot_of_row = width_index * slots_per + (rows - pos_per) // PBS
    slot_ok = jnp.take(wanted, jnp.clip(slot_of_row, 0, dp_count - 1)) >= 0
    valid = (rows < pos_per) | slot_ok
    target = (rows < pos_per)[:, None] & (
        (width_index * pos_per + rows)[:, None]
        == jnp.arange(query_rows, dtype=jnp.int32)[None, :]
    )

    masked = jnp.where(valid[:, None], scores, jnp.float32(-1e30))
    local_top = jnp.max(masked, axis=0)
    local_total = jnp.sum(
        jnp.where(valid[:, None], jnp.exp(masked - local_top), jnp.float32(0.0)), axis=0
    )
    local_own = jnp.sum(jnp.where(target, scores, jnp.float32(0.0)), axis=0)
    stats = lax.all_gather(jnp.stack([local_top, local_total, local_own]), "mp", axis=0)
    top = jnp.max(stats[:, 0], axis=0)
    total = jnp.sum(stats[:, 1] * jnp.exp(stats[:, 0] - top), axis=0)
    own_score = jnp.sum(stats[:, 2], axis=0)
    lse = top + jnp.log(total)
    losses = lse - own_score

    prob = jnp.where(valid[:, None], jnp.exp(masked - lse), jnp.float32(0.0))
    grad_scores = (prob - target.astype(jnp.float32)).astype(jnp.bfloat16)

    query_part = factor * lax.dot_general(
        grad_scores, mine, (((0,), (1,)), ((), ())), preferred_element_type=jnp.float32
    )
    query_grad = lax.psum_scatter(query_part, "mp", scatter_dimension=1, tiled=True)
    query_grad = query_grad.reshape(query_rows, shard_width)

    cand_grad = factor * jnp.dot(grad_scores, q_full, preferred_element_type=jnp.float32)
    cand_grad = cand_grad.reshape(row_count, mp_count, shard_width).transpose(1, 0, 2)
    pos_back = lax.all_to_all(
        cand_grad[:, :pos_per], "mp", split_axis=0, concat_axis=0, tiled=True
    ).reshape(query_rows, shard_width)
    neg_back = lax.all_to_all(
        cand_grad[:, pos_per:].astype(jnp.bfloat16), "mp", split_axis=0, concat_axis=0, tiled=True
    ).reshape(dp_count, PBS, shard_width)

    returned = lax.all_to_all(
        neg_back, "dp", split_axis=0, concat_axis=0, tiled=True
    ).astype(jnp.float32)
    selector = (asked[None, :] == jnp.arange(block_count, dtype=jnp.int32)[:, None]).astype(
        jnp.float32
    )
    block_grad = jnp.einsum("kr,rpd->kpd", selector, returned, precision=lax.Precision.HIGHEST)
    passage_grad = block_grad.reshape(block_count * PBS, shard_width).at[positives].add(pos_back)
    return (losses, query_grad, passage_grad)


def solution(mesh):
    in_specs = (P("dp", "mp"), P("dp", "mp"), P("dp"), P())
    out_specs = (P("dp"), P("dp", "mp"), P("dp", "mp"))
    return jax.shard_map(body, mesh=mesh, in_specs=in_specs, out_specs=out_specs, check_vma=False)
```

time: 569 us -> 417 us (0.73)
  waiting for transfers between devices: 434 us -> 192 us
  other arithmetic: 26.3 us -> 63.8 us
  blocking collectives: 24.2 us -> 56.9 us
  local copies, waits for them, and re-layouts: 15.2 us -> 28.6 us
  starting transfers between devices: 24.4 us -> 33.2 us
    reduce_scatter x1, waiting for transfers between devices: 155 us -> 0.01 us  [body(): lax.psum_scatter(query_part, 'mp', scatter_dimension=1, tiled=True)]
    all_gather x1, waiting for transfers between devices: 97.9 us -> 0.02 us  [body(): q_full = lax.all_gather(queries, 'mp', axis=1, tiled=True)]
    all_to_all x0 -> x1, blocking collectives: none -> 47.9 us  [body(): lax.all_to_all(cand_grad[:, pos_per:].astype(jnp.bfloat16), 'mp', split_a...]
    or x1, other arithmetic: 0.01 us -> 35.5 us  [body(): valid = (rows < pos_per) | slot_ok]
    all_gather x3 -> x1, blocking collectives: 24.2 us -> 9.02 us  [body(): lax.all_gather(jnp.stack([local_top, local_total, local_own]), 'mp', axis=0)]
    all_to_all x1 -> x3, waiting for transfers between devices: 87.9 us -> 98.4 us  [the longest x1 85.6 us: body(): lax.all_to_all(neg_back, 'dp', split_axis=0, concat_axis=0, tiled=True)]
    reshape x0 -> x1, local copies, waits for them, and re-layouts: none -> 9.23 us  [body(): cand_grad.reshape(row_count, mp_count, shard_width).transpose(1, 0, 2)]
    all_to_all x1 -> x3, starting transfers between devices: 10.9 us -> 19.7 us  [the longest x1 11.2 us: body(): lax.all_to_all(neg_back, 'dp', split_axis=0, concat_axis=0, tiled=True)]
  transfers between devices with their start and end apart: 4 -> 6, of which waited for: 4 -> 3; matrix products, arithmetic and copies ran while one was open for 2% -> 18% of each run, Pallas kernels for 0% -> 0%
where the time goes in v1:
time: 417 us; the launch traced here: 416 us
  waiting for transfers between devices  192 us (46%)
  other arithmetic  63.8 us (15%)
  blocking collectives  56.9 us (14%)
  starting transfers between devices  33.2 us (8%)
  local copies, waits for them, and re-layouts  28.6 us (7%)
  matrix products  26.7 us (6%)
  between operations  14.3 us (3%)
    all_to_all x1, waiting for transfers between devices, body(): lax.all_to_all(outgoing, 'dp', split_axis=0, concat_axis=0, tiled=True)  93.7 us
    all_to_all x1, waiting for transfers between devices, body(): lax.all_to_all(neg_back, 'dp', split_axis=0, concat_axis=0, tiled=True)  85.6 us
    all_to_all x1, blocking collectives, body(): lax.all_to_all(cand_grad[:, pos_per:].astype(jnp.bfloat16), 'mp', split_a...  47.9 us
    or x1, other arithmetic, body(): valid = (rows < pos_per) | slot_ok  35.5 us
    all_to_all x1, starting transfers between devices, body(): lax.all_to_all(outgoing, 'dp', split_axis=0, concat_axis=0, tiled=True)  13.5 us
    all_to_all x1, waiting for transfers between devices, body(): mine = lax.all_to_all(send, 'mp', split_axis=0, concat_axis=0, tiled=True)  12.9 us
    all_to_all x1, starting transfers between devices, body(): lax.all_to_all(neg_back, 'dp', split_axis=0, concat_axis=0, tiled=True)  11.2 us
    reshape x1, local copies, waits for them, and re-layouts, body(): cand_grad.reshape(row_count, mp_count, shard_width).transpose(1, 0, 2)  9.23 us
  transfers between devices with their start and end apart: 6, of which 3 were waited for; matrix products, arithmetic and copies ran while one was open for 18% of the time, Pallas kernels for 0%

profile of v1, /device:TPU:1, one launch (start us, length us, event | category | flops | bytes accessed | tf_op | source)
XLA Modules:
  0.0 415.7 jit_solution(13492782562870780625)
XLA Ops:
  7.2 1.1 compare_reduce_fusion.57
  8.3 0.9 dynamic-slice_reduce_fusion
  9.3 2.8 gather_fusion.1
  12.1 4.0 select_select_fusion
  16.1 13.5 %all-to-all-start = ((bf16[64,128,256]{2,1,0:T(8,128)(2,1)}), bf16[64,128,256]{2,1,0:T(8,128)(2,1)}, u32[]{:S(2)}, u32[]{:S(2)}) async-start(bf16[64,128,256]{2,1,0:T(8,128)(2,1)} %select_select_fusion), calls=%async_computation | async-start | bytes 8388608 | tf_op jit(solution)/shard_map/all_to_all | solution.py:24
  29.6 2.0 gather_fusion
  31.8 93.7 %all-to-all-done = bf16[64,128,256]{2,1,0:T(8,128)(2,1)} async-done(((bf16[64,128,256]{2,1,0:T(8,128)(2,1)}), bf16[64,128,256]{2,1,0:T(8,128)(2,1)}, u32[]{:S(2)}, u32[]{:S(2)}) %all-to-all-start) | async-done | bytes 4194336 | tf_op jit(solution)/shard_map/all_to_all | solution.py:24
  125.5 4.6 %pad_maximum_fusion = bf16[4,2176,256]{2,1,0:T(8,128)(2,1)} fusion(bf16[4,2048,256]{2,1,0:T(8,128)(2,1)} %bitcast.67, bf16[4,128,256]{2,1,0:T(8,128)(2,1)S(1)} %broadcast_select_fusion), kind=kLoop, calls=%fused_computation.7 | loop fusion | flops 8912896 | bytes 8912896 | tf_op jit(solution)/shard_map/concatenate | solution.py:28
  130.1 5.0 %all-to-all-start.1 = ((bf16[4,2176,256]{2,1,0:T(8,128)(2,1)}), bf16[4,2176,256]{2,1,0:T(8,128)(2,1)}, u32[]{:S(2)}, u32[]{:S(2)}) async-start(bf16[4,2176,256]{2,1,0:T(8,128)(2,1)} %pad_maximum_fusion), calls=%async_computation.1 | async-start | bytes 8912896 | tf_op jit(solution)/shard_map/all_to_all | solution.py:35
  135.1 0.8 copy.17
  138.6 0.7 constant_dynamic-slice_fusion
  140.0 0.7 fusion.26
  140.7 4.4 %fusion.18 = s32[2176]{0:T(1024)S(1)} fusion(s32[]{:T(128)} %bitcast.57, s32[]{:T(128)} %bitcast.58, s32[]{:T(128)} %bitcast.59, s32[]{:T(128)} %bitcast.60, s32[]{:T(128)} %bitcast.61, s32[]{:T(128)} %bitcast.63, s32[]{:T(128)} %bitcast.62, s32[]{:T(128)S(6)} %mul.27), kind=kLoop, calls=%fused_computation.111 | loop fusion | flops 71808 | bytes 8736 | tf_op jit(solution)/shard_map/jit(_take)/gather | solution.py:46
  145.1 0.7 fusion.27
  145.8 0.7 fusion.28
  146.6 35.5 %fusion.17 = pred[2176]{0:T(1024)(128)(4,1)S(1)} fusion(pred[2176]{0:T(1024)(128)(4,1)S(1)} %get-tuple-element.81, pred[2176]{0:T(1024)(128)(4,1)S(1)} %get-tuple-element.82, pred[2176]{0:T(1024)(128)(4,1)S(1)} %get-tuple-element.83, pred[2176]{0:T(1024)(128)(4,1)S(1)} %get-tuple-element.84, pred[2176]{0:T(1024)(128)(4,1)S(1)} %get-tuple-element.85, ...), kind=kLoop, calls=%fused_computation.110 | loop fusion | flops 184960 | bytes 135144 | tf_op jit(solution)/shard_map/or | solution.py:47
  182.1 12.9 %all-to-all-done.1 = bf16[4,2176,256]{2,1,0:T(8,128)(2,1)} async-done(((bf16[4,2176,256]{2,1,0:T(8,128)(2,1)}), bf16[4,2176,256]{2,1,0:T(8,128)(2,1)}, u32[]{:S(2)}, u32[]{:S(2)}) %all-to-all-start.1) | async-done | bytes 4456480 | tf_op jit(solution)/shard_map/all_to_all | solution.py:35
  195.0 5.0 %select_reduce_fusion.2 = (f32[512]{0:T(512)S(1)}, f32[2176,512]{1,0:T(8,128)S(1)}) fusion(pred[2176]{0:T(1024)(128)(4,1)S(1)} %fusion.17, bf16[4,2176,256]{2,1,0:T(8,128)(2,1)} %all-to-all-done.1, bf16[512,4,256]{0,2,1:T(8,128)(2,1)} %bitcast.120), kind=kOutput, calls=%fused_computation.16 | convolution fusion | flops 2285043200 | bytes 9965696 | tf_op jit(solution)/shard_map/dot_general | solution.py:40
  200.0 2.6 select_reduce_fusion.1
  202.6 9.0 %all-gather.1 = f32[4,3,512]{2,1,0:T(4,128)S(1)} all-gather(f32[1,3,512]{2,1,0:T(4,128)S(1)} %maximum_bitcast_fusion), channel_id=2, replica_groups=mesh['dp'=64,'mp'=4] {'mp'}, dimensions={0}, use_global_device_ids=true | all-gather | bytes 30720 | tf_op jit(solution)/shard_map/all_gather | solution.py:59
  212.3 8.1 %convolution_multiply_fusion = f32[2176,1024]{0,1:T(8,128)} fusion(bf16[512,1024]{0,1:T(8,128)(2,1)S(1)} %copy-done.5, f32[2176,512]{1,0:T(8,128)S(1)} %get-tuple-element.80, f32[512]{0:T(512)S(1)} %get-tuple-element.10, s32[2176]{0:T(1024)S(1)} %iota_add_fusion, pred[2176]{0:T(1024)(128)(4,1)S(1)} %iota_compare_fusion.2, pred[2176]{0:T(1024)(128)(4,1)S(1)} %fusion.17), kind=kOutput, calls=%fused_computation.4 | convolution fusion | flops 2292842496 | bytes 14433024 | tf_op jit(solution)/shard_map/dot_general | solution.py:75
  220.4 9.2 %copy.21 = f32[2176,4,256]{2,0,1:T(8,128)} copy(f32[2176,4,256]{0,2,1:T(8,128)} %bitcast.114) | data formatting | bytes 17825792 | tf_op jit(solution)/shard_map/reshape | solution.py:76
  229.6 3.8 slice.164
  233.4 47.9 %all_to_all.25 = bf16[4,2048,256]{2,1,0:T(8,128)(2,1)} all-to-all(bf16[4,2048,256]{2,1,0:T(8,128)(2,1)S(1)} %slice.164), channel_id=1, replica_groups=mesh['dp'=64,'mp'=4] {'mp'}, dimensions={0} | all-to-all | bytes 8388608 | tf_op jit(solution)/shard_map/all_to_all | solution.py:80
  281.3 11.2 %all-to-all-start.3 = ((bf16[64,128,256]{2,1,0:T(8,128)(2,1)}), bf16[64,128,256]{2,1,0:T(8,128)(2,1)}, u32[]{:S(2)}, u32[]{:S(2)}) async-start(bf16[64,128,256]{2,1,0:T(8,128)(2,1)} %bitcast.113), calls=%async_computation.4 | async-start | bytes 8388608 | tf_op jit(solution)/shard_map/all_to_all | solution.py:84
  292.6 8.4 %fusion.6 = f32[512,4,256]{2,0,1:T(8,128)} fusion(bf16[4,2176,256]{2,1,0:T(8,128)(2,1)} %all-to-all-done.1, f32[2176,512]{1,0:T(8,128)} %copy-done.2, f32[512]{0:T(512)S(1)} %get-tuple-element.10, s32[2176]{0:T(1024)S(1)} %iota_add_fusion, pred[2176]{0:T(1024)(128)(4,1)S(1)} %iota_compare_fusion.2, pred[2176]{0:T(1024)(128)(4,1)S(1)} %fusion.17), kind=kOutput, calls=%fused_computation.19 | convolution fusion | flops 2291138560 | bytes 11025152 | tf_op jit(solution)/shard_map/dot_general | solution.py:69
  301.0 1.9 slice.160
  302.8 85.6 %all-to-all-done.3 = bf16[64,128,256]{2,1,0:T(8,128)(2,1)} async-done(((bf16[64,128,256]{2,1,0:T(8,128)(2,1)}), bf16[64,128,256]{2,1,0:T(8,128)(2,1)}, u32[]{:S(2)}, u32[]{:S(2)}) %all-to-all-start.3) | async-done | bytes 4194336 | tf_op jit(solution)/shard_map/all_to_all | solution.py:84
  388.4 3.5 all-to-all-start.4
  391.9 5.2 %fusion.2 = f32[32,128,256]{2,0,1:T(8,128)S(1)} fusion(bf16[64,128,256]{2,1,0:T(8,128)(2,1)} %all-to-all-done.3, s32[64]{0:T(128)S(1)} %get-tuple-element.7), kind=kOutput, calls=%fused_computation.13 | convolution fusion | flops 134219776 | bytes 8388864 | tf_op jit(solution)/shard_map/kr,rpd->kpd/dot_general | solution.py:90
  397.1 4.4 %copy.23 = f32[32,128,256]{2,1,0:T(8,128)} copy(f32[32,128,256]{2,0,1:T(8,128)S(1)} %fusion.2) | data formatting | bytes 8388608 | tf_op jit(solution)/shard_map/kr,rpd->kpd/dot_general | solution.py:90
  401.5 7.3 %scatter_fusion = f32[4096,256]{1,0:T(8,128)} fusion(f32[4096,256]{1,0:T(8,128)} %bitcast.112, s32[512]{0:T(512)S(1)} %compare_select_fusion.11, f32[512,256]{1,0:T(8,128)S(1)} %bitcast.115), kind=kCustom, calls=%fused_computation.2 | custom fusion | flops 131072 | bytes 1574912 | tf_op jit(solution)/shard_map/scatter-add | solution.py:91
  (61 shorter events, 4.2 us)
Async XLA Ops:
  7.2 2.1 copy-start
  16.1 13.5 %copy-start.4 = (s32[512]{0:T(512)S(1)}, s32[512]{0:T(512)}, u32[]{:S(2)}) copy-start(s32[512]{0:T(512)} %param.6) | copy-start | bytes 6148
  16.1 109.4 %all-to-all-start = ((bf16[64,128,256]{2,1,0:T(8,128)(2,1)}), bf16[64,128,256]{2,1,0:T(8,128)(2,1)}, u32[]{:S(2)}, u32[]{:S(2)}) async-start(bf16[64,128,256]{2,1,0:T(8,128)(2,1)} %select_select_fusion), calls=%async_computation | async-start | bytes 8388608 | tf_op jit(solution)/shard_map/all_to_all | solution.py:24
  130.1 5.1 %copy-start.3 = (bf16[512,256]{1,0:T(8,128)(2,1)S(1)}, bf16[512,256]{1,0:T(8,128)(2,1)}, u32[]{:S(2)}) copy-start(bf16[512,256]{1,0:T(8,128)(2,1)} %param.4) | copy-start | bytes 786436
  130.1 64.9 %all-to-all-start.1 = ((bf16[4,2176,256]{2,1,0:T(8,128)(2,1)}), bf16[4,2176,256]{2,1,0:T(8,128)(2,1)}, u32[]{:S(2)}, u32[]{:S(2)}) async-start(bf16[4,2176,256]{2,1,0:T(8,128)(2,1)} %pad_maximum_fusion), calls=%async_computation.1 | async-start | bytes 8912896 | tf_op jit(solution)/shard_map/all_to_all | solution.py:35
  135.1 47.0 %all-gather.4.cloned.1.call-start = ((), (), s32[]{:S(2)}) async-start(), calls=%async_computation.6 | async-start | bytes 1310720 | tf_op jit(solution)/shard_map/all_gather | solution.py:37
  200.0 20.4 %copy-start.2 = (f32[2176,512]{1,0:T(8,128)}, f32[2176,512]{1,0:T(8,128)S(1)}, u32[]{:S(2)}) copy-start(f32[2176,512]{1,0:T(8,128)S(1)} %get-tuple-element.80) | copy-start | bytes 13369348
  200.0 12.3 %copy-start.5 = (bf16[512,1024]{0,1:T(8,128)(2,1)S(1)}, bf16[512,1024]{0,1:T(8,128)(2,1)}, u32[]{:S(2)}) copy-start(bf16[512,1024]{0,1:T(8,128)(2,1)} %all-gather.4.cloned.1.call-done) | copy-start | bytes 3145732
  281.3 107.1 %all-to-all-start.3 = ((bf16[64,128,256]{2,1,0:T(8,128)(2,1)}), bf16[64,128,256]{2,1,0:T(8,128)(2,1)}, u32[]{:S(2)}, u32[]{:S(2)}) async-start(bf16[64,128,256]{2,1,0:T(8,128)(2,1)} %bitcast.113), calls=%async_computation.4 | async-start | bytes 8388608 | tf_op jit(solution)/shard_map/all_to_all | solution.py:84
  292.5 116.4 %reduce-scatter.2.cloned.1.call-start = ((), (), s32[]{:S(2)}) async-start(), calls=%async_computation.7 | async-start | bytes 2621440 | tf_op jit(solution)/shard_map/reduce_scatter | solution.py:72
  388.4 13.1 %all-to-all-start.4 = ((f32[4,128,256]{2,1,0:T(8,128)}), f32[4,128,256]{2,1,0:T(8,128)S(1)}, u32[]{:S(2)}, u32[]{:S(2)}) async-start(f32[4,128,256]{2,1,0:T(8,128)} %slice.160), calls=%async_computation.5 | async-start | bytes 1048576 | tf_op jit(solution)/shard_map/all_to_all | solution.py:77
  401.5 7.3 %copy-start.1 = (bf16[4096,256]{1,0:T(8,128)(2,1)S(1)}, bf16[4096,256]{1,0:T(8,128)(2,1)}, u32[]{:S(2)}) copy-start(bf16[4096,256]{1,0:T(8,128)(2,1)} %param.5) | copy-start | bytes 6291460
Sparse Core Ops, SparseCore 0:
  138.3 30.1 all-gather.3
  301.1 31.3 reduce-scatter.1

commit v2 on v1

v2 whole, which is shorter than its diff:
```python
import jax
import jax.numpy as jnp
from jax import lax
from jax.sharding import PartitionSpec as P

PBS = 128
HALVES = 2


def body(queries, passages, positives, negatives):
    dp_count = lax.axis_size("dp")
    mp_count = lax.axis_size("mp")
    own_index = lax.axis_index("dp")
    width_index = lax.axis_index("mp")
    query_rows, shard_width = queries.shape
    factor = (shard_width * mp_count) ** (-0.5)
    block_count = passages.shape[0] // PBS
    slots_per = dp_count // mp_count
    pos_per = query_rows // mp_count
    part = PBS // HALVES
    blocks = passages.reshape(block_count, PBS, shard_width)

    asked = lax.dynamic_index_in_dim(negatives, own_index, 1, keepdims=False)
    outgoing = jnp.take(blocks, jnp.maximum(asked, 0), axis=0)
    outgoing = jnp.where((asked >= 0)[:, None, None], outgoing, jnp.zeros_like(outgoing))
    wanted = lax.dynamic_index_in_dim(negatives, own_index, 0, keepdims=False)
    my_slots = lax.dynamic_slice_in_dim(wanted, width_index * slots_per, slots_per) >= 0

    q_full = lax.all_gather(queries, "mp", axis=1, tiled=True)
    q4 = q_full.reshape(query_rows, mp_count, shard_width)
    positive_rows = jnp.take(passages, positives, axis=0)

    mine, valid = [], []
    for h in range(HALVES):
        fetched = lax.all_to_all(
            outgoing[:, h * part:(h + 1) * part], "dp", split_axis=0, concat_axis=0, tiled=True
        )
        send = fetched.reshape(mp_count, slots_per * part, shard_width)
        ok = jnp.broadcast_to(my_slots[:, None], (slots_per, part)).reshape(-1)
        if h == 0:
            send = jnp.concatenate(
                [positive_rows.reshape(mp_count, pos_per, shard_width), send], axis=1
            )
            ok = jnp.concatenate([jnp.ones((pos_per,), bool), ok])
        mine.append(lax.all_to_all(send, "mp", split_axis=0, concat_axis=0, tiled=True))
        valid.append(ok)

    scores = [
        factor
        * lax.dot_general(c, q4, (((0, 2), (1, 2)), ((), ())), preferred_element_type=jnp.float32)
        for c in mine
    ]
    masked = [jnp.where(v[:, None], s, jnp.float32(-1e30)) for s, v in zip(scores, valid)]
    local_top = jnp.max(jnp.stack([jnp.max(x, axis=0) for x in masked]), axis=0)
    local_total = sum(
        jnp.sum(jnp.where(v[:, None], jnp.exp(x - local_top), jnp.float32(0.0)), axis=0)
        for x, v in zip(masked, valid)
    )
    target = (width_index * pos_per + jnp.arange(pos_per, dtype=jnp.int32))[:, None] == jnp.arange(
        query_rows, dtype=jnp.int32
    )[None, :]
    local_own = jnp.sum(jnp.where(target, scores[0][:pos_per], jnp.float32(0.0)), axis=0)
    stats = lax.all_gather(jnp.stack([local_top, local_total, local_own]), "mp", axis=0)
    top = jnp.max(stats[:, 0], axis=0)
    total = jnp.sum(stats[:, 1] * jnp.exp(stats[:, 0] - top), axis=0)
    own_score = jnp.sum(stats[:, 2], axis=0)
    lse = top + jnp.log(total)
    losses = lse - own_score

    grads = []
    for h in range(HALVES):
        prob = jnp.where(valid[h][:, None], jnp.exp(masked[h] - lse), jnp.float32(0.0))
        if h == 0:
            prob = jnp.concatenate([prob[:pos_per] - target.astype(jnp.float32), prob[pos_per:]])
        grads.append(prob.astype(jnp.bfloat16))

    query_part = sum(
        lax.dot_general(g, c, (((0,), (1,)), ((), ())), preferred_element_type=jnp.float32)
        for g, c in zip(grads, mine)
    )
    query_grad = lax.psum_scatter(factor * query_part, "mp", scatter_dimension=1, tiled=True)
    query_grad = query_grad.reshape(query_rows, shard_width)

    returned, pos_back = [], None
    for h in range(HALVES):
        cand = factor * jnp.dot(grads[h], q_full, preferred_element_type=jnp.float32)
        rows = cand.shape[0]
        pieces = []
        if h == 0:
            pos = cand[:pos_per]
            rounded = lax.reduce_precision(pos, exponent_bits=8, mantissa_bits=7)
            high = rounded.astype(jnp.bfloat16)
            low = (pos - rounded).astype(jnp.bfloat16)
            for x in (high, low):
                pieces.append(x.reshape(pos_per, mp_count, shard_width).transpose(1, 0, 2))
            cand = cand[pos_per:]
            rows -= pos_per
        neg = cand.astype(jnp.bfloat16).reshape(rows, mp_count, shard_width).transpose(1, 0, 2)
        pieces.append(neg)
        sent = lax.all_to_all(
            jnp.concatenate(pieces, axis=1), "mp", split_axis=0, concat_axis=0, tiled=True
        )
        if h == 0:
            pos_back = (
                sent[:, :pos_per].astype(jnp.float32) + sent[:, pos_per:2 * pos_per].astype(jnp.float32)
            ).reshape(query_rows, shard_width)
            sent = sent[:, 2 * pos_per:]
        back = lax.all_to_all(
            sent.reshape(dp_count, part, shard_width), "dp", split_axis=0, concat_axis=0, tiled=True
        )
        returned.append(back)
    returned = jnp.concatenate(returned, axis=1).astype(jnp.float32)

    selector = (asked[None, :] == jnp.arange(block_count, dtype=jnp.int32)[:, None]).astype(
        jnp.float32
    )
    block_grad = jnp.einsum("kr,rpd->kpd", selector, returned, precision=lax.Precision.HIGHEST)
    passage_grad = block_grad.reshape(block_count * PBS, shard_width).at[positives].add(pos_back)
    return (losses, query_grad, passage_grad)


def solution(mesh):
    in_specs = (P("dp", "mp"), P("dp", "mp"), P("dp"), P())
    out_specs = (P("dp"), P("dp", "mp"), P("dp", "mp"))
    return jax.shard_map(body, mesh=mesh, in_specs=in_specs, out_specs=out_specs, check_vma=False)
```

time: 417 us -> 432 us (1.036)
  blocking collectives: 56.9 us -> 161 us
  waiting for transfers between devices: 192 us -> 146 us
  other arithmetic: 63.8 us -> 24 us
  matrix products: 26.7 us -> 21.8 us
    all_to_all x1 -> x3, blocking collectives: 47.9 us -> 152 us  [the longest x2 121 us: body(): lax.all_to_all(outgoing[:, h * part:(h + 1) * part], 'dp', split_axis=0,...]
    all_to_all x4 -> x5, waiting for transfers between devices: 192 us -> 146 us  [the longest x2 86.8 us: body(): lax.all_to_all(sent.reshape(dp_count, part, shard_width), 'dp', split_axi...]
    or x1 -> x0, other arithmetic: 35.5 us -> none  [body(): valid = (rows < pos_per) | slot_ok]
    gather x30 -> x0, other arithmetic: 6.93 us -> none  [body(): slot_ok = jnp.take(wanted, jnp.clip(slot_of_row, 0, dp_count - 1)) >= 0]
    all_to_all x0 -> x2, local copies, waits for them, and re-layouts: none -> 5.26 us  [body(): lax.all_to_all(sent.reshape(dp_count, part, shard_width), 'dp', split_axi...]
    dot_general x1, matrix products: 5.21 us -> 0.72 us  [body(): jnp.einsum('kr,rpd->kpd', selector, returned, precision=lax.Precision.HIG...]
    reshape x1 -> x5, local copies, waits for them, and re-layouts: 9.23 us -> 7.18 us  [the longest x2 6.8 us: body(): cand.astype(jnp.bfloat16).reshape(rows, mp_count, shard_width)]
    all_to_all x4 -> x5, starting transfers between devices: 33.1 us -> 33.7 us  [the longest x2 20 us: body(): lax.all_to_all(sent.reshape(dp_count, part, shard_width), 'dp', split_axi...]
  transfers between devices with their start and end apart: 6 -> 7, of which waited for: 3 -> 5; matrix products, arithmetic and copies ran while one was open for 18% -> 12% of each run, Pallas kernels for 0% -> 0%
where the time goes in v2:
time: 432 us; the launch traced here: 431 us
  blocking collectives  161 us (37%)
  waiting for transfers between devices  146 us (34%)
  starting transfers between devices  34 us (8%)
  local copies, waits for them, and re-layouts  29.2 us (7%)
  other arithmetic  24 us (6%)
  matrix products  21.8 us (5%)
  between operations  14.4 us (3%)
    all_to_all x2, blocking collectives, body(): lax.all_to_all(outgoing[:, h * part:(h + 1) * part], 'dp', split_axis=0,...  121 us
    all_to_all x2, waiting for transfers between devices, body(): lax.all_to_all(sent.reshape(dp_count, part, shard_width), 'dp', split_axi...  86.8 us
    all_to_all x2, waiting for transfers between devices, body(): lax.all_to_all(send, 'mp', split_axis=0, concat_axis=0, tiled=True)  52.2 us
    all_to_all x1, blocking collectives, body(): lax.all_to_all(jnp.concatenate(pieces, axis=1), 'mp', split_axis=0, conca...  30.6 us
    all_to_all x2, starting transfers between devices, body(): lax.all_to_all(sent.reshape(dp_count, part, shard_width), 'dp', split_axi...  20 us
    dot_general x2, matrix products, body(): lax.dot_general(g, c, (((0,), (1,)), ((), ())), preferred_element_type=jn...  10.2 us
    all_gather x1, blocking collectives, body(): lax.all_gather(jnp.stack([local_top, local_total, local_own]), 'mp', axis=0)  9.14 us
    all_to_all x2, starting transfers between devices, body(): lax.all_to_all(send, 'mp', split_axis=0, concat_axis=0, tiled=True)  9.09 us
  transfers between devices with their start and end apart: 7, of which 5 were waited for; matrix products, arithmetic and copies ran while one was open for 12% of the time, Pallas kernels for 0%

profile of v2, /device:TPU:1, one launch (start us, length us, event | category | flops | bytes accessed | tf_op | source)
XLA Modules:
  0.0 430.8 jit_solution(1757947262718900918)
XLA Ops:
  9.3 2.8 gather_fusion.1
  12.1 2.7 select_select_fusion
  15.3 64.3 %all_to_all.40 = bf16[64,64,256]{2,1,0:T(8,128)(2,1)} all-to-all(bf16[64,64,256]{2,1,0:T(8,128)(2,1)S(1)} %get-tuple-element.12), channel_id=1, replica_groups=mesh['dp'=64,'mp'=4] {'dp'}, dimensions={0} | all-to-all | bytes 4194304 | tf_op jit(solution)/shard_map/all_to_all | solution.py:35
  79.7 57.0 %all_to_all.41 = bf16[64,64,256]{2,1,0:T(8,128)(2,1)} all-to-all(bf16[64,64,256]{2,1,0:T(8,128)(2,1)S(1)} %get-tuple-element.11), channel_id=1, replica_groups=mesh['dp'=64,'mp'=4] {'dp'}, dimensions={0} | all-to-all | bytes 4194304 | tf_op jit(solution)/shard_map/all_to_all | solution.py:35
  136.6 4.6 %all-to-all-start.3 = ((bf16[4,1024,256]{2,1,0:T(8,128)(2,1)}), bf16[4,1024,256]{2,1,0:T(8,128)(2,1)}, u32[]{:S(2)}, u32[]{:S(2)}) async-start(bf16[4,1024,256]{2,1,0:T(8,128)(2,1)} %bitcast.68), calls=%async_computation.3 | async-start | bytes 4194304 | tf_op jit(solution)/shard_map/all_to_all | solution.py:45
  142.2 2.0 gather_fusion
  144.3 3.2 pad_maximum_fusion.1
  147.4 28.3 %all-to-all-done.3 = bf16[4,1024,256]{2,1,0:T(8,128)(2,1)} async-done(((bf16[4,1024,256]{2,1,0:T(8,128)(2,1)}), bf16[4,1024,256]{2,1,0:T(8,128)(2,1)}, u32[]{:S(2)}, u32[]{:S(2)}) %all-to-all-start.3) | async-done | bytes 2097184 | tf_op jit(solution)/shard_map/all_to_all | solution.py:45
  175.7 4.5 %all-to-all-start.1 = ((bf16[4,1152,256]{2,1,0:T(8,128)(2,1)}), bf16[4,1152,256]{2,1,0:T(8,128)(2,1)}, u32[]{:S(2)}, u32[]{:S(2)}) async-start(bf16[4,1152,256]{2,1,0:T(8,128)(2,1)} %pad_maximum_fusion.1), calls=%async_computation.1 | async-start | bytes 4718592 | tf_op jit(solution)/shard_map/all_to_all | solution.py:45
  181.2 3.1 fusion.25
  184.4 23.9 %all-to-all-done.1 = bf16[4,1152,256]{2,1,0:T(8,128)(2,1)} async-done(((bf16[4,1152,256]{2,1,0:T(8,128)(2,1)}), bf16[4,1152,256]{2,1,0:T(8,128)(2,1)}, u32[]{:S(2)}, u32[]{:S(2)}) %all-to-all-start.1) | async-done | bytes 2359328 | tf_op jit(solution)/shard_map/all_to_all | solution.py:45
  208.3 3.4 select_reduce_fusion.2
  213.0 9.1 %all-gather.1 = f32[4,3,512]{2,1,0:T(4,128)S(1)} all-gather(f32[1,3,512]{2,1,0:T(4,128)S(1)} %maximum_bitcast_fusion), channel_id=2, replica_groups=mesh['dp'=64,'mp'=4] {'mp'}, dimensions={0}, use_global_device_ids=true | all-gather | bytes 30720 | tf_op jit(solution)/shard_map/all_gather | solution.py:63
  222.8 2.8 multiply_convert_fusion
  225.6 4.0 copy.33
  229.6 4.6 %all-to-all-start.6 = ((bf16[4,1024,256]{2,1,0:T(8,128)(2,1)}), bf16[4,1024,256]{2,1,0:T(8,128)(2,1)}, u32[]{:S(2)}, u32[]{:S(2)}) async-start(bf16[4,1024,256]{2,1,0:T(8,128)(2,1)} %bitcast.26), calls=%async_computation.7 | async-start | bytes 4194304 | tf_op jit(solution)/shard_map/all_to_all | solution.py:100
  234.2 2.1 exponential_select_fusion
  239.6 1.9 slice.86
  242.3 2.8 copy.32
  246.6 1.7 pad_maximum_fusion
  248.3 7.3 %all-to-all-done.6 = bf16[4,1024,256]{2,1,0:T(8,128)(2,1)} async-done(((bf16[4,1024,256]{2,1,0:T(8,128)(2,1)}), bf16[4,1024,256]{2,1,0:T(8,128)(2,1)}, u32[]{:S(2)}, u32[]{:S(2)}) %all-to-all-start.6) | async-done | bytes 2097184 | tf_op jit(solution)/shard_map/all_to_all | solution.py:100
  255.6 30.6 %all_to_all.42 = bf16[4,1280,256]{2,1,0:T(8,128)(2,1)} all-to-all(bf16[4,1280,256]{2,1,0:T(8,128)(2,1)} %pad_maximum_fusion), channel_id=1, replica_groups=mesh['dp'=64,'mp'=4] {'mp'}, dimensions={0} | all-to-all | bytes 5242880 | tf_op jit(solution)/shard_map/all_to_all | solution.py:100
  286.2 14.0 %all-to-all-start.7 = ((bf16[64,64,256]{2,1,0:T(8,128)(2,1)}), bf16[64,64,256]{2,1,0:T(8,128)(2,1)S(1)}, u32[]{:S(2)}, u32[]{:S(2)}) async-start(bf16[64,64,256]{2,1,0:T(8,128)(2,1)} %bitcast.27), calls=%async_computation.8 | async-start | bytes 4194304 | tf_op jit(solution)/shard_map/all_to_all | solution.py:108
  300.2 5.1 %fusion.7 = f32[512,4,256]{2,0,1:T(8,128)} fusion(bf16[4,1024,256]{2,1,0:T(8,128)(2,1)} %all-to-all-done.3, f32[1024,512]{1,0:T(8,128)} %copy-done.5, f32[512]{0:T(512)S(1)} %get-tuple-element.8, pred[1024]{0:T(1024)(128)(4,1)S(1)} %reshape.118), kind=kOutput, calls=%fused_computation.26 | convolution fusion | flops 1075314688 | bytes 6294528 | tf_op jit(solution)/shard_map/dot_general | solution.py:78
  306.7 44.7 %all-to-all-done.7 = bf16[64,64,256]{2,1,0:T(8,128)(2,1)S(1)} async-done(((bf16[64,64,256]{2,1,0:T(8,128)(2,1)}), bf16[64,64,256]{2,1,0:T(8,128)(2,1)S(1)}, u32[]{:S(2)}, u32[]{:S(2)}) %all-to-all-start.7) | async-done | bytes 2097184 | tf_op jit(solution)/shard_map/all_to_all | solution.py:108
  351.4 6.0 %all-to-all-start.5 = ((bf16[64,64,256]{2,1,0:T(8,128)(2,1)}), bf16[64,64,256]{2,1,0:T(8,128)(2,1)}, u32[]{:S(2)}, u32[]{:S(2)}) async-start(bf16[64,64,256]{2,1,0:T(8,128)(2,1)} %bitcast.67), calls=%async_computation.6 | async-start | bytes 4194304 | tf_op jit(solution)/shard_map/all_to_all | solution.py:108
  357.7 5.2 %add_multiply_fusion = f32[512,4,256]{2,0,1:T(8,128)} fusion(f32[512,4,256]{2,0,1:T(8,128)} %fusion.7, bf16[4,1152,256]{2,1,0:T(8,128)(2,1)} %all-to-all-done.1, bf16[1024,512]{1,0:T(8,128)(2,1)S(1)} %copy-done.8, bf16[128,512]{1,0:T(8,128)(2,1)S(1)} %fusion.10), kind=kOutput, calls=%fused_computation.20 | convolution fusion | flops 1211367424 | bytes 7733248 | tf_op jit(solution)/shard_map/dot_general | solution.py:78
  364.0 2.5 copy.35
  366.5 42.1 %all-to-all-done.5 = bf16[64,64,256]{2,1,0:T(8,128)(2,1)} async-done(((bf16[64,64,256]{2,1,0:T(8,128)(2,1)}), bf16[64,64,256]{2,1,0:T(8,128)(2,1)}, u32[]{:S(2)}, u32[]{:S(2)}) %all-to-all-start.5) | async-done | bytes 2097184 | tf_op jit(solution)/shard_map/all_to_all | solution.py:108
  408.6 2.8 copy.34
  412.1 4.4 %copy.36 = f32[32,128,256]{2,1,0:T(8,128)} copy(f32[32,128,256]{2,0,1:T(8,128)S(1)} %fusion) | data formatting | bytes 8388608 | tf_op jit(solution)/shard_map/kr,rpd->kpd/dot_general | solution.py:117
  416.6 7.3 %scatter_fusion = f32[4096,256]{1,0:T(8,128)} fusion(f32[4096,256]{1,0:T(8,128)} %bitcast.65, s32[512]{0:T(512)S(1)} %compare_select_fusion, f32[512,256]{1,0:T(8,128)S(1)} %bitcast.71), kind=kCustom, calls=%fused_computation.2 | custom fusion | flops 131072 | bytes 1574912 | tf_op jit(solution)/shard_map/scatter-add | solution.py:118
  (65 shorter events, 15.7 us)
Async XLA Ops:
  7.2 2.1 copy-start
  136.6 4.6 %copy-start.9 = (bf16[512,256]{1,0:T(8,128)(2,1)S(1)}, bf16[512,256]{1,0:T(8,128)(2,1)}, u32[]{:S(2)}) copy-start(bf16[512,256]{1,0:T(8,128)(2,1)} %param.4) | copy-start | bytes 786436
  136.6 5.5 %copy-start.10 = (s32[512]{0:T(512)S(1)}, s32[512]{0:T(512)}, u32[]{:S(2)}) copy-start(s32[512]{0:T(512)} %param.6) | copy-start | bytes 6148
  136.6 39.1 %all-to-all-start.3 = ((bf16[4,1024,256]{2,1,0:T(8,128)(2,1)}), bf16[4,1024,256]{2,1,0:T(8,128)(2,1)}, u32[]{:S(2)}, u32[]{:S(2)}) async-start(bf16[4,1024,256]{2,1,0:T(8,128)(2,1)} %bitcast.68), calls=%async_computation.3 | async-start | bytes 4194304 | tf_op jit(solution)/shard_map/all_to_all | solution.py:45
  141.2 40.0 %all-gather.4.cloned.1.call-start = ((), (), s32[]{:S(2)}) async-start(), calls=%async_computation.9 | async-start | bytes 1310720 | tf_op jit(solution)/shard_map/all_gather | solution.py:29
  175.7 32.5 %all-to-all-start.1 = ((bf16[4,1152,256]{2,1,0:T(8,128)(2,1)}), bf16[4,1152,256]{2,1,0:T(8,128)(2,1)}, u32[]{:S(2)}, u32[]{:S(2)}) async-start(bf16[4,1152,256]{2,1,0:T(8,128)(2,1)} %pad_maximum_fusion.1), calls=%async_computation.1 | async-start | bytes 4718592 | tf_op jit(solution)/shard_map/all_to_all | solution.py:45
  184.4 38.5 %copy-start.5 = (f32[1024,512]{1,0:T(8,128)}, f32[1024,512]{1,0:T(8,128)S(1)}, u32[]{:S(2)}) copy-start(f32[1024,512]{1,0:T(8,128)S(1)} %get-tuple-element.20) | copy-start | bytes 6291460
  211.6 1.4 copy-start.2
  211.7 11.1 %copy-start.11 = (bf16[512,1024]{0,1:T(8,128)(2,1)S(1)}, bf16[512,1024]{0,1:T(8,128)(2,1)}, u32[]{:S(2)}) copy-start(bf16[512,1024]{0,1:T(8,128)(2,1)} %all-gather.4.cloned.1.call-done) | copy-start | bytes 3145732
  229.6 26.0 %all-to-all-start.6 = ((bf16[4,1024,256]{2,1,0:T(8,128)(2,1)}), bf16[4,1024,256]{2,1,0:T(8,128)(2,1)}, u32[]{:S(2)}, u32[]{:S(2)}) async-start(bf16[4,1024,256]{2,1,0:T(8,128)(2,1)} %bitcast.26), calls=%async_computation.7 | async-start | bytes 4194304 | tf_op jit(solution)/shard_map/all_to_all | solution.py:100
  236.4 1.6 copy-start.12
  236.5 1.0 copy-start.7
  239.5 2.8 copy-start.6
  286.2 65.3 %all-to-all-start.7 = ((bf16[64,64,256]{2,1,0:T(8,128)(2,1)}), bf16[64,64,256]{2,1,0:T(8,128)(2,1)S(1)}, u32[]{:S(2)}, u32[]{:S(2)}) async-start(bf16[64,64,256]{2,1,0:T(8,128)(2,1)} %bitcast.27), calls=%async_computation.8 | async-start | bytes 4194304 | tf_op jit(solution)/shard_map/all_to_all | solution.py:108
  300.2 5.1 %copy-start.3 = (bf16[4,1280,256]{2,1,0:T(8,128)(2,1)S(1)}, bf16[4,1280,256]{2,1,0:T(8,128)(2,1)}, u32[]{:S(2)}) copy-start(bf16[4,1280,256]{2,1,0:T(8,128)(2,1)} %all_to_all.42) | copy-start | bytes 7864324
  306.7 51.0 %copy-start.8 = (bf16[1024,512]{1,0:T(8,128)(2,1)S(1)}, bf16[1024,512]{1,0:T(8,128)(2,1)}, u32[]{:S(2)}) copy-start(bf16[1024,512]{1,0:T(8,128)(2,1)} %copy-done.7) | copy-start | bytes 3145732
  351.4 57.2 %all-to-all-start.5 = ((bf16[64,64,256]{2,1,0:T(8,128)(2,1)}), bf16[64,64,256]{2,1,0:T(8,128)(2,1)}, u32[]{:S(2)}, u32[]{:S(2)}) async-start(bf16[64,64,256]{2,1,0:T(8,128)(2,1)} %bitcast.67), calls=%async_computation.6 | async-start | bytes 4194304 | tf_op jit(solution)/shard_map/all_to_all | solution.py:108
  357.5 66.5 %reduce-scatter.2.cloned.1.call-start = ((), (), s32[]{:S(2)}) async-start(), calls=%async_computation.10 | async-start | bytes 2621440 | tf_op jit(solution)/shard_map/reduce_scatter | solution.py:81
  366.5 44.9 %copy-start.4 = (bf16[64,64,256]{2,0,1:T(8,128)(2,1)S(1)}, bf16[64,64,256]{2,0,1:T(8,128)(2,1)}, u32[]{:S(2)}) copy-start(bf16[64,64,256]{2,0,1:T(8,128)(2,1)} %copy.35) | copy-start | bytes 6291460
  416.6 7.3 %copy-start.1 = (bf16[4096,256]{1,0:T(8,128)(2,1)S(1)}, bf16[4096,256]{1,0:T(8,128)(2,1)}, u32[]{:S(2)}) copy-start(bf16[4096,256]{1,0:T(8,128)(2,1)} %param.5) | copy-start | bytes 6291460
Sparse Core Ops, SparseCore 0:
  144.4 30.5 all-gather.3
  363.0 31.3 reduce-scatter.1

commit v3 on v1

v3 whole, which is shorter than its diff:
```python
import jax
import jax.numpy as jnp
from jax import lax
from jax.sharding import PartitionSpec as P

PBS = 128


def body(queries, passages, positives, negatives):
    dp_count = lax.axis_size("dp")
    mp_count = lax.axis_size("mp")
    own_index = lax.axis_index("dp")
    width_index = lax.axis_index("mp")
    query_rows, shard_width = queries.shape
    factor = (shard_width * mp_count) ** (-0.5)
    block_count = passages.shape[0] // PBS
    pos_per = query_rows // mp_count
    quarter = PBS // mp_count
    blocks = passages.reshape(block_count, PBS, shard_width)

    asked = lax.dynamic_index_in_dim(negatives, own_index, 1, keepdims=False)
    outgoing = jnp.take(blocks, jnp.maximum(asked, 0), axis=0)
    outgoing = jnp.where((asked >= 0)[:, None, None], outgoing, jnp.zeros_like(outgoing))
    fetched = lax.all_to_all(
        outgoing.reshape(dp_count * mp_count, quarter, shard_width),
        ("dp", "mp"),
        split_axis=0,
        concat_axis=0,
        tiled=True,
    )
    neg = fetched.reshape(dp_count, mp_count, quarter, shard_width)
    wanted = lax.dynamic_index_in_dim(negatives, own_index, 0, keepdims=False)
    slot_ok = (wanted >= 0)[:, None, None]

    q_full = lax.all_gather(queries, "mp", axis=1, tiled=True)
    q4 = q_full.reshape(query_rows, mp_count, shard_width)
    positive_rows = jnp.take(passages, positives, axis=0)
    pos_all = lax.all_gather(positive_rows, "mp", axis=1, tiled=True)
    pos_mine = lax.dynamic_slice_in_dim(pos_all, width_index * pos_per, pos_per, 0)

    pos_scores = factor * lax.dot_general(
        pos_mine, q_full, (((1,), (1,)), ((), ())), preferred_element_type=jnp.float32
    )
    neg_scores = factor * lax.dot_general(
        neg, q4, (((1, 3), (1, 2)), ((), ())), preferred_element_type=jnp.float32
    )
    masked = jnp.where(slot_ok, neg_scores, jnp.float32(-1e30))
    local_top = jnp.maximum(jnp.max(pos_scores, axis=0), jnp.max(masked, axis=(0, 1)))
    local_total = jnp.sum(jnp.exp(pos_scores - local_top), axis=0) + jnp.sum(
        jnp.where(slot_ok, jnp.exp(masked - local_top), jnp.float32(0.0)), axis=(0, 1)
    )
    target = (width_index * pos_per + jnp.arange(pos_per, dtype=jnp.int32))[:, None] == jnp.arange(
        query_rows, dtype=jnp.int32
    )[None, :]
    local_own = jnp.sum(jnp.where(target, pos_scores, jnp.float32(0.0)), axis=0)
    stats = lax.all_gather(jnp.stack([local_top, local_total, local_own]), "mp", axis=0)
    top = jnp.max(stats[:, 0], axis=0)
    total = jnp.sum(stats[:, 1] * jnp.exp(stats[:, 0] - top), axis=0)
    own_score = jnp.sum(stats[:, 2], axis=0)
    lse = top + jnp.log(total)
    losses = lse - own_score

    pos_grads = (jnp.exp(pos_scores - lse) - target.astype(jnp.float32)).astype(jnp.bfloat16)
    neg_grads = jnp.where(slot_ok, jnp.exp(masked - lse), jnp.float32(0.0)).astype(jnp.bfloat16)

    query_part = lax.dot_general(
        pos_grads,
        pos_mine.reshape(pos_per, mp_count, shard_width),
        (((0,), (0,)), ((), ())),
        preferred_element_type=jnp.float32,
    ) + lax.dot_general(
        neg_grads, neg, (((0, 1), (0, 2)), ((), ())), preferred_element_type=jnp.float32
    )
    query_grad = lax.psum_scatter(factor * query_part, "mp", scatter_dimension=1, tiled=True)
    query_grad = query_grad.reshape(query_rows, shard_width)

    cand_grad = factor * lax.dot_general(
        neg_grads, q4, (((2,), (0,)), ((), ())), preferred_element_type=jnp.float32
    )
    sending = cand_grad.astype(jnp.bfloat16).transpose(0, 2, 1, 3)
    returned = lax.all_to_all(
        sending.reshape(dp_count * mp_count, quarter, shard_width),
        ("dp", "mp"),
        split_axis=0,
        concat_axis=0,
        tiled=True,
    )
    returned = returned.reshape(dp_count, PBS, shard_width).astype(jnp.float32)

    all_pos_grads = lax.all_gather(pos_grads, "mp", axis=0, tiled=True)
    pos_back = factor * jnp.dot(all_pos_grads, queries, preferred_element_type=jnp.float32)

    selector = (asked[None, :] == jnp.arange(block_count, dtype=jnp.int32)[:, None]).astype(
        jnp.float32
    )
    block_grad = jnp.einsum("kr,rpd->kpd", selector, returned, precision=lax.Precision.HIGHEST)
    passage_grad = block_grad.reshape(block_count * PBS, shard_width).at[positives].add(pos_back)
    return (losses, query_grad, passage_grad)


def solution(mesh):
    in_specs = (P("dp", "mp"), P("dp", "mp"), P("dp"), P())
    out_specs = (P("dp"), P("dp", "mp"), P("dp", "mp"))
    return jax.shard_map(body, mesh=mesh, in_specs=in_specs, out_specs=out_specs, check_vma=False)
```

time: 417 us -> 286 us (0.69)
  other arithmetic: 63.8 us -> 17.3 us
  blocking collectives: 56.9 us -> 22.2 us
  waiting for transfers between devices: 192 us -> 169 us
  local copies, waits for them, and re-layouts: 28.6 us -> 11.6 us
  starting transfers between devices: 33.2 us -> 27.6 us
    all_to_all x4 -> x2, waiting for transfers between devices: 192 us -> 99.1 us  [the longest x1 77.1 us: body(): lax.all_to_all(sending.reshape(dp_count * mp_count, quarter, shard_width)...]
    all_to_all x1 -> x0, blocking collectives: 47.9 us -> none  [body(): lax.all_to_all(cand_grad[:, pos_per:].astype(jnp.bfloat16), 'mp', split_a...]
    or x1 -> x0, other arithmetic: 35.5 us -> none  [body(): valid = (rows < pos_per) | slot_ok]
    all_gather x0 -> x1, waiting for transfers between devices: none -> 35.1 us  [body(): pos_all = lax.all_gather(positive_rows, 'mp', axis=1, tiled=True)]
    all_gather x1, waiting for transfers between devices: 0.02 us -> 34.5 us  [body(): q_full = lax.all_gather(queries, 'mp', axis=1, tiled=True)]
    all_gather x0 -> x1, blocking collectives: none -> 13.2 us  [body(): all_pos_grads = lax.all_gather(pos_grads, 'mp', axis=0, tiled=True)]
    reshape x1 -> x0, local copies, waits for them, and re-layouts: 9.23 us -> none  [body(): cand_grad.reshape(row_count, mp_count, shard_width).transpose(1, 0, 2)]
    gather x30 -> x0, other arithmetic: 6.93 us -> none  [body(): slot_ok = jnp.take(wanted, jnp.clip(slot_of_row, 0, dp_count - 1)) >= 0]
  transfers between devices with their start and end apart: 6 -> 5, of which waited for: 3 -> 4; matrix products, arithmetic and copies ran while one was open for 18% -> 11% of each run, Pallas kernels for 0% -> 0%
where the time goes in v3:
time: 286 us
  waiting for transfers between devices  169 us (59%)
  starting transfers between devices  27.6 us (10%)
  matrix products  24.2 us (8%)
  blocking collectives  22.2 us (8%)
  other arithmetic  17.3 us (6%)
  between operations  13.9 us (5%)
  local copies, waits for them, and re-layouts  11.6 us (4%)
    all_to_all x1, waiting for transfers between devices, body(): lax.all_to_all(sending.reshape(dp_count * mp_count, quarter, shard_width)...  77.1 us
    all_gather x1, waiting for transfers between devices, body(): pos_all = lax.all_gather(positive_rows, 'mp', axis=1, tiled=True)  35.1 us
    all_gather x1, waiting for transfers between devices, body(): q_full = lax.all_gather(queries, 'mp', axis=1, tiled=True)  34.5 us
    all_to_all x1, waiting for transfers between devices, body(): lax.all_to_all(outgoing.reshape(dp_count * mp_count, quarter, shard_width...  22 us
    all_to_all x1, starting transfers between devices, body(): lax.all_to_all(outgoing.reshape(dp_count * mp_count, quarter, shard_width...  16.7 us
    all_gather x1, blocking collectives, body(): all_pos_grads = lax.all_gather(pos_grads, 'mp', axis=0, tiled=True)  13.2 us
    all_to_all x1, starting transfers between devices, body(): lax.all_to_all(sending.reshape(dp_count * mp_count, quarter, shard_width)...  10.7 us
    all_gather x1, blocking collectives, body(): lax.all_gather(jnp.stack([local_top, local_total, local_own]), 'mp', axis=0)  9.02 us
  transfers between devices with their start and end apart: 5, of which 4 were waited for; matrix products, arithmetic and copies ran while one was open for 11% of the time, Pallas kernels for 0%

profile of v3, /device:TPU:1, one launch (start us, length us, event | category | flops | bytes accessed | tf_op | source)
XLA Modules:
  0.0 285.7 jit_solution(1490939043671389826)
XLA Ops:
  7.2 1.1 dynamic-slice_reduce_fusion
  8.3 0.9 compare_reduce_fusion
  9.3 0.1 broadcast_in_dim.87
  9.5 0.1 broadcast_in_dim.84
  9.7 2.8 gather_fusion.1
  12.5 4.3 %select_select_fusion = bf16[256,32,256]{2,1,0:T(8,128)(2,1)} fusion(bf16[256,32,256]{2,1,0:T(8,128)(2,1)} %bitcast.80, pred[256]{0:T(512)(128)(4,1)S(1)} %broadcast_in_dim.87, pred[256]{0:T(512)(128)(4,1)S(1)} %broadcast_in_dim.84), kind=kLoop, calls=%fused_computation.10 | loop fusion | flops 4194304 | bytes 8389120 | tf_op jit(solution)/shard_map/jit(_where)/select_n | solution.py:23
  16.8 16.7 %all-to-all-start = ((bf16[256,32,256]{2,1,0:T(8,128)(2,1)}), bf16[256,32,256]{2,1,0:T(8,128)(2,1)}, u32[]{:S(2)}, u32[]{:S(2)}) async-start(bf16[256,32,256]{2,1,0:T(8,128)(2,1)} %select_select_fusion), calls=%async_computation | async-start | bytes 8388608 | tf_op jit(solution)/shard_map/all_to_all | solution.py:24
  33.6 2.0 gather_fusion
  35.6 0.8 broadcast_select_fusion
  36.5 0.8 copy.22
  37.4 0.7 compare_bitcast_fusion
  38.1 35.1 %all-gather.5.cloned.1.call-done = bf16[512,1024]{1,0:T(8,128)(2,1)} async-done(((bf16[512,256]{1,0:T(8,128)(2,1)}), bf16[512,1024]{1,0:T(8,128)(2,1)}) %all-gather.5.cloned.1.call-update) | async-done | bytes 1048592 | tf_op jit(solution)/shard_map/all_gather | solution.py:38
  73.2 1.0 constant_dynamic-slice_fusion.1
  74.2 34.5 %all-gather.7.cloned.1.call-done = bf16[512,1024]{0,1:T(8,128)(2,1)} async-done(((bf16[512,256]{0,1:T(8,128)(2,1)}), bf16[512,1024]{0,1:T(8,128)(2,1)}) %all-gather.7.cloned.1.call-update) | async-done | bytes 1048592 | tf_op jit(solution)/shard_map/all_gather | solution.py:35
  108.7 1.5 fusion.19
  110.2 22.0 %all-to-all-done = bf16[256,32,256]{2,1,0:T(8,128)(2,1)} async-done(((bf16[256,32,256]{2,1,0:T(8,128)(2,1)}), bf16[256,32,256]{2,1,0:T(8,128)(2,1)}, u32[]{:S(2)}, u32[]{:S(2)}) %all-to-all-start) | async-done | bytes 4194336 | tf_op jit(solution)/shard_map/all_to_all | solution.py:24
  132.2 4.9 %fusion.3 = (f32[512]{0:T(512)S(1)}, f32[64,32,512,1]{2,1,3,0:T(8,128)S(1)}) fusion(pred[64]{0:T(512)(128)(4,1)S(1)} %compare_bitcast_fusion, bf16[64,4,32,256]{3,2,1,0:T(8,128)(2,1)} %bitcast.3, bf16[512,4,256,1]{0,2,1,3:T(8,128)(2,1)} %bitcast.83), kind=kOutput, calls=%fused_computation.11 | convolution fusion | flops 2150628864 | bytes 9439296 | tf_op jit(solution)/shard_map/dot_general | solution.py:44
  137.2 1.3 select_reduce_fusion
  138.6 9.0 %all-gather.1 = f32[4,3,512]{2,1,0:T(4,128)S(1)} all-gather(f32[1,3,512]{2,1,0:T(4,128)S(1)} %maximum_bitcast_fusion), channel_id=2, replica_groups=mesh['dp'=64,'mp'=4] {'mp'}, dimensions={0}, use_global_device_ids=true | all-gather | bytes 30720 | tf_op jit(solution)/shard_map/all_gather | solution.py:56
  147.7 0.6 fusion.17
  148.3 4.5 %multiply_convert_fusion = bf16[64,32,4,256]{3,1,2,0:T(8,128)(2,1)} fusion(bf16[512,4,256,1]{0,2,1,3:T(8,128)(2,1)S(1)} %bitcast.84, f32[64,32,512,1]{2,1,3,0:T(8,128)S(1)} %get-tuple-element.18, f32[512]{0:T(512)S(1)} %get-tuple-element.10, pred[64]{0:T(512)(128)(4,1)S(1)} %compare_bitcast_fusion), kind=kOutput, calls=%fused_computation.3 | convolution fusion | flops 2156920832 | bytes 9439296 | tf_op jit(solution)/shard_map/dot_general | solution.py:77
  152.8 10.7 %all-to-all-start.1 = ((bf16[256,32,256]{2,1,0:T(8,128)(2,1)}), bf16[256,32,256]{2,1,0:T(8,128)(2,1)}, u32[]{:S(2)}, u32[]{:S(2)}) async-start(bf16[256,32,256]{2,1,0:T(8,128)(2,1)} %bitcast.81), calls=%async_computation.2 | async-start | bytes 8388608 | tf_op jit(solution)/shard_map/all_to_all | solution.py:81
  163.5 0.2 reduce-scatter.2.cloned.1.call-start
  163.7 0.2 copy.25
  164.0 0.5 fusion.6
  164.5 7.3 %fusion.5 = f32[512,4,256]{2,0,1:T(8,128)} fusion(f32[512,4,256]{2,0,1:T(8,128)S(1)} %fusion.6, bf16[64,4,32,256]{3,2,1,0:T(8,128)(2,1)} %bitcast.3, f32[64,32,512,1]{2,1,3,0:T(8,128)} %copy-done.1, f32[512]{0:T(512)S(1)} %get-tuple-element.10, pred[64]{0:T(512)(128)(4,1)S(1)} %compare_bitcast_fusion), kind=kOutput, calls=%fused_computation.14 | convolution fusion | flops 2153775104 | bytes 12585024 | tf_op jit(solution)/shard_map/dot_general | solution.py:71
  171.8 13.2 %all_gather.19 = bf16[512,512]{1,0:T(8,128)(2,1)S(1)} all-gather(bf16[128,512]{1,0:T(8,128)(2,1)S(1)} %subtract_convert_fusion), channel_id=1, replica_groups=mesh['dp'=64,'mp'=4] {'mp'}, dimensions={0}, use_global_device_ids=true | all-gather | bytes 655360 | tf_op jit(solution)/shard_map/all_gather | solution.py:90
  185.0 0.3 convolution_multiply_fusion
  185.3 77.1 %all-to-all-done.1 = bf16[256,32,256]{2,1,0:T(8,128)(2,1)} async-done(((bf16[256,32,256]{2,1,0:T(8,128)(2,1)}), bf16[256,32,256]{2,1,0:T(8,128)(2,1)}, u32[]{:S(2)}, u32[]{:S(2)}) %all-to-all-start.1) | async-done | bytes 4194336 | tf_op jit(solution)/shard_map/all_to_all | solution.py:81
  262.4 5.2 %fusion.1 = f32[32,128,256]{2,0,1:T(8,128)S(1)} fusion(bf16[64,128,256]{2,1,0:T(8,128)(2,1)} %bitcast.24, s32[64]{0:T(128)S(1)} %get-tuple-element.7), kind=kOutput, calls=%fused_computation.6 | convolution fusion | flops 134219776 | bytes 8388864 | tf_op jit(solution)/shard_map/kr,rpd->kpd/dot_general | solution.py:96
  267.6 4.4 %copy.31 = f32[32,128,256]{2,1,0:T(8,128)} copy(f32[32,128,256]{2,0,1:T(8,128)S(1)} %fusion.1) | data formatting | bytes 8388608 | tf_op jit(solution)/shard_map/kr,rpd->kpd/dot_general | solution.py:96
  272.0 7.2 %scatter_fusion = f32[4096,256]{1,0:T(8,128)} fusion(f32[4096,256]{1,0:T(8,128)} %bitcast.79, s32[512]{0:T(512)S(1)} %compare_select_fusion, f32[512,256]{1,0:T(8,128)S(1)} %convolution_multiply_fusion), kind=kCustom, calls=%fused_computation.2 | custom fusion | flops 131072 | bytes 1574912 | tf_op jit(solution)/shard_map/scatter-add | solution.py:97
  (31 shorter events, 0.6 us)
Async XLA Ops:
  7.2 2.5 copy-start
  16.8 16.7 %copy-start.4 = (s32[512]{0:T(512)S(1)}, s32[512]{0:T(512)}, u32[]{:S(2)}) copy-start(s32[512]{0:T(512)} %param.6) | copy-start | bytes 6148
  16.8 19.6 %copy-start.2 = (bf16[512,256]{1,0:T(8,128)(2,1)S(1)}, bf16[512,256]{1,0:T(8,128)(2,1)}, u32[]{:S(2)}) copy-start(bf16[512,256]{1,0:T(8,128)(2,1)} %param.4) | copy-start | bytes 786436
  16.8 115.4 %all-to-all-start = ((bf16[256,32,256]{2,1,0:T(8,128)(2,1)}), bf16[256,32,256]{2,1,0:T(8,128)(2,1)}, u32[]{:S(2)}, u32[]{:S(2)}) async-start(bf16[256,32,256]{2,1,0:T(8,128)(2,1)} %select_select_fusion), calls=%async_computation | async-start | bytes 8388608 | tf_op jit(solution)/shard_map/all_to_all | solution.py:24
  33.5 39.7 %all-gather.5.cloned.1.call-start = ((), (), s32[]{:S(2)}) async-start(), calls=%async_computation.3 | async-start | bytes 1310720 | tf_op jit(solution)/shard_map/all_gather | solution.py:38
  36.4 72.2 %all-gather.7.cloned.1.call-start = ((), (), s32[]{:S(2)}) async-start(), calls=%async_computation.4 | async-start | bytes 1310720 | tf_op jit(solution)/shard_map/all_gather | solution.py:35
  137.2 15.6 %copy-start.1 = (f32[64,32,512,1]{2,1,3,0:T(8,128)}, f32[64,32,512,1]{2,1,3,0:T(8,128)S(1)}, u32[]{:S(2)}) copy-start(f32[64,32,512,1]{2,1,3,0:T(8,128)S(1)} %get-tuple-element.18) | copy-start | bytes 12582916
  137.2 11.1 %copy-start.3 = (bf16[512,1024]{0,1:T(8,128)(2,1)S(1)}, bf16[512,1024]{0,1:T(8,128)(2,1)}, u32[]{:S(2)}) copy-start(bf16[512,1024]{0,1:T(8,128)(2,1)} %all-gather.7.cloned.1.call-done) | copy-start | bytes 3145732
  152.8 109.5 %all-to-all-start.1 = ((bf16[256,32,256]{2,1,0:T(8,128)(2,1)}), bf16[256,32,256]{2,1,0:T(8,128)(2,1)}, u32[]{:S(2)}, u32[]{:S(2)}) async-start(bf16[256,32,256]{2,1,0:T(8,128)(2,1)} %bitcast.81), calls=%async_computation.2 | async-start | bytes 8388608 | tf_op jit(solution)/shard_map/all_to_all | solution.py:81
  163.5 115.7 %reduce-scatter.2.cloned.1.call-start = ((), (), s32[]{:S(2)}) async-start(), calls=%async_computation.5 | async-start | bytes 2621440 | tf_op jit(solution)/shard_map/reduce_scatter | solution.py:74
Sparse Core Ops, SparseCore 0:
  36.7 36.4 all-gather.4
  75.0 33.6 all-gather.6
  171.9 47.9 reduce-scatter.1

commit v4 on v3

--- a/solution.py
+++ b/solution.py
@@ -20,7 +20,6 @@
 
     asked = lax.dynamic_index_in_dim(negatives, own_index, 1, keepdims=False)
     outgoing = jnp.take(blocks, jnp.maximum(asked, 0), axis=0)
-    outgoing = jnp.where((asked >= 0)[:, None, None], outgoing, jnp.zeros_like(outgoing))
     fetched = lax.all_to_all(
         outgoing.reshape(dp_count * mp_count, quarter, shard_width),
         ("dp", "mp"),
@@ -32,11 +31,13 @@
     wanted = lax.dynamic_index_in_dim(negatives, own_index, 0, keepdims=False)
     slot_ok = (wanted >= 0)[:, None, None]
 
-    q_full = lax.all_gather(queries, "mp", axis=1, tiled=True)
+    positive_rows = jnp.take(passages, positives, axis=0)
+    both = lax.all_gather(
+        jnp.concatenate([queries, positive_rows], axis=0), "mp", axis=1, tiled=True
+    )
+    q_full = both[:query_rows]
     q4 = q_full.reshape(query_rows, mp_count, shard_width)
-    positive_rows = jnp.take(passages, positives, axis=0)
-    pos_all = lax.all_gather(positive_rows, "mp", axis=1, tiled=True)
-    pos_mine = lax.dynamic_slice_in_dim(pos_all, width_index * pos_per, pos_per, 0)
+    pos_mine = lax.dynamic_slice_in_dim(both, query_rows + width_index * pos_per, pos_per, 0)
 
     pos_scores = factor * lax.dot_general(
         pos_mine, q_full, (((1,), (1,)), ((), ())), preferred_element_type=jnp.float32
@@ -85,16 +86,18 @@
         concat_axis=0,
         tiled=True,
     )
-    returned = returned.reshape(dp_count, PBS, shard_width).astype(jnp.float32)
+    returned = returned.reshape(dp_count, PBS * shard_width)
 
     all_pos_grads = lax.all_gather(pos_grads, "mp", axis=0, tiled=True)
     pos_back = factor * jnp.dot(all_pos_grads, queries, preferred_element_type=jnp.float32)
+    pos_part = jnp.zeros((block_count * PBS, shard_width), jnp.float32).at[positives].add(pos_back)
+    returned, pos_part = lax.optimization_barrier((returned, pos_part))
 
     selector = (asked[None, :] == jnp.arange(block_count, dtype=jnp.int32)[:, None]).astype(
-        jnp.float32
+        jnp.bfloat16
     )
-    block_grad = jnp.einsum("kr,rpd->kpd", selector, returned, precision=lax.Precision.HIGHEST)
-    passage_grad = block_grad.reshape(block_count * PBS, shard_width).at[positives].add(pos_back)
+    block_grad = jnp.dot(selector, returned, preferred_element_type=jnp.float32)
+    passage_grad = block_grad.reshape(block_count * PBS, shard_width) + pos_part
     return (losses, query_grad, passage_grad)
 
 

time: 286 us -> 293 us (1.024)
  local copies, waits for them, and re-layouts: 11.6 us -> 21 us
  waiting for transfers between devices: 169 us -> 161 us
  other arithmetic: 17.3 us -> 21.4 us
    all_gather x2 -> x1, waiting for transfers between devices: 69.6 us -> 53 us  [body(): lax.all_gather(jnp.concatenate([queries, positive_rows], axis=0), 'mp', a...]
    all_to_all x1, waiting for transfers between devices: 22 us -> 36.6 us  [body(): lax.all_to_all(outgoing.reshape(dp_count * mp_count, quarter, shard_width...]
    reshape x0 -> x2, local copies, waits for them, and re-layouts: none -> 12.2 us  [the longest x1 7.37 us: body(): returned = returned.reshape(dp_count, PBS * shard_width)]
    add x0 -> x1, other arithmetic: none -> 6.02 us  [body(): passage_grad = block_grad.reshape(block_count * PBS, shard_width) + pos_part]
    all_to_all x1, waiting for transfers between devices: 77.1 us -> 71.6 us  [body(): lax.all_to_all(sending.reshape(dp_count * mp_count, quarter, shard_width)...]
    dot_general x1 -> x0, local copies, waits for them, and re-layouts: 4.45 us -> none  [body(): jnp.einsum('kr,rpd->kpd', selector, returned, precision=lax.Precision.HIG...]
  transfers between devices with their start and end apart: 5 -> 4, of which waited for: 4 -> 3; matrix products, arithmetic and copies ran while one was open for 11% -> 16% of each run, Pallas kernels for 0% -> 0%
where the time goes in v4:
time: 293 us; the launch traced here: 292 us
  waiting for transfers between devices  161 us (55%)
  starting transfers between devices  27.6 us (9%)
  matrix products  24.1 us (8%)
  blocking collectives  22.3 us (8%)
  other arithmetic  21.4 us (7%)
  local copies, waits for them, and re-layouts  21 us (7%)
  between operations  14.3 us (5%)
    all_to_all x1, waiting for transfers between devices, body(): lax.all_to_all(sending.reshape(dp_count * mp_count, quarter, shard_width)...  71.6 us
    all_gather x1, waiting for transfers between devices, body(): lax.all_gather(jnp.concatenate([queries, positive_rows], axis=0), 'mp', a...  53 us
    all_to_all x1, waiting for transfers between devices, body(): lax.all_to_all(outgoing.reshape(dp_count * mp_count, quarter, shard_width...  36.6 us
    all_to_all x1, starting transfers between devices, body(): lax.all_to_all(outgoing.reshape(dp_count * mp_count, quarter, shard_width...  16.7 us
    all_gather x1, blocking collectives, body(): all_pos_grads = lax.all_gather(pos_grads, 'mp', axis=0, tiled=True)  13.2 us
    all_to_all x1, starting transfers between devices, body(): lax.all_to_all(sending.reshape(dp_count * mp_count, quarter, shard_width)...  10.6 us
    all_gather x1, blocking collectives, body(): lax.all_gather(jnp.stack([local_top, local_total, local_own]), 'mp', axis=0)  9.02 us
    reshape x1, local copies, waits for them, and re-layouts, body(): returned = returned.reshape(dp_count, PBS * shard_width)  7.37 us
  transfers between devices with their start and end apart: 4, of which 3 were waited for; matrix products, arithmetic and copies ran while one was open for 16% of the time, Pallas kernels for 0%

profile of v4, /device:TPU:1, one launch (start us, length us, event | category | flops | bytes accessed | tf_op | source)
XLA Modules:
  0.0 291.8 jit_solution(8093044953717239663)
XLA Ops:
  7.2 1.1 compare_reduce_fusion
  8.3 0.9 dynamic-slice_reduce_fusion
  9.5 2.8 gather_fusion.1
  12.3 4.1 %broadcast_select_fusion = bf16[256,32,256]{2,1,0:T(8,128)(2,1)} fusion(bf16[256,32,256]{2,1,0:T(8,128)(2,1)} %bitcast.74, pred[256]{0:T(512)(128)(4,1)S(1)} %broadcast_in_dim.71), kind=kLoop, calls=%fused_computation.8 | loop fusion | flops 2097152 | bytes 8388864 | tf_op jit(solution)/shard_map/jit(_take)/select_n | solution.py:22
  16.3 16.7 %all-to-all-start = ((bf16[256,32,256]{2,1,0:T(8,128)(2,1)}), bf16[256,32,256]{2,1,0:T(8,128)(2,1)}, u32[]{:S(2)}, u32[]{:S(2)}) async-start(bf16[256,32,256]{2,1,0:T(8,128)(2,1)} %broadcast_select_fusion), calls=%async_computation | async-start | bytes 8388608 | tf_op jit(solution)/shard_map/all_to_all | solution.py:23
  33.1 2.0 gather_fusion
  35.2 0.8 pad_maximum_fusion
  36.1 0.7 compare_bitcast_fusion
  36.8 53.0 %all-gather.4.cloned.1.call-done = bf16[1024,1024]{1,0:T(8,128)(2,1)} async-done(((bf16[1024,256]{1,0:T(8,128)(2,1)}), bf16[1024,1024]{1,0:T(8,128)(2,1)}) %all-gather.4.cloned.1.call-update) | async-done | bytes 2097168 | tf_op jit(solution)/shard_map/all_gather | solution.py:35
  89.8 1.3 slice.21
  91.1 1.4 copy.20
  92.4 1.0 constant_dynamic-slice_fusion.1
  93.4 1.7 fusion.19
  95.1 36.6 %all-to-all-done = bf16[256,32,256]{2,1,0:T(8,128)(2,1)} async-done(((bf16[256,32,256]{2,1,0:T(8,128)(2,1)}), bf16[256,32,256]{2,1,0:T(8,128)(2,1)}, u32[]{:S(2)}, u32[]{:S(2)}) %all-to-all-start) | async-done | bytes 4194336 | tf_op jit(solution)/shard_map/all_to_all | solution.py:23
  131.7 4.9 %fusion.1 = (f32[512]{0:T(512)S(1)}, f32[64,32,512,1]{2,1,3,0:T(8,128)S(1)}) fusion(pred[64]{0:T(512)(128)(4,1)S(1)} %compare_bitcast_fusion, bf16[64,4,32,256]{3,2,1,0:T(8,128)(2,1)} %bitcast.3, bf16[512,4,256,1]{0,2,1,3:T(8,128)(2,1)} %bitcast.77), kind=kOutput, calls=%fused_computation.9 | convolution fusion | flops 2150628864 | bytes 9439296 | tf_op jit(solution)/shard_map/dot_general | solution.py:45
  136.7 1.3 select_reduce_fusion
  138.2 9.0 %all-gather.1 = f32[4,3,512]{2,1,0:T(4,128)S(1)} all-gather(f32[1,3,512]{2,1,0:T(4,128)S(1)} %maximum_bitcast_fusion), channel_id=2, replica_groups=mesh['dp'=64,'mp'=4] {'mp'}, dimensions={0}, use_global_device_ids=true | all-gather | bytes 30720 | tf_op jit(solution)/shard_map/all_gather | solution.py:57
  147.2 0.6 fusion.17
  147.8 4.5 %multiply_convert_fusion = bf16[64,32,4,256]{3,1,2,0:T(8,128)(2,1)} fusion(bf16[512,4,256,1]{0,2,1,3:T(8,128)(2,1)S(1)} %bitcast.78, f32[64,32,512,1]{2,1,3,0:T(8,128)S(1)} %get-tuple-element.22, f32[512]{0:T(512)S(1)} %get-tuple-element.14, pred[64]{0:T(512)(128)(4,1)S(1)} %compare_bitcast_fusion), kind=kOutput, calls=%fused_computation.3 | convolution fusion | flops 2156920832 | bytes 9439296 | tf_op jit(solution)/shard_map/dot_general | solution.py:78
  152.3 10.6 %all-to-all-start.1 = ((bf16[256,32,256]{2,1,0:T(8,128)(2,1)}), bf16[256,32,256]{2,1,0:T(8,128)(2,1)}, u32[]{:S(2)}, u32[]{:S(2)}) async-start(bf16[256,32,256]{2,1,0:T(8,128)(2,1)} %bitcast.75), calls=%async_computation.2 | async-start | bytes 8388608 | tf_op jit(solution)/shard_map/all_to_all | solution.py:82
  163.0 0.2 reduce-scatter.2.cloned.1.call-start
  163.2 0.2 copy.23
  163.5 0.5 fusion.6
  164.0 7.3 %fusion.3 = f32[512,4,256]{2,0,1:T(8,128)} fusion(f32[512,4,256]{2,0,1:T(8,128)S(1)} %fusion.6, bf16[64,4,32,256]{3,2,1,0:T(8,128)(2,1)} %bitcast.3, f32[64,32,512,1]{2,1,3,0:T(8,128)} %copy-done.1, f32[512]{0:T(512)S(1)} %get-tuple-element.14, pred[64]{0:T(512)(128)(4,1)S(1)} %compare_bitcast_fusion), kind=kOutput, calls=%fused_computation.12 | convolution fusion | flops 2153775104 | bytes 12585024 | tf_op jit(solution)/shard_map/dot_general | solution.py:72
  171.3 13.2 %all_gather.15 = bf16[512,512]{1,0:T(8,128)(2,1)S(1)} all-gather(bf16[128,512]{1,0:T(8,128)(2,1)S(1)} %subtract_convert_fusion), channel_id=1, replica_groups=mesh['dp'=64,'mp'=4] {'mp'}, dimensions={0}, use_global_device_ids=true | all-gather | bytes 655360 | tf_op jit(solution)/shard_map/all_gather | solution.py:91
  184.5 0.3 convolution_multiply_fusion
  184.8 5.5 %scatter_custom_fusion = f32[4096,256]{1,0:T(8,128)} fusion(s32[512]{0:T(512)S(1)} %compare_select_fusion, f32[512,256]{1,0:T(8,128)S(1)} %convolution_multiply_fusion, f32[]{:T(128)} %constant.72.clone.1), kind=kCustom, calls=%fused_computation.13 | custom fusion | flops 131072 | bytes 4194308 | tf_op jit(solution)/shard_map/scatter-add | solution.py:93
  190.3 71.6 %all-to-all-done.1 = bf16[256,32,256]{2,1,0:T(8,128)(2,1)} async-done(((bf16[256,32,256]{2,1,0:T(8,128)(2,1)}), bf16[256,32,256]{2,1,0:T(8,128)(2,1)}, u32[]{:S(2)}, u32[]{:S(2)}) %all-to-all-start.1) | async-done | bytes 4194336 | tf_op jit(solution)/shard_map/all_to_all | solution.py:82
  261.9 7.4 %reshape.103 = bf16[64,32768]{1,0:T(8,128)(2,1)} reshape(bf16[256,32,256]{2,1,0:T(8,128)(2,1)} %all-to-all-done.1) | data formatting | bytes 8388608 | tf_op jit(solution)/shard_map/reshape | solution.py:89
  269.2 4.8 %fusion.8 = f32[32,32768]{1,0:T(8,128)} fusion(bf16[64,32768]{1,0:T(8,128)(2,1)} %reshape.103, s32[64]{0:T(128)S(1)} %get-tuple-element.9), kind=kOutput, calls=%fused_computation.29 | convolution fusion | flops 134219776 | bytes 8388864 | tf_op jit(solution)/shard_map/dot_general | solution.py:99
  274.1 4.9 %reshape.104 = f32[4096,256]{1,0:T(8,128)} reshape(f32[32,32768]{1,0:T(8,128)} %fusion.8) | data formatting | bytes 8388608 | tf_op jit(solution)/shard_map/reshape | solution.py:100
  279.0 6.0 %add.79 = f32[4096,256]{1,0:T(8,128)} add(f32[4096,256]{1,0:T(8,128)} %reshape.104, f32[4096,256]{1,0:T(8,128)} %scatter_custom_fusion) | non-fusion elementwise | flops 1048576 | bytes 12582912 | tf_op jit(solution)/shard_map/add | solution.py:100
  (29 shorter events, 0.8 us)
Async XLA Ops:
  7.2 2.3 copy-start
  16.3 16.7 %copy-start.4 = (s32[512]{0:T(512)S(1)}, s32[512]{0:T(512)}, u32[]{:S(2)}) copy-start(s32[512]{0:T(512)} %param.6) | copy-start | bytes 6148
  16.3 18.9 %copy-start.3 = (bf16[512,256]{1,0:T(8,128)(2,1)S(1)}, bf16[512,256]{1,0:T(8,128)(2,1)}, u32[]{:S(2)}) copy-start(bf16[512,256]{1,0:T(8,128)(2,1)} %param.4) | copy-start | bytes 786436
  16.3 115.4 %all-to-all-start = ((bf16[256,32,256]{2,1,0:T(8,128)(2,1)}), bf16[256,32,256]{2,1,0:T(8,128)(2,1)}, u32[]{:S(2)}, u32[]{:S(2)}) async-start(bf16[256,32,256]{2,1,0:T(8,128)(2,1)} %broadcast_select_fusion), calls=%async_computation | async-start | bytes 8388608 | tf_op jit(solution)/shard_map/all_to_all | solution.py:23
  33.0 56.8 %all-gather.4.cloned.1.call-start = ((), (), s32[]{:S(2)}) async-start(), calls=%async_computation.3 | async-start | bytes 2621440 | tf_op jit(solution)/shard_map/all_gather | solution.py:35
  136.7 15.7 %copy-start.1 = (f32[64,32,512,1]{2,1,3,0:T(8,128)}, f32[64,32,512,1]{2,1,3,0:T(8,128)S(1)}, u32[]{:S(2)}) copy-start(f32[64,32,512,1]{2,1,3,0:T(8,128)S(1)} %get-tuple-element.22) | copy-start | bytes 12582916
  136.7 11.1 %copy-start.2 = (bf16[512,1024]{0,1:T(8,128)(2,1)S(1)}, bf16[512,1024]{0,1:T(8,128)(2,1)}, u32[]{:S(2)}) copy-start(bf16[512,1024]{0,1:T(8,128)(2,1)} %copy.20) | copy-start | bytes 3145732
  152.3 109.5 %all-to-all-start.1 = ((bf16[256,32,256]{2,1,0:T(8,128)(2,1)}), bf16[256,32,256]{2,1,0:T(8,128)(2,1)}, u32[]{:S(2)}, u32[]{:S(2)}) async-start(bf16[256,32,256]{2,1,0:T(8,128)(2,1)} %bitcast.75), calls=%async_computation.2 | async-start | bytes 8388608 | tf_op jit(solution)/shard_map/all_to_all | solution.py:82
  163.0 122.0 %reduce-scatter.2.cloned.1.call-start = ((), (), s32[]{:S(2)}) async-start(), calls=%async_computation.4 | async-start | bytes 2621440 | tf_op jit(solution)/shard_map/reduce_scatter | solution.py:75
Sparse Core Ops, SparseCore 0:
  36.2 53.5 all-gather.3
  171.4 47.9 reduce-scatter.1

commit v5 on v4

--- a/solution.py
+++ b/solution.py
@@ -19,7 +19,7 @@
     blocks = passages.reshape(block_count, PBS, shard_width)
 
     asked = lax.dynamic_index_in_dim(negatives, own_index, 1, keepdims=False)
-    outgoing = jnp.take(blocks, jnp.maximum(asked, 0), axis=0)
+    outgoing = jnp.take(blocks, jnp.maximum(asked, 0), axis=0, mode="clip")
     fetched = lax.all_to_all(
         outgoing.reshape(dp_count * mp_count, quarter, shard_width),
         ("dp", "mp"),
@@ -31,7 +31,7 @@
     wanted = lax.dynamic_index_in_dim(negatives, own_index, 0, keepdims=False)
     slot_ok = (wanted >= 0)[:, None, None]
 
-    positive_rows = jnp.take(passages, positives, axis=0)
+    positive_rows = jnp.take(passages, positives, axis=0, mode="clip")
     both = lax.all_gather(
         jnp.concatenate([queries, positive_rows], axis=0), "mp", axis=1, tiled=True
     )
@@ -86,7 +86,7 @@
         concat_axis=0,
         tiled=True,
     )
-    returned = returned.reshape(dp_count, PBS * shard_width)
+    returned = returned.reshape(dp_count, PBS, shard_width)
 
     all_pos_grads = lax.all_gather(pos_grads, "mp", axis=0, tiled=True)
     pos_back = factor * jnp.dot(all_pos_grads, queries, preferred_element_type=jnp.float32)
@@ -96,7 +96,7 @@
     selector = (asked[None, :] == jnp.arange(block_count, dtype=jnp.int32)[:, None]).astype(
         jnp.bfloat16
     )
-    block_grad = jnp.dot(selector, returned, preferred_element_type=jnp.float32)
+    block_grad = jnp.einsum("kr,rpd->kpd", selector, returned, preferred_element_type=jnp.float32)
     passage_grad = block_grad.reshape(block_count * PBS, shard_width) + pos_part
     return (losses, query_grad, passage_grad)
 

time: 293 us -> 275 us (0.939)
  local copies, waits for them, and re-layouts: 21 us -> 11.5 us
  other arithmetic: 21.4 us -> 13.2 us
    reshape x2 -> x0, local copies, waits for them, and re-layouts: 12.2 us -> none  [the longest x1 7.37 us: body(): returned = returned.reshape(dp_count, PBS * shard_width)]
    select_n x3 -> x1, other arithmetic: 4.2 us -> 0.01 us  [body(): jnp.zeros((block_count * PBS, shard_width), jnp.float32).at[positives]]
    add x1, other arithmetic: 6.02 us -> 2.82 us  [body(): passage_grad = block_grad.reshape(block_count * PBS, shard_width) + pos_part]
  transfers between devices with their start and end apart: 4 -> 4, of which waited for: 3 -> 3; matrix products, arithmetic and copies ran while one was open for 16% -> 12% of each run, Pallas kernels for 0% -> 0%
where the time goes in v5:
time: 275 us; the launch traced here: 274 us
  waiting for transfers between devices  161 us (59%)
  starting transfers between devices  27.6 us (10%)
  matrix products  24.4 us (9%)
  blocking collectives  22.2 us (8%)
  between operations  14.2 us (5%)
  other arithmetic  13.2 us (5%)
  local copies, waits for them, and re-layouts  11.5 us (4%)
    all_to_all x1, waiting for transfers between devices, body(): lax.all_to_all(sending.reshape(dp_count * mp_count, quarter, shard_width)...  71.5 us
    all_gather x1, waiting for transfers between devices, body(): lax.all_gather(jnp.concatenate([queries, positive_rows], axis=0), 'mp', a...  53.2 us
    all_to_all x1, waiting for transfers between devices, body(): lax.all_to_all(outgoing.reshape(dp_count * mp_count, quarter, shard_width...  36.6 us
    all_to_all x1, starting transfers between devices, body(): lax.all_to_all(outgoing.reshape(dp_count * mp_count, quarter, shard_width...  16.7 us
    all_gather x1, blocking collectives, body(): all_pos_grads = lax.all_gather(pos_grads, 'mp', axis=0, tiled=True)  13.2 us
    all_to_all x1, starting transfers between devices, body(): lax.all_to_all(sending.reshape(dp_count * mp_count, quarter, shard_width)...  10.6 us
    all_gather x1, blocking collectives, body(): lax.all_gather(jnp.stack([local_top, local_total, local_own]), 'mp', axis=0)  9.02 us
    dot_general x1, matrix products, body(): lax.dot_general(neg_grads, neg, (((0, 1), (0, 2)), ((), ())), preferred_e...  7.29 us
  transfers between devices with their start and end apart: 4, of which 3 were waited for; matrix products, arithmetic and copies ran while one was open for 12% of the time, Pallas kernels for 0%

profile of v5, /device:TPU:1, one launch (start us, length us, event | category | flops | bytes accessed | tf_op | source)
XLA Modules:
  0.0 274.5 jit_solution(10906907558701376987)
XLA Ops:
  7.2 1.1 dynamic-slice_reduce_fusion
  8.3 0.5 copy-done
  8.8 2.8 %gather_fusion.1 = bf16[64,128,256]{2,1,0:T(8,128)(2,1)} fusion(bf16[32,128,256]{2,1,0:T(8,128)(2,1)S(1)} %bitcast.78, s32[1024]{0:T(1024)S(1)} %pad_clamp_fusion), kind=kCustom, calls=%fused_computation.1 | custom fusion | bytes 8388864 | tf_op jit(solution)/shard_map/jit(_take)/gather | solution.py:22
  11.6 16.7 %all-to-all-start = ((bf16[256,32,256]{2,1,0:T(8,128)(2,1)}), bf16[256,32,256]{2,1,0:T(8,128)(2,1)}, u32[]{:S(2)}, u32[]{:S(2)}) async-start(bf16[256,32,256]{2,1,0:T(8,128)(2,1)} %bitcast.79), calls=%async_computation | async-start | bytes 8388608 | tf_op jit(solution)/shard_map/all_to_all | solution.py:23
  28.3 2.0 gather_fusion
  30.3 0.8 pad_maximum_fusion
  31.2 0.7 compare_bitcast_fusion
  31.9 53.2 %all-gather.4.cloned.1.call-done = bf16[1024,1024]{1,0:T(8,128)(2,1)} async-done(((bf16[1024,256]{1,0:T(8,128)(2,1)}), bf16[1024,1024]{1,0:T(8,128)(2,1)}) %all-gather.4.cloned.1.call-update) | async-done | bytes 2097168 | tf_op jit(solution)/shard_map/all_gather | solution.py:35
  85.1 1.3 slice.21
  86.4 1.4 copy.22
  87.7 1.0 constant_dynamic-slice_fusion.1
  88.7 1.7 fusion.22
  90.4 36.6 %all-to-all-done = bf16[256,32,256]{2,1,0:T(8,128)(2,1)} async-done(((bf16[256,32,256]{2,1,0:T(8,128)(2,1)}), bf16[256,32,256]{2,1,0:T(8,128)(2,1)}, u32[]{:S(2)}, u32[]{:S(2)}) %all-to-all-start) | async-done | bytes 4194336 | tf_op jit(solution)/shard_map/all_to_all | solution.py:23
  127.0 4.9 %fusion.3 = (f32[512]{0:T(512)S(1)}, f32[64,32,512,1]{2,1,3,0:T(8,128)S(1)}) fusion(pred[64]{0:T(512)(128)(4,1)S(1)} %compare_bitcast_fusion, bf16[64,4,32,256]{3,2,1,0:T(8,128)(2,1)} %bitcast.3, bf16[512,4,256,1]{0,2,1,3:T(8,128)(2,1)} %bitcast.82), kind=kOutput, calls=%fused_computation.11 | convolution fusion | flops 2150628864 | bytes 9439296 | tf_op jit(solution)/shard_map/dot_general | solution.py:45
  132.0 1.3 select_reduce_fusion
  133.3 0.1 exponential_reduce_fusion
  133.4 9.0 %all-gather.1 = f32[4,3,512]{2,1,0:T(4,128)S(1)} all-gather(f32[1,3,512]{2,1,0:T(4,128)S(1)} %maximum_bitcast_fusion), channel_id=2, replica_groups=mesh['dp'=64,'mp'=4] {'mp'}, dimensions={0}, use_global_device_ids=true | all-gather | bytes 30720 | tf_op jit(solution)/shard_map/all_gather | solution.py:57
  142.5 0.6 fusion.20
  143.1 4.5 %multiply_convert_fusion = bf16[64,32,4,256]{3,1,2,0:T(8,128)(2,1)} fusion(bf16[512,4,256,1]{0,2,1,3:T(8,128)(2,1)S(1)} %bitcast.83, f32[64,32,512,1]{2,1,3,0:T(8,128)S(1)} %get-tuple-element.22, f32[512]{0:T(512)S(1)} %get-tuple-element.14, pred[64]{0:T(512)(128)(4,1)S(1)} %compare_bitcast_fusion), kind=kOutput, calls=%fused_computation.3 | convolution fusion | flops 2156920832 | bytes 9439296 | tf_op jit(solution)/shard_map/dot_general | solution.py:78
  147.6 10.6 %all-to-all-start.1 = ((bf16[256,32,256]{2,1,0:T(8,128)(2,1)}), bf16[256,32,256]{2,1,0:T(8,128)(2,1)}, u32[]{:S(2)}, u32[]{:S(2)}) async-start(bf16[256,32,256]{2,1,0:T(8,128)(2,1)} %bitcast.80), calls=%async_computation.2 | async-start | bytes 8388608 | tf_op jit(solution)/shard_map/all_to_all | solution.py:82
  158.3 0.2 reduce-scatter.2.cloned.1.call-start
  158.5 0.2 copy.25
  158.7 0.1 subtract_convert_fusion
  158.8 0.5 fusion.8
  159.2 7.3 %fusion.5 = f32[512,4,256]{2,0,1:T(8,128)} fusion(f32[512,4,256]{2,0,1:T(8,128)S(1)} %fusion.8, bf16[64,4,32,256]{3,2,1,0:T(8,128)(2,1)} %bitcast.3, f32[64,32,512,1]{2,1,3,0:T(8,128)} %copy-done.2, f32[512]{0:T(512)S(1)} %get-tuple-element.14, pred[64]{0:T(512)(128)(4,1)S(1)} %compare_bitcast_fusion), kind=kOutput, calls=%fused_computation.14 | convolution fusion | flops 2153775104 | bytes 12585024 | tf_op jit(solution)/shard_map/dot_general | solution.py:72
  166.6 13.2 %all_gather.15 = bf16[512,512]{1,0:T(8,128)(2,1)S(1)} all-gather(bf16[128,512]{1,0:T(8,128)(2,1)S(1)} %subtract_convert_fusion), channel_id=1, replica_groups=mesh['dp'=64,'mp'=4] {'mp'}, dimensions={0}, use_global_device_ids=true | all-gather | bytes 655360 | tf_op jit(solution)/shard_map/all_gather | solution.py:91
  179.8 0.3 convolution_multiply_fusion
  180.1 5.5 %scatter_custom_fusion = f32[4096,256]{1,0:T(8,128)} fusion(s32[512]{0:T(512)S(1)} %compare_select_fusion, f32[512,256]{1,0:T(8,128)S(1)} %convolution_multiply_fusion, f32[]{:T(128)} %constant.24.clone.1), kind=kCustom, calls=%fused_computation.15 | custom fusion | flops 131072 | bytes 4194308 | tf_op jit(solution)/shard_map/scatter-add | solution.py:93
  185.6 71.5 %all-to-all-done.1 = bf16[256,32,256]{2,1,0:T(8,128)(2,1)} async-done(((bf16[256,32,256]{2,1,0:T(8,128)(2,1)}), bf16[256,32,256]{2,1,0:T(8,128)(2,1)}, u32[]{:S(2)}, u32[]{:S(2)}) %all-to-all-start.1) | async-done | bytes 4194336 | tf_op jit(solution)/shard_map/all_to_all | solution.py:82
  257.1 5.2 %fusion.1 = f32[32,128,256]{2,0,1:T(8,128)S(1)} fusion(bf16[64,128,256]{2,1,0:T(8,128)(2,1)} %bitcast.24, s32[64]{0:T(128)S(1)} %get-tuple-element.9), kind=kOutput, calls=%fused_computation.7 | convolution fusion | flops 134219776 | bytes 8388864 | tf_op jit(solution)/shard_map/kr,rpd->kpd/dot_general | solution.py:99
  262.4 2.4 copy.31
  264.8 2.8 %bitcast_add_fusion = f32[4096,256]{1,0:T(8,128)} fusion(f32[4096,256]{1,0:T(8,128)S(1)} %copy-done.1, f32[32,128,256]{2,1,0:T(8,128)S(1)} %copy.31), kind=kLoop, calls=%fused_computation.4 | loop fusion | flops 1048576 | bytes 12582912 | tf_op jit(solution)/shard_map/add | solution.py:100
  (24 shorter events, 0.2 us)
Async XLA Ops:
  7.2 1.6 copy-start
  11.6 16.7 %copy-start.5 = (s32[512]{0:T(512)S(1)}, s32[512]{0:T(512)}, u32[]{:S(2)}) copy-start(s32[512]{0:T(512)} %param.6) | copy-start | bytes 6148
  11.6 18.7 %copy-start.4 = (bf16[512,256]{1,0:T(8,128)(2,1)S(1)}, bf16[512,256]{1,0:T(8,128)(2,1)}, u32[]{:S(2)}) copy-start(bf16[512,256]{1,0:T(8,128)(2,1)} %param.4) | copy-start | bytes 786436
  11.6 115.4 %all-to-all-start = ((bf16[256,32,256]{2,1,0:T(8,128)(2,1)}), bf16[256,32,256]{2,1,0:T(8,128)(2,1)}, u32[]{:S(2)}, u32[]{:S(2)}) async-start(bf16[256,32,256]{2,1,0:T(8,128)(2,1)} %bitcast.79), calls=%async_computation | async-start | bytes 8388608 | tf_op jit(solution)/shard_map/all_to_all | solution.py:23
  28.3 56.8 %all-gather.4.cloned.1.call-start = ((), (), s32[]{:S(2)}) async-start(), calls=%async_computation.3 | async-start | bytes 2621440 | tf_op jit(solution)/shard_map/all_gather | solution.py:35
  132.0 15.7 %copy-start.2 = (f32[64,32,512,1]{2,1,3,0:T(8,128)}, f32[64,32,512,1]{2,1,3,0:T(8,128)S(1)}, u32[]{:S(2)}) copy-start(f32[64,32,512,1]{2,1,3,0:T(8,128)S(1)} %get-tuple-element.22) | copy-start | bytes 12582916
  132.0 11.1 %copy-start.3 = (bf16[512,1024]{0,1:T(8,128)(2,1)S(1)}, bf16[512,1024]{0,1:T(8,128)(2,1)}, u32[]{:S(2)}) copy-start(bf16[512,1024]{0,1:T(8,128)(2,1)} %copy.22) | copy-start | bytes 3145732
  147.6 109.5 %all-to-all-start.1 = ((bf16[256,32,256]{2,1,0:T(8,128)(2,1)}), bf16[256,32,256]{2,1,0:T(8,128)(2,1)}, u32[]{:S(2)}, u32[]{:S(2)}) async-start(bf16[256,32,256]{2,1,0:T(8,128)(2,1)} %bitcast.80), calls=%async_computation.2 | async-start | bytes 8388608 | tf_op jit(solution)/shard_map/all_to_all | solution.py:82
  158.3 109.4 %reduce-scatter.2.cloned.1.call-start = ((), (), s32[]{:S(2)}) async-start(), calls=%async_computation.4 | async-start | bytes 2621440 | tf_op jit(solution)/shard_map/reduce_scatter | solution.py:75
  262.3 2.4 copy-start.1
Sparse Core Ops, SparseCore 0:
  31.5 53.5 all-gather.3
  166.7 47.9 reduce-scatter.1

commit v6 on v5

--- a/solution.py
+++ b/solution.py
@@ -93,11 +93,13 @@
     pos_part = jnp.zeros((block_count * PBS, shard_width), jnp.float32).at[positives].add(pos_back)
     returned, pos_part = lax.optimization_barrier((returned, pos_part))
 
-    selector = (asked[None, :] == jnp.arange(block_count, dtype=jnp.int32)[:, None]).astype(
-        jnp.bfloat16
+    returned = jnp.where((asked >= 0)[:, None, None], returned.astype(jnp.float32), jnp.float32(0.0))
+    passage_grad = (
+        pos_part.reshape(block_count, PBS, shard_width)
+        .at[jnp.maximum(asked, 0)]
+        .add(returned, mode="clip")
+        .reshape(block_count * PBS, shard_width)
     )
-    block_grad = jnp.einsum("kr,rpd->kpd", selector, returned, preferred_element_type=jnp.float32)
-    passage_grad = block_grad.reshape(block_count * PBS, shard_width) + pos_part
     return (losses, query_grad, passage_grad)
 
 

time: 275 us -> 290 us (1.055)
  other arithmetic: 13.2 us -> 35.2 us
  matrix products: 24.4 us -> 19.2 us
    scatter-add x0 -> x1, other arithmetic: none -> 18.7 us  [body(): passage_grad = pos_part.reshape(block_count, PBS, shard_width).at[jnp.max...]
    select_n x0 -> x1, other arithmetic: none -> 6.73 us  [body(): jnp.where((asked >= 0)[:, None, None], returned.astype(jnp.float32), jnp....]
    dot_general x1 -> x0, matrix products: 5.21 us -> none  [body(): jnp.einsum('kr,rpd->kpd', selector, returned, preferred_element_type=jnp....]
  transfers between devices with their start and end apart: 4 -> 4, of which waited for: 3 -> 3; matrix products, arithmetic and copies ran while one was open for 12% -> 16% of each run, Pallas kernels for 0% -> 0%
where the time goes in v6:
time: 290 us; the launch traced here: 289 us
  waiting for transfers between devices  162 us (56%)
  other arithmetic  35.2 us (12%)
  starting transfers between devices  27.6 us (10%)
  blocking collectives  21.9 us (8%)
  matrix products  19.2 us (7%)
  between operations  14.2 us (5%)
  local copies, waits for them, and re-layouts  9.07 us (3%)
    all_to_all x1, waiting for transfers between devices, body(): lax.all_to_all(sending.reshape(dp_count * mp_count, quarter, shard_width)...  71.6 us
    all_gather x1, waiting for transfers between devices, body(): lax.all_gather(jnp.concatenate([queries, positive_rows], axis=0), 'mp', a...  53.8 us
    all_to_all x1, waiting for transfers between devices, body(): lax.all_to_all(outgoing.reshape(dp_count * mp_count, quarter, shard_width...  36.6 us
    scatter-add x1, other arithmetic, body(): passage_grad = pos_part.reshape(block_count, PBS, shard_width).at[jnp.max...  18.7 us
    all_to_all x1, starting transfers between devices, body(): lax.all_to_all(outgoing.reshape(dp_count * mp_count, quarter, shard_width...  16.7 us
    all_gather x1, blocking collectives, body(): all_pos_grads = lax.all_gather(pos_grads, 'mp', axis=0, tiled=True)  12.9 us
    all_to_all x1, starting transfers between devices, body(): lax.all_to_all(sending.reshape(dp_count * mp_count, quarter, shard_width)...  10.6 us
    all_gather x1, blocking collectives, body(): lax.all_gather(jnp.stack([local_top, local_total, local_own]), 'mp', axis=0)  9.02 us
  transfers between devices with their start and end apart: 4, of which 3 were waited for; matrix products, arithmetic and copies ran while one was open for 16% of the time, Pallas kernels for 0%

profile of v6, /device:TPU:1, one launch (start us, length us, event | category | flops | bytes accessed | tf_op | source)
XLA Modules:
  0.0 289.4 jit_solution(7842154391108050056)
XLA Ops:
  7.2 1.1 clamp_reduce_fusion
  8.3 0.5 copy-done
  8.8 2.8 gather_fusion.1
  11.6 16.7 %all-to-all-start = ((bf16[256,32,256]{2,1,0:T(8,128)(2,1)}), bf16[256,32,256]{2,1,0:T(8,128)(2,1)}, u32[]{:S(2)}, u32[]{:S(2)}) async-start(bf16[256,32,256]{2,1,0:T(8,128)(2,1)} %bitcast.78), calls=%async_computation | async-start | bytes 8388608 | tf_op jit(solution)/shard_map/all_to_all | solution.py:23
  28.3 0.0 all-gather.4.cloned.1.call-start
  28.3 2.0 gather_fusion
  30.3 0.8 pad_maximum_fusion
  31.2 53.8 %all-gather.4.cloned.1.call-done = bf16[1024,1024]{1,0:T(8,128)(2,1)} async-done(((bf16[1024,256]{1,0:T(8,128)(2,1)}), bf16[1024,1024]{1,0:T(8,128)(2,1)}) %all-gather.4.cloned.1.call-update) | async-done | bytes 2097168 | tf_op jit(solution)/shard_map/all_gather | solution.py:35
  85.1 1.3 slice.21
  86.4 1.4 copy.20
  87.7 1.0 constant_dynamic-slice_fusion.1
  88.7 1.7 fusion.17
  90.4 36.6 %all-to-all-done = bf16[256,32,256]{2,1,0:T(8,128)(2,1)} async-done(((bf16[256,32,256]{2,1,0:T(8,128)(2,1)}), bf16[256,32,256]{2,1,0:T(8,128)(2,1)}, u32[]{:S(2)}, u32[]{:S(2)}) %all-to-all-start) | async-done | bytes 4194336 | tf_op jit(solution)/shard_map/all_to_all | solution.py:23
  127.0 4.9 %fusion.1 = (f32[512]{0:T(512)S(1)}, f32[64,32,512,1]{2,1,3,0:T(8,128)S(1)}) fusion(pred[64]{0:T(512)(128)(4,1)S(1)} %compare_bitcast_fusion, bf16[64,4,32,256]{3,2,1,0:T(8,128)(2,1)} %bitcast.3, bf16[512,4,256,1]{0,2,1,3:T(8,128)(2,1)} %bitcast.81), kind=kOutput, calls=%fused_computation.10 | convolution fusion | flops 2150628864 | bytes 9439296 | tf_op jit(solution)/shard_map/dot_general | solution.py:45
  132.0 1.3 select_reduce_fusion
  133.3 0.1 exponential_reduce_fusion
  133.4 9.0 %all-gather.1 = f32[4,3,512]{2,1,0:T(4,128)S(1)} all-gather(f32[1,3,512]{2,1,0:T(4,128)S(1)} %maximum_bitcast_fusion), channel_id=2, replica_groups=mesh['dp'=64,'mp'=4] {'mp'}, dimensions={0}, use_global_device_ids=true | all-gather | bytes 30720 | tf_op jit(solution)/shard_map/all_gather | solution.py:57
  142.5 0.6 fusion.15
  143.1 4.5 %multiply_convert_fusion = bf16[64,32,4,256]{3,1,2,0:T(8,128)(2,1)} fusion(bf16[512,4,256,1]{0,2,1,3:T(8,128)(2,1)S(1)} %bitcast.82, f32[64,32,512,1]{2,1,3,0:T(8,128)S(1)} %get-tuple-element.22, f32[512]{0:T(512)S(1)} %get-tuple-element.14, pred[64]{0:T(512)(128)(4,1)S(1)} %compare_bitcast_fusion), kind=kOutput, calls=%fused_computation.5 | convolution fusion | flops 2156920832 | bytes 9439296 | tf_op jit(solution)/shard_map/dot_general | solution.py:78
  147.6 10.6 %all-to-all-start.1 = ((bf16[256,32,256]{2,1,0:T(8,128)(2,1)}), bf16[256,32,256]{2,1,0:T(8,128)(2,1)}, u32[]{:S(2)}, u32[]{:S(2)}) async-start(bf16[256,32,256]{2,1,0:T(8,128)(2,1)} %bitcast.79), calls=%async_computation.2 | async-start | bytes 8388608 | tf_op jit(solution)/shard_map/all_to_all | solution.py:82
  158.3 0.2 reduce-scatter.2.cloned.1.call-start
  158.5 0.2 copy.23
  158.7 0.1 subtract_convert_fusion
  158.8 0.5 fusion.6
  159.2 7.3 %fusion.3 = f32[512,4,256]{2,0,1:T(8,128)} fusion(f32[512,4,256]{2,0,1:T(8,128)S(1)} %fusion.6, bf16[64,4,32,256]{3,2,1,0:T(8,128)(2,1)} %bitcast.3, f32[64,32,512,1]{2,1,3,0:T(8,128)} %copy-done.1, f32[512]{0:T(512)S(1)} %get-tuple-element.14, pred[64]{0:T(512)(128)(4,1)S(1)} %compare_bitcast_fusion), kind=kOutput, calls=%fused_computation.13 | convolution fusion | flops 2153775104 | bytes 12585024 | tf_op jit(solution)/shard_map/dot_general | solution.py:72
  166.6 0.2 compare_reduce_fusion
  166.8 12.9 %all_gather.15 = bf16[512,512]{1,0:T(8,128)(2,1)S(1)} all-gather(bf16[128,512]{1,0:T(8,128)(2,1)S(1)} %subtract_convert_fusion), channel_id=1, replica_groups=mesh['dp'=64,'mp'=4] {'mp'}, dimensions={0}, use_global_device_ids=true | all-gather | bytes 655360 | tf_op jit(solution)/shard_map/all_gather | solution.py:91
  179.7 0.3 convolution_multiply_fusion
  180.0 5.5 %scatter_custom_fusion = f32[4096,256]{1,0:T(8,128)} fusion(s32[512]{0:T(512)S(1)} %compare_select_fusion, f32[512,256]{1,0:T(8,128)S(1)} %convolution_multiply_fusion, f32[]{:T(128)} %constant.10.clone.1), kind=kCustom, calls=%fused_computation.14 | custom fusion | flops 131072 | bytes 4194308 | tf_op jit(solution)/shard_map/scatter-add | solution.py:93
  185.5 71.6 %all-to-all-done.1 = bf16[256,32,256]{2,1,0:T(8,128)(2,1)} async-done(((bf16[256,32,256]{2,1,0:T(8,128)(2,1)}), bf16[256,32,256]{2,1,0:T(8,128)(2,1)}, u32[]{:S(2)}, u32[]{:S(2)}) %all-to-all-start.1) | async-done | bytes 4194336 | tf_op jit(solution)/shard_map/all_to_all | solution.py:82
  257.1 6.7 %convert_select_fusion = f32[64,128,256]{2,1,0:T(8,128)} fusion(bf16[64,128,256]{2,1,0:T(8,128)(2,1)} %bitcast.23, pred[64]{0:T(512)(128)(4,1)S(1)} %compare_reduce_fusion), kind=kLoop, calls=%fused_computation.4 | loop fusion | flops 4194304 | bytes 12582976 | tf_op jit(solution)/shard_map/jit(_where)/select_n | solution.py:96
  263.9 18.7 %scatter_fusion = f32[32,128,256]{2,1,0:T(8,128)} fusion(f32[32,128,256]{2,1,0:T(8,128)} %bitcast.76, s32[64]{0:T(128)S(1)} %get-tuple-element.9, f32[64,128,256]{2,1,0:T(8,128)} %convert_select_fusion), kind=kCustom, calls=%fused_computation.3 | custom fusion | flops 2097152 | bytes 25166080 | tf_op jit(solution)/shard_map/scatter-add | solution.py:100
  (24 shorter events, 0.2 us)
Async XLA Ops:
  7.2 1.6 copy-start
  11.6 16.7 %copy-start.5 = (s32[512]{0:T(512)S(1)}, s32[512]{0:T(512)}, u32[]{:S(2)}) copy-start(s32[512]{0:T(512)} %param.6) | copy-start | bytes 6148
  11.6 18.7 %copy-start.3 = (bf16[512,256]{1,0:T(8,128)(2,1)S(1)}, bf16[512,256]{1,0:T(8,128)(2,1)}, u32[]{:S(2)}) copy-start(bf16[512,256]{1,0:T(8,128)(2,1)} %param.4) | copy-start | bytes 786436
  11.6 19.6 %copy-start.4 = (s32[64,64]{1,0:T(8,128)S(1)}, s32[64,64]{1,0:T(8,128)}, u32[]{:S(2)}) copy-start(s32[64,64]{1,0:T(8,128)} %param.7) | copy-start | bytes 49156
  11.6 115.4 %all-to-all-start = ((bf16[256,32,256]{2,1,0:T(8,128)(2,1)}), bf16[256,32,256]{2,1,0:T(8,128)(2,1)}, u32[]{:S(2)}, u32[]{:S(2)}) async-start(bf16[256,32,256]{2,1,0:T(8,128)(2,1)} %bitcast.78), calls=%async_computation | async-start | bytes 8388608 | tf_op jit(solution)/shard_map/all_to_all | solution.py:23
  28.3 56.8 %all-gather.4.cloned.1.call-start = ((), (), s32[]{:S(2)}) async-start(), calls=%async_computation.3 | async-start | bytes 2621440 | tf_op jit(solution)/shard_map/all_gather | solution.py:35
  132.0 15.7 %copy-start.1 = (f32[64,32,512,1]{2,1,3,0:T(8,128)}, f32[64,32,512,1]{2,1,3,0:T(8,128)S(1)}, u32[]{:S(2)}) copy-start(f32[64,32,512,1]{2,1,3,0:T(8,128)S(1)} %get-tuple-element.22) | copy-start | bytes 12582916
  132.0 11.1 %copy-start.2 = (bf16[512,1024]{0,1:T(8,128)(2,1)S(1)}, bf16[512,1024]{0,1:T(8,128)(2,1)}, u32[]{:S(2)}) copy-start(bf16[512,1024]{0,1:T(8,128)(2,1)} %copy.20) | copy-start | bytes 3145732
  147.6 109.5 %all-to-all-start.1 = ((bf16[256,32,256]{2,1,0:T(8,128)(2,1)}), bf16[256,32,256]{2,1,0:T(8,128)(2,1)}, u32[]{:S(2)}, u32[]{:S(2)}) async-start(bf16[256,32,256]{2,1,0:T(8,128)(2,1)} %bitcast.79), calls=%async_computation.2 | async-start | bytes 8388608 | tf_op jit(solution)/shard_map/all_to_all | solution.py:82
  158.3 124.3 %reduce-scatter.2.cloned.1.call-start = ((), (), s32[]{:S(2)}) async-start(), calls=%async_computation.4 | async-start | bytes 2621440 | tf_op jit(solution)/shard_map/reduce_scatter | solution.py:75
Sparse Core Ops, SparseCore 0:
  31.5 53.5 all-gather.3
  166.7 47.9 reduce-scatter.1

commit v7 on v5

--- a/solution.py
+++ b/solution.py
@@ -20,6 +20,11 @@
 
     asked = lax.dynamic_index_in_dim(negatives, own_index, 1, keepdims=False)
     outgoing = jnp.take(blocks, jnp.maximum(asked, 0), axis=0, mode="clip")
+    positive_rows = jnp.take(passages, positives, axis=0, mode="clip")
+    both = lax.all_gather(
+        jnp.concatenate([queries, positive_rows], axis=0), "mp", axis=1, tiled=True
+    )
+    outgoing, both = lax.optimization_barrier((outgoing, both))
     fetched = lax.all_to_all(
         outgoing.reshape(dp_count * mp_count, quarter, shard_width),
         ("dp", "mp"),
@@ -31,10 +36,6 @@
     wanted = lax.dynamic_index_in_dim(negatives, own_index, 0, keepdims=False)
     slot_ok = (wanted >= 0)[:, None, None]
 
-    positive_rows = jnp.take(passages, positives, axis=0, mode="clip")
-    both = lax.all_gather(
-        jnp.concatenate([queries, positive_rows], axis=0), "mp", axis=1, tiled=True
-    )
     q_full = both[:query_rows]
     q4 = q_full.reshape(query_rows, mp_count, shard_width)
     pos_mine = lax.dynamic_slice_in_dim(both, query_rows + width_index * pos_per, pos_per, 0)

time: 275 us -> 314 us (1.14)
  waiting for transfers between devices: 161 us -> 202 us
    all_to_all x1, waiting for transfers between devices: 36.6 us -> 94 us  [body(): lax.all_to_all(outgoing.reshape(dp_count * mp_count, quarter, shard_width...]
    all_gather x1, waiting for transfers between devices: 53.2 us -> 36.3 us  [body(): lax.all_gather(jnp.concatenate([queries, positive_rows], axis=0), 'mp', a...]
  transfers between devices with their start and end apart: 4 -> 4, of which waited for: 3 -> 3; matrix products, arithmetic and copies ran while one was open for 12% -> 10% of each run, Pallas kernels for 0% -> 0%
where the time goes in v7:
time: 314 us
  waiting for transfers between devices  202 us (64%)
  starting transfers between devices  25.7 us (8%)
  matrix products  24.4 us (8%)
  blocking collectives  22.1 us (7%)
  other arithmetic  14.8 us (5%)
  between operations  14.2 us (5%)
  local copies, waits for them, and re-layouts  10.4 us (3%)
    all_to_all x1, waiting for transfers between devices, body(): lax.all_to_all(outgoing.reshape(dp_count * mp_count, quarter, shard_width...  94 us
    all_to_all x1, waiting for transfers between devices, body(): lax.all_to_all(sending.reshape(dp_count * mp_count, quarter, shard_width)...  71.5 us
    all_gather x1, waiting for transfers between devices, body(): lax.all_gather(jnp.concatenate([queries, positive_rows], axis=0), 'mp', a...  36.3 us
    all_to_all x1, starting transfers between devices, body(): lax.all_to_all(outgoing.reshape(dp_count * mp_count, quarter, shard_width...  14.7 us
    all_gather x1, blocking collectives, body(): all_pos_grads = lax.all_gather(pos_grads, 'mp', axis=0, tiled=True)  13.1 us
    all_to_all x1, starting transfers between devices, body(): lax.all_to_all(sending.reshape(dp_count * mp_count, quarter, shard_width)...  10.7 us
    all_gather x1, blocking collectives, body(): lax.all_gather(jnp.stack([local_top, local_total, local_own]), 'mp', axis=0)  9.02 us
    dot_general x1, matrix products, body(): lax.dot_general(neg_grads, neg, (((0, 1), (0, 2)), ((), ())), preferred_e...  7.32 us
  transfers between devices with their start and end apart: 4, of which 3 were waited for; matrix products, arithmetic and copies ran while one was open for 10% of the time, Pallas kernels for 0%

profile of v7, /device:TPU:1, one launch (start us, length us, event | category | flops | bytes accessed | tf_op | source)
XLA Modules:
  0.0 313.6 jit_solution(4010440321498903130)
XLA Ops:
  7.2 0.8 pad_clamp_fusion
  8.1 0.7 copy-done
  8.8 1.9 gather_fusion.1
  10.7 1.8 pad_maximum_fusion
  12.5 0.9 dynamic-slice_reduce_fusion
  13.5 2.8 gather_fusion
  16.3 36.3 %all-gather.4.cloned.1.call-done = bf16[1024,1024]{1,0:T(8,128)(2,1)} async-done(((bf16[1024,256]{1,0:T(8,128)(2,1)}), bf16[1024,1024]{1,0:T(8,128)(2,1)}) %all-gather.4.cloned.1.call-update) | async-done | bytes 2097168 | tf_op jit(solution)/shard_map/all_gather | solution.py:24
  52.6 14.7 %all-to-all-start = ((bf16[256,32,256]{2,1,0:T(8,128)(2,1)}), bf16[256,32,256]{2,1,0:T(8,128)(2,1)}, u32[]{:S(2)}, u32[]{:S(2)}) async-start(bf16[256,32,256]{2,1,0:T(8,128)(2,1)} %bitcast.79), calls=%async_computation | async-start | bytes 8388608 | tf_op jit(solution)/shard_map/all_to_all | solution.py:28
  67.4 0.7 compare_bitcast_fusion
  68.1 1.3 copy.22
  69.5 1.0 constant_dynamic-slice_fusion.1
  70.4 1.7 fusion.22
  72.2 94.0 %all-to-all-done = bf16[256,32,256]{2,1,0:T(8,128)(2,1)} async-done(((bf16[256,32,256]{2,1,0:T(8,128)(2,1)}), bf16[256,32,256]{2,1,0:T(8,128)(2,1)}, u32[]{:S(2)}, u32[]{:S(2)}) %all-to-all-start) | async-done | bytes 4194336 | tf_op jit(solution)/shard_map/all_to_all | solution.py:28
  166.1 4.9 %fusion.3 = (f32[512]{0:T(512)S(1)}, f32[64,32,512,1]{2,1,3,0:T(8,128)S(1)}) fusion(pred[64]{0:T(512)(128)(4,1)S(1)} %compare_bitcast_fusion, bf16[64,4,32,256]{3,2,1,0:T(8,128)(2,1)} %bitcast.3, bf16[512,4,256,1]{0,2,1,3:T(8,128)(2,1)} %bitcast.82), kind=kOutput, calls=%fused_computation.11 | convolution fusion | flops 2150628864 | bytes 9439296 | tf_op jit(solution)/shard_map/dot_general | solution.py:46
  171.1 1.3 select_reduce_fusion
  172.4 0.1 exponential_reduce_fusion
  172.5 9.0 %all-gather.1 = f32[4,3,512]{2,1,0:T(4,128)S(1)} all-gather(f32[1,3,512]{2,1,0:T(4,128)S(1)} %maximum_bitcast_fusion), channel_id=2, replica_groups=mesh['dp'=64,'mp'=4] {'mp'}, dimensions={0}, use_global_device_ids=true | all-gather | bytes 30720 | tf_op jit(solution)/shard_map/all_gather | solution.py:58
  181.6 0.6 fusion.20
  182.2 4.5 %multiply_convert_fusion = bf16[64,32,4,256]{3,1,2,0:T(8,128)(2,1)} fusion(bf16[512,4,256,1]{0,2,1,3:T(8,128)(2,1)S(1)} %bitcast.83, f32[64,32,512,1]{2,1,3,0:T(8,128)S(1)} %get-tuple-element.26, f32[512]{0:T(512)S(1)} %get-tuple-element.18, pred[64]{0:T(512)(128)(4,1)S(1)} %compare_bitcast_fusion), kind=kOutput, calls=%fused_computation.3 | convolution fusion | flops 2156920832 | bytes 9439296 | tf_op jit(solution)/shard_map/dot_general | solution.py:79
  186.7 10.7 %all-to-all-start.1 = ((bf16[256,32,256]{2,1,0:T(8,128)(2,1)}), bf16[256,32,256]{2,1,0:T(8,128)(2,1)}, u32[]{:S(2)}, u32[]{:S(2)}) async-start(bf16[256,32,256]{2,1,0:T(8,128)(2,1)} %bitcast.80), calls=%async_computation.2 | async-start | bytes 8388608 | tf_op jit(solution)/shard_map/all_to_all | solution.py:83
  197.4 0.2 reduce-scatter.2.cloned.1.call-start
  197.6 0.2 copy.25
  197.8 0.1 subtract_convert_fusion
  197.9 0.5 fusion.8
  198.4 7.3 %fusion.5 = f32[512,4,256]{2,0,1:T(8,128)} fusion(f32[512,4,256]{2,0,1:T(8,128)S(1)} %fusion.8, bf16[64,4,32,256]{3,2,1,0:T(8,128)(2,1)} %bitcast.3, f32[64,32,512,1]{2,1,3,0:T(8,128)} %copy-done.2, f32[512]{0:T(512)S(1)} %get-tuple-element.18, pred[64]{0:T(512)(128)(4,1)S(1)} %compare_bitcast_fusion), kind=kOutput, calls=%fused_computation.14 | convolution fusion | flops 2153775104 | bytes 12585024 | tf_op jit(solution)/shard_map/dot_general | solution.py:73
  205.8 13.1 %all_gather.15 = bf16[512,512]{1,0:T(8,128)(2,1)S(1)} all-gather(bf16[128,512]{1,0:T(8,128)(2,1)S(1)} %subtract_convert_fusion), channel_id=1, replica_groups=mesh['dp'=64,'mp'=4] {'mp'}, dimensions={0}, use_global_device_ids=true | all-gather | bytes 655360 | tf_op jit(solution)/shard_map/all_gather | solution.py:92
  218.9 0.3 convolution_multiply_fusion
  219.2 5.5 %scatter_custom_fusion = f32[4096,256]{1,0:T(8,128)} fusion(s32[512]{0:T(512)S(1)} %compare_select_fusion, f32[512,256]{1,0:T(8,128)S(1)} %convolution_multiply_fusion, f32[]{:T(128)} %constant.24.clone.1), kind=kCustom, calls=%fused_computation.15 | custom fusion | flops 131072 | bytes 4194308 | tf_op jit(solution)/shard_map/scatter-add | solution.py:94
  224.7 71.5 %all-to-all-done.1 = bf16[256,32,256]{2,1,0:T(8,128)(2,1)} async-done(((bf16[256,32,256]{2,1,0:T(8,128)(2,1)}), bf16[256,32,256]{2,1,0:T(8,128)(2,1)}, u32[]{:S(2)}, u32[]{:S(2)}) %all-to-all-start.1) | async-done | bytes 4194336 | tf_op jit(solution)/shard_map/all_to_all | solution.py:83
  296.3 5.2 %fusion.1 = f32[32,128,256]{2,0,1:T(8,128)S(1)} fusion(bf16[64,128,256]{2,1,0:T(8,128)(2,1)} %bitcast.24, s32[64]{0:T(128)S(1)} %get-tuple-element.13), kind=kOutput, calls=%fused_computation.7 | convolution fusion | flops 134219776 | bytes 8388864 | tf_op jit(solution)/shard_map/kr,rpd->kpd/dot_general | solution.py:100
  301.5 2.4 copy.31
  303.9 2.8 bitcast_add_fusion
  (25 shorter events, 0.2 us)
Async XLA Ops:
  7.2 1.6 copy-start
  7.2 45.5 %all-gather.4.cloned.1.call-start = ((), (), s32[]{:S(2)}) async-start(), calls=%async_computation.3 | async-start | bytes 2621440 | tf_op jit(solution)/shard_map/all_gather | solution.py:24
  52.6 15.5 %slice-start = ((bf16[1024,1024]{1,0:T(8,128)(2,1)}), bf16[512,1024]{1,0:T(8,128)(2,1)S(1)}, s32[]{:S(2)}) async-start(bf16[1024,1024]{1,0:T(8,128)(2,1)} %all-gather.4.cloned.1.call-done), calls=%async_computation.5 | async-start | bytes 2097152 | tf_op jit(solution)/shard_map/slice | solution.py:39
  52.6 113.5 %all-to-all-start = ((bf16[256,32,256]{2,1,0:T(8,128)(2,1)}), bf16[256,32,256]{2,1,0:T(8,128)(2,1)}, u32[]{:S(2)}, u32[]{:S(2)}) async-start(bf16[256,32,256]{2,1,0:T(8,128)(2,1)} %bitcast.79), calls=%async_computation | async-start | bytes 8388608 | tf_op jit(solution)/shard_map/all_to_all | solution.py:28
  171.1 15.7 %copy-start.2 = (f32[64,32,512,1]{2,1,3,0:T(8,128)}, f32[64,32,512,1]{2,1,3,0:T(8,128)S(1)}, u32[]{:S(2)}) copy-start(f32[64,32,512,1]{2,1,3,0:T(8,128)S(1)} %get-tuple-element.26) | copy-start | bytes 12582916
  171.1 11.1 %copy-start.3 = (bf16[512,1024]{0,1:T(8,128)(2,1)S(1)}, bf16[512,1024]{0,1:T(8,128)(2,1)}, u32[]{:S(2)}) copy-start(bf16[512,1024]{0,1:T(8,128)(2,1)} %copy.22) | copy-start | bytes 3145732
  186.7 109.5 %all-to-all-start.1 = ((bf16[256,32,256]{2,1,0:T(8,128)(2,1)}), bf16[256,32,256]{2,1,0:T(8,128)(2,1)}, u32[]{:S(2)}, u32[]{:S(2)}) async-start(bf16[256,32,256]{2,1,0:T(8,128)(2,1)} %bitcast.80), calls=%async_computation.2 | async-start | bytes 8388608 | tf_op jit(solution)/shard_map/all_to_all | solution.py:83
  197.4 109.4 %reduce-scatter.2.cloned.1.call-start = ((), (), s32[]{:S(2)}) async-start(), calls=%async_computation.4 | async-start | bytes 2621440 | tf_op jit(solution)/shard_map/reduce_scatter | solution.py:76
  198.4 7.4 %copy-start.5 = (s32[512]{0:T(512)S(1)}, s32[512]{0:T(512)}, u32[]{:S(2)}) copy-start(s32[512]{0:T(512)} %param.6) | copy-start | bytes 6148
  198.4 20.5 %copy-start.4 = (bf16[512,256]{1,0:T(8,128)(2,1)S(1)}, bf16[512,256]{1,0:T(8,128)(2,1)}, u32[]{:S(2)}) copy-start(bf16[512,256]{1,0:T(8,128)(2,1)} %param.4) | copy-start | bytes 786436
  301.5 2.4 copy-start.1
Sparse Core Ops, SparseCore 0:
  12.7 39.9 all-gather.3
  205.9 47.9 reduce-scatter.1

commit v8 on v5

--- a/solution.py
+++ b/solution.py
@@ -54,7 +54,16 @@
         query_rows, dtype=jnp.int32
     )[None, :]
     local_own = jnp.sum(jnp.where(target, pos_scores, jnp.float32(0.0)), axis=0)
-    stats = lax.all_gather(jnp.stack([local_top, local_total, local_own]), "mp", axis=0)
+    local = jnp.stack([local_top, local_total, local_own])
+    got = jnp.stack(
+        [local]
+        + [
+            lax.ppermute(local, "mp", [(i, (i + k) % mp_count) for i in range(mp_count)])
+            for k in range(1, mp_count)
+        ]
+    )
+    source_order = (width_index - jnp.arange(mp_count, dtype=jnp.int32)) % mp_count
+    stats = jnp.take(got, source_order, axis=0, mode="clip")
     top = jnp.max(stats[:, 0], axis=0)
     total = jnp.sum(stats[:, 1] * jnp.exp(stats[:, 0] - top), axis=0)
     own_score = jnp.sum(stats[:, 2], axis=0)

time: 275 us -> 274 us (level)
  blocking collectives: 22.2 us -> 13.1 us
  matrix products: 24.4 us -> 27.2 us
    all_gather x1 -> x0, blocking collectives: 9.02 us -> none  [body(): lax.all_gather(jnp.stack([local_top, local_total, local_own]), 'mp', axis=0)]
    ppermute x0 -> x3, starting transfers between devices: none -> 2.85 us  [body(): lax.ppermute(local, 'mp', [(i, (i + k) % mp_count) for i in range(mp_coun...]
  transfers between devices with their start and end apart: 4 -> 7, of which waited for: 3 -> 4; matrix products, arithmetic and copies ran while one was open for 12% -> 12% of each run, Pallas kernels for 0% -> 0%
where the time goes in v8:
time: 274 us; the launch traced here: 273 us
  waiting for transfers between devices  162 us (59%)
  starting transfers between devices  29.4 us (11%)
  matrix products  27.2 us (10%)
  between operations  14.3 us (5%)
  local copies, waits for them, and re-layouts  14.1 us (5%)
  other arithmetic  13.2 us (5%)
  blocking collectives  13.1 us (5%)
    all_to_all x1, waiting for transfers between devices, body(): lax.all_to_all(sending.reshape(dp_count * mp_count, quarter, shard_width)...  71.6 us
    all_gather x1, waiting for transfers between devices, body(): lax.all_gather(jnp.concatenate([queries, positive_rows], axis=0), 'mp', a...  53.1 us
    all_to_all x1, waiting for transfers between devices, body(): lax.all_to_all(outgoing.reshape(dp_count * mp_count, quarter, shard_width...  35.9 us
    all_to_all x1, starting transfers between devices, body(): lax.all_to_all(outgoing.reshape(dp_count * mp_count, quarter, shard_width...  16.7 us
    all_gather x1, blocking collectives, body(): all_pos_grads = lax.all_gather(pos_grads, 'mp', axis=0, tiled=True)  13.1 us
    all_to_all x1, starting transfers between devices, body(): lax.all_to_all(sending.reshape(dp_count * mp_count, quarter, shard_width)...  9.85 us
    dot_general x1, matrix products, body(): lax.dot_general(neg_grads, neg, (((0, 1), (0, 2)), ((), ())), preferred_e...  7.32 us
    dot_general x1, matrix products, body(): lax.dot_general(neg_grads, q4, (((2,), (0,)), ((), ())), preferred_elemen...  6.64 us
  transfers between devices with their start and end apart: 7, of which 4 were waited for; matrix products, arithmetic and copies ran while one was open for 12% of the time, Pallas kernels for 0%

profile of v8, /device:TPU:1, one launch (start us, length us, event | category | flops | bytes accessed | tf_op | source)
XLA Modules:
  0.0 273.3 jit_solution(603737520003696978)
XLA Ops:
  7.2 1.1 dynamic-slice_reduce_fusion
  8.3 0.5 copy-done
  8.8 2.8 %gather_fusion.1 = bf16[64,128,256]{2,1,0:T(8,128)(2,1)} fusion(bf16[32,128,256]{2,1,0:T(8,128)(2,1)S(1)} %bitcast.83, s32[1024]{0:T(1024)S(1)} %pad_clamp_fusion.1), kind=kCustom, calls=%fused_computation.1 | custom fusion | bytes 8388864 | tf_op jit(solution)/shard_map/jit(_take)/gather | solution.py:22
  11.6 16.7 %all-to-all-start = ((bf16[256,32,256]{2,1,0:T(8,128)(2,1)}), bf16[256,32,256]{2,1,0:T(8,128)(2,1)}, u32[]{:S(2)}, u32[]{:S(2)}) async-start(bf16[256,32,256]{2,1,0:T(8,128)(2,1)} %bitcast.84), calls=%async_computation | async-start | bytes 8388608 | tf_op jit(solution)/shard_map/all_to_all | solution.py:23
  28.3 2.0 gather_fusion
  30.3 0.8 pad_maximum_fusion
  31.2 0.7 compare_bitcast_fusion
  31.9 53.1 %all-gather.2.cloned.1.call-done = bf16[1024,1024]{1,0:T(8,128)(2,1)} async-done(((bf16[1024,256]{1,0:T(8,128)(2,1)}), bf16[1024,1024]{1,0:T(8,128)(2,1)}) %all-gather.2.cloned.1.call-update) | async-done | bytes 2097168 | tf_op jit(solution)/shard_map/all_gather | solution.py:35
  85.1 1.3 slice.23
  86.4 1.4 copy.31
  87.7 1.0 constant_dynamic-slice_fusion.1
  88.7 2.4 fusion.25
  91.1 35.9 %all-to-all-done = bf16[256,32,256]{2,1,0:T(8,128)(2,1)} async-done(((bf16[256,32,256]{2,1,0:T(8,128)(2,1)}), bf16[256,32,256]{2,1,0:T(8,128)(2,1)}, u32[]{:S(2)}, u32[]{:S(2)}) %all-to-all-start) | async-done | bytes 4194336 | tf_op jit(solution)/shard_map/all_to_all | solution.py:23
  127.0 4.9 %fusion.3 = (f32[512]{0:T(512)S(1)}, f32[64,32,512,1]{2,1,3,0:T(8,128)S(1)}) fusion(pred[64]{0:T(512)(128)(4,1)S(1)} %compare_bitcast_fusion, bf16[64,4,32,256]{3,2,1,0:T(8,128)(2,1)} %bitcast.3, bf16[512,4,256,1]{0,2,1,3:T(8,128)(2,1)} %bitcast.87), kind=kOutput, calls=%fused_computation.12 | convolution fusion | flops 2150628864 | bytes 9439296 | tf_op jit(solution)/shard_map/dot_general | solution.py:45
  132.0 2.0 copy-done.2
  133.9 1.3 select_reduce_fusion
  135.5 0.4 collective-permute-start
  135.9 2.4 collective-permute-start.2
  138.2 1.2 collective-permute-done.1
  139.5 0.6 gather_fusion.2
  140.1 0.6 fusion.23
  140.7 6.6 %multiply_convert_fusion = bf16[64,32,4,256]{3,1,2,0:T(8,128)(2,1)} fusion(bf16[512,4,256,1]{0,2,1,3:T(8,128)(2,1)S(1)} %bitcast.88, f32[64,32,512,1]{2,1,3,0:T(8,128)} %copy-done.2, f32[512]{0:T(512)S(1)} %get-tuple-element.14, pred[64]{0:T(512)(128)(4,1)S(1)} %compare_bitcast_fusion), kind=kOutput, calls=%fused_computation.4 | convolution fusion | flops 2156920832 | bytes 9439296 | tf_op jit(solution)/shard_map/dot_general | solution.py:87
  147.4 9.8 %all-to-all-start.1 = ((bf16[256,32,256]{2,1,0:T(8,128)(2,1)}), bf16[256,32,256]{2,1,0:T(8,128)(2,1)}, u32[]{:S(2)}, u32[]{:S(2)}) async-start(bf16[256,32,256]{2,1,0:T(8,128)(2,1)} %bitcast.85), calls=%async_computation.2 | async-start | bytes 8388608 | tf_op jit(solution)/shard_map/all_to_all | solution.py:91
  157.6 0.5 fusion.8
  158.0 7.3 %fusion.5 = f32[512,4,256]{2,0,1:T(8,128)} fusion(f32[512,4,256]{2,0,1:T(8,128)S(1)} %fusion.8, bf16[64,4,32,256]{3,2,1,0:T(8,128)(2,1)} %bitcast.3, f32[64,32,512,1]{2,1,3,0:T(8,128)} %copy-done.2, f32[512]{0:T(512)S(1)} %get-tuple-element.14, pred[64]{0:T(512)(128)(4,1)S(1)} %compare_bitcast_fusion), kind=kOutput, calls=%fused_computation.15 | convolution fusion | flops 2153775104 | bytes 12585024 | tf_op jit(solution)/shard_map/dot_general | solution.py:81
  165.4 13.1 %all_gather.7 = bf16[512,512]{1,0:T(8,128)(2,1)S(1)} all-gather(bf16[128,512]{1,0:T(8,128)(2,1)S(1)} %subtract_convert_fusion), channel_id=1, replica_groups=mesh['dp'=64,'mp'=4] {'mp'}, dimensions={0}, use_global_device_ids=true | all-gather | bytes 655360 | tf_op jit(solution)/shard_map/all_gather | solution.py:100
  178.5 0.3 convolution_multiply_fusion
  178.8 5.5 %scatter_custom_fusion = f32[4096,256]{1,0:T(8,128)} fusion(s32[512]{0:T(512)S(1)} %compare_select_fusion, f32[512,256]{1,0:T(8,128)S(1)} %convolution_multiply_fusion, f32[]{:T(128)} %constant.54.clone.1), kind=kCustom, calls=%fused_computation.16 | custom fusion | flops 131072 | bytes 4194308 | tf_op jit(solution)/shard_map/scatter-add | solution.py:102
  184.4 71.6 %all-to-all-done.1 = bf16[256,32,256]{2,1,0:T(8,128)(2,1)} async-done(((bf16[256,32,256]{2,1,0:T(8,128)(2,1)}), bf16[256,32,256]{2,1,0:T(8,128)(2,1)}, u32[]{:S(2)}, u32[]{:S(2)}) %all-to-all-start.1) | async-done | bytes 4194336 | tf_op jit(solution)/shard_map/all_to_all | solution.py:91
  256.0 5.2 %fusion.1 = f32[32,128,256]{2,0,1:T(8,128)S(1)} fusion(bf16[64,128,256]{2,1,0:T(8,128)(2,1)} %bitcast.28, s32[64]{0:T(128)S(1)} %get-tuple-element.9), kind=kOutput, calls=%fused_computation.8 | convolution fusion | flops 134219776 | bytes 8388864 | tf_op jit(solution)/shard_map/kr,rpd->kpd/dot_general | solution.py:108
  261.2 2.4 copy.41
  263.6 2.8 %bitcast_add_fusion = f32[4096,256]{1,0:T(8,128)} fusion(f32[4096,256]{1,0:T(8,128)S(1)} %copy-done.1, f32[32,128,256]{2,1,0:T(8,128)S(1)} %copy.41), kind=kLoop, calls=%fused_computation.5 | loop fusion | flops 1048576 | bytes 12582912 | tf_op jit(solution)/shard_map/add | solution.py:109
  (39 shorter events, 0.8 us)
Async XLA Ops:
  7.2 1.6 copy-start
  11.6 16.7 %copy-start.8 = (s32[512]{0:T(512)S(1)}, s32[512]{0:T(512)}, u32[]{:S(2)}) copy-start(s32[512]{0:T(512)} %param.6) | copy-start | bytes 6148
  11.6 18.7 %copy-start.4 = (bf16[512,256]{1,0:T(8,128)(2,1)S(1)}, bf16[512,256]{1,0:T(8,128)(2,1)}, u32[]{:S(2)}) copy-start(bf16[512,256]{1,0:T(8,128)(2,1)} %param.4) | copy-start | bytes 786436
  11.6 115.4 %all-to-all-start = ((bf16[256,32,256]{2,1,0:T(8,128)(2,1)}), bf16[256,32,256]{2,1,0:T(8,128)(2,1)}, u32[]{:S(2)}, u32[]{:S(2)}) async-start(bf16[256,32,256]{2,1,0:T(8,128)(2,1)} %bitcast.84), calls=%async_computation | async-start | bytes 8388608 | tf_op jit(solution)/shard_map/all_to_all | solution.py:23
  28.3 56.8 %all-gather.2.cloned.1.call-start = ((), (), s32[]{:S(2)}) async-start(), calls=%async_computation.3 | async-start | bytes 2621440 | tf_op jit(solution)/shard_map/all_gather | solution.py:35
  131.9 2.0 copy-start.2
  131.9 3.3 %copy-start.6 = (f32[128,512]{1,0:T(8,128)S(1)}, f32[128,512]{1,0:T(8,128)}, u32[]{:S(2)}) copy-start(f32[128,512]{1,0:T(8,128)} %get-tuple-element.22) | copy-start | bytes 786436
  131.9 8.8 %copy-start.3 = (bf16[512,1024]{0,1:T(8,128)(2,1)S(1)}, bf16[512,1024]{0,1:T(8,128)(2,1)}, u32[]{:S(2)}) copy-start(bf16[512,1024]{0,1:T(8,128)(2,1)} %copy.31) | copy-start | bytes 3145732
  135.4 4.1 %collective-permute-start.1 = (f32[3,512]{1,0:T(4,128)S(1)}, f32[3,512]{1,0:T(4,128)S(1)}, u32[]{:S(2)}, u32[]{:S(2)}) collective-permute-start(f32[3,512]{1,0:T(4,128)S(1)} %get-tuple-element.20), channel_id=1, source_target_pairs={{0,2},{1,3},{2,0},{3,1},{4,6},{5,7},{6,4},{7,5},{8,10},{9,11},{10,... | collective-permute-start | bytes 18440 | tf_op jit(solution)/shard_map/ppermute | solution.py:61
  135.5 4.0 %collective-permute-start = (f32[3,512]{1,0:T(4,128)S(1)}, f32[3,512]{1,0:T(4,128)S(1)}, u32[]{:S(2)}, u32[]{:S(2)}) collective-permute-start(f32[3,512]{1,0:T(4,128)S(1)} %get-tuple-element.20), channel_id=1, source_target_pairs={{0,1},{1,2},{2,3},{3,0},{4,5},{5,6},{6,7},{7,4},{8,9},{9,10},{10,1... | collective-permute-start | bytes 18440 | tf_op jit(solution)/shard_map/ppermute | solution.py:61
  135.9 3.6 %collective-permute-start.2 = (f32[3,512]{1,0:T(4,128)S(1)}, f32[3,512]{1,0:T(4,128)S(1)}, u32[]{:S(2)}, u32[]{:S(2)}) collective-permute-start(f32[3,512]{1,0:T(4,128)S(1)} %get-tuple-element.20), channel_id=1, source_target_pairs={{0,3},{1,0},{2,1},{3,2},{4,7},{5,4},{6,5},{7,6},{8,11},{9,8},{10,9... | collective-permute-start | bytes 18440 | tf_op jit(solution)/shard_map/ppermute | solution.py:61
  147.4 10.1 %copy-start.7 = (f32[128,512]{1,0:T(8,128)S(1)}, f32[128,512]{1,0:T(8,128)}, u32[]{:S(2)}) copy-start(f32[128,512]{1,0:T(8,128)} %get-tuple-element.22) | copy-start | bytes 786436
  147.4 108.6 %all-to-all-start.1 = ((bf16[256,32,256]{2,1,0:T(8,128)(2,1)}), bf16[256,32,256]{2,1,0:T(8,128)(2,1)}, u32[]{:S(2)}, u32[]{:S(2)}) async-start(bf16[256,32,256]{2,1,0:T(8,128)(2,1)} %bitcast.85), calls=%async_computation.2 | async-start | bytes 8388608 | tf_op jit(solution)/shard_map/all_to_all | solution.py:91
  157.2 109.2 %reduce-scatter.2.cloned.1.call-start = ((), (), s32[]{:S(2)}) async-start(), calls=%async_computation.4 | async-start | bytes 2621440 | tf_op jit(solution)/shard_map/reduce_scatter | solution.py:84
  158.0 20.5 %copy-start.5 = (bf16[512,256]{1,0:T(8,128)(2,1)S(1)}, bf16[512,256]{1,0:T(8,128)(2,1)}, u32[]{:S(2)}) copy-start(bf16[512,256]{1,0:T(8,128)(2,1)} %param.4) | copy-start | bytes 786436
  261.2 2.4 copy-start.1
Sparse Core Ops, SparseCore 0:
  31.5 53.5 all-gather.1
  165.5 47.7 reduce-scatter.1

commit v9 on v5

--- a/solution.py
+++ b/solution.py
@@ -4,6 +4,14 @@
 from jax.sharding import PartitionSpec as P
 
 PBS = 128
+
+
+def from_sources(payload, me, n):
+    got = [payload(0)] + [
+        lax.ppermute(payload(k), "mp", [(i, (i + k) % n) for i in range(n)]) for k in range(1, n)
+    ]
+    order = (me - jnp.arange(n, dtype=jnp.int32)) % n
+    return jnp.take(jnp.stack(got), order, axis=0, mode="clip")
 
 
 def body(queries, passages, positives, negatives):
@@ -32,12 +40,22 @@
     slot_ok = (wanted >= 0)[:, None, None]
 
     positive_rows = jnp.take(passages, positives, axis=0, mode="clip")
-    both = lax.all_gather(
-        jnp.concatenate([queries, positive_rows], axis=0), "mp", axis=1, tiled=True
+    sources = from_sources(
+        lambda k: jnp.concatenate(
+            [
+                queries,
+                lax.dynamic_slice_in_dim(
+                    positive_rows, ((width_index + k) % mp_count) * pos_per, pos_per, 0
+                ),
+            ],
+            axis=0,
+        ),
+        width_index,
+        mp_count,
     )
-    q_full = both[:query_rows]
-    q4 = q_full.reshape(query_rows, mp_count, shard_width)
-    pos_mine = lax.dynamic_slice_in_dim(both, query_rows + width_index * pos_per, pos_per, 0)
+    q4 = sources[:, :query_rows].transpose(1, 0, 2)
+    q_full = q4.reshape(query_rows, mp_count * shard_width)
+    pos_mine = sources[:, query_rows:].transpose(1, 0, 2).reshape(pos_per, mp_count * shard_width)
 
     pos_scores = factor * lax.dot_general(
         pos_mine, q_full, (((1,), (1,)), ((), ())), preferred_element_type=jnp.float32
@@ -54,7 +72,8 @@
         query_rows, dtype=jnp.int32
     )[None, :]
     local_own = jnp.sum(jnp.where(target, pos_scores, jnp.float32(0.0)), axis=0)
-    stats = lax.all_gather(jnp.stack([local_top, local_total, local_own]), "mp", axis=0)
+    local = jnp.stack([local_top, local_total, local_own])
+    stats = from_sources(lambda k: local, width_index, mp_count)
     top = jnp.max(stats[:, 0], axis=0)
     total = jnp.sum(stats[:, 1] * jnp.exp(stats[:, 0] - top), axis=0)
     own_score = jnp.sum(stats[:, 2], axis=0)
@@ -72,8 +91,17 @@
     ) + lax.dot_general(
         neg_grads, neg, (((0, 1), (0, 2)), ((), ())), preferred_element_type=jnp.float32
     )
-    query_grad = lax.psum_scatter(factor * query_part, "mp", scatter_dimension=1, tiled=True)
-    query_grad = query_grad.reshape(query_rows, shard_width)
+    query_part = factor * query_part
+    query_grad = jnp.sum(
+        from_sources(
+            lambda k: lax.dynamic_index_in_dim(
+                query_part, (width_index + k) % mp_count, 1, keepdims=False
+            ),
+            width_index,
+            mp_count,
+        ),
+        axis=0,
+    )
 
     cand_grad = factor * lax.dot_general(
         neg_grads, q4, (((2,), (0,)), ((), ())), preferred_element_type=jnp.float32
@@ -88,7 +116,9 @@
     )
     returned = returned.reshape(dp_count, PBS, shard_width)
 
-    all_pos_grads = lax.all_gather(pos_grads, "mp", axis=0, tiled=True)
+    all_pos_grads = from_sources(lambda k: pos_grads, width_index, mp_count).reshape(
+        query_rows, query_rows
+    )
     pos_back = factor * jnp.dot(all_pos_grads, queries, preferred_element_type=jnp.float32)
     pos_part = jnp.zeros((block_count * PBS, shard_width), jnp.float32).at[positives].add(pos_back)
     returned, pos_part = lax.optimization_barrier((returned, pos_part))

time: 275 us -> 261 us (0.949)
  blocking collectives: 22.2 us -> 0 us
  starting transfers between devices: 27.6 us -> 41.4 us
  between operations: 14.2 us -> 0.99 us
  waiting for transfers between devices: 161 us -> 152 us
  other arithmetic: 13.2 us -> 20.9 us
  local copies, waits for them, and re-layouts: 11.5 us -> 17.6 us
  matrix products: 24.4 us -> 27.3 us
    ppermute x0 -> x12, waiting for transfers between devices: none -> 61.7 us  [from_sources(): lax.ppermute(payload(k), 'mp', [(i, (i + k) % n) for i in range(n)])]
    all_gather x1 -> x0, waiting for transfers between devices: 53.2 us -> none  [body(): lax.all_gather(jnp.concatenate([queries, positive_rows], axis=0), 'mp', a...]
    all_to_all x1, waiting for transfers between devices: 71.5 us -> 30.5 us  [body(): lax.all_to_all(sending.reshape(dp_count * mp_count, quarter, shard_width)...]
    all_to_all x1, waiting for transfers between devices: 36.6 us -> 59.8 us  [body(): lax.all_to_all(outgoing.reshape(dp_count * mp_count, quarter, shard_width...]
    all_gather x2 -> x0, blocking collectives: 22.2 us -> none  [the longest x1 13.2 us: body(): all_pos_grads = lax.all_gather(pos_grads, 'mp', axis=0, tiled=True)]
    ppermute x0 -> x12, starting transfers between devices: none -> 14.9 us  [from_sources(): lax.ppermute(payload(k), 'mp', [(i, (i + k) % n) for i in range(n)])]
    gather x0 -> x4, local copies, waits for them, and re-layouts: none -> 6.5 us  [from_sources(): return jnp.take(jnp.stack(got), order, axis=0, mode='clip')]
    another operation x0 -> x7, other arithmetic: none -> 5.47 us  [from_sources(): return jnp.take(jnp.stack(got), order, axis=0, mode='clip')]
  transfers between devices with their start and end apart: 4 -> 14, of which waited for: 3 -> 9; matrix products, arithmetic and copies ran while one was open for 12% -> 13% of each run, Pallas kernels for 0% -> 0%
where the time goes in v9:
time: 261 us; the launch traced here: 260 us
  waiting for transfers between devices  152 us (58%)
  starting transfers between devices  41.4 us (16%)
  matrix products  27.3 us (10%)
  other arithmetic  20.9 us (8%)
  local copies, waits for them, and re-layouts  17.6 us (7%)
    ppermute x12, waiting for transfers between devices, from_sources(): lax.ppermute(payload(k), 'mp', [(i, (i + k) % n) for i in range(n)])  61.7 us
    all_to_all x1, waiting for transfers between devices, body(): lax.all_to_all(outgoing.reshape(dp_count * mp_count, quarter, shard_width...  59.8 us
    all_to_all x1, waiting for transfers between devices, body(): lax.all_to_all(sending.reshape(dp_count * mp_count, quarter, shard_width)...  30.5 us
    all_to_all x1, starting transfers between devices, body(): lax.all_to_all(outgoing.reshape(dp_count * mp_count, quarter, shard_width...  16.7 us
    ppermute x12, starting transfers between devices, from_sources(): lax.ppermute(payload(k), 'mp', [(i, (i + k) % n) for i in range(n)])  14.9 us
    all_to_all x1, starting transfers between devices, body(): lax.all_to_all(sending.reshape(dp_count * mp_count, quarter, shard_width)...  9.85 us
    dot_general x1, matrix products, body(): lax.dot_general(neg_grads, q4, (((2,), (0,)), ((), ())), preferred_elemen...  6.93 us
    gather x4, local copies, waits for them, and re-layouts, from_sources(): return jnp.take(jnp.stack(got), order, axis=0, mode='clip')  6.5 us
  transfers between devices with their start and end apart: 14, of which 9 were waited for; matrix products, arithmetic and copies ran while one was open for 13% of the time, Pallas kernels for 0%

profile of v9, /device:TPU:1, one launch (start us, length us, event | category | flops | bytes accessed | tf_op | source)
XLA Modules:
  0.0 260.3 jit_solution(1167450683745057328)
XLA Ops:
  2.2 2.8 %gather_fusion.2 = bf16[64,128,256]{2,1,0:T(8,128)(2,1)} fusion(bf16[32,128,256]{2,1,0:T(8,128)(2,1)S(1)} %bitcast.118, s32[1024]{0:T(1024)S(1)} %pad_clamp_fusion), kind=kCustom, calls=%fused_computation.2 | custom fusion | bytes 8388864 | tf_op jit(solution)/shard_map/jit(_take)/gather | solution.py:30
  5.1 16.7 %all-to-all-start = ((bf16[256,32,256]{2,1,0:T(8,128)(2,1)}), bf16[256,32,256]{2,1,0:T(8,128)(2,1)}, u32[]{:S(2)}, u32[]{:S(2)}) async-start(bf16[256,32,256]{2,1,0:T(8,128)(2,1)} %bitcast.119), calls=%async_computation | async-start | bytes 8388608 | tf_op jit(solution)/shard_map/all_to_all | solution.py:31
  21.8 2.0 gather_fusion
  24.8 1.4 collective-permute-start
  26.2 2.4 collective-permute-start.1
  30.5 11.6 %collective-permute-done = bf16[640,256]{1,0:T(8,128)(2,1)S(1)} collective-permute-done((bf16[640,256]{1,0:T(8,128)(2,1)}, bf16[640,256]{1,0:T(8,128)(2,1)S(1)}, u32[]{:S(2)}, u32[]{:S(2)}) %collective-permute-start) | collective-permute-done | bytes 327712 | tf_op jit(solution)/shard_map/ppermute | solution.py:11
  42.1 13.6 %collective-permute-done.1 = bf16[640,256]{1,0:T(8,128)(2,1)} collective-permute-done((bf16[640,256]{1,0:T(8,128)(2,1)S(1)}, bf16[640,256]{1,0:T(8,128)(2,1)}, u32[]{:S(2)}, u32[]{:S(2)}) %collective-permute-start.1) | collective-permute-done | bytes 327712 | tf_op jit(solution)/shard_map/ppermute | solution.py:11
  55.7 1.4 pad_maximum_fusion.1
  57.1 1.8 gather_fusion.1
  58.9 1.8 fusion.32
  60.7 59.8 %all-to-all-done = bf16[256,32,256]{2,1,0:T(8,128)(2,1)} async-done(((bf16[256,32,256]{2,1,0:T(8,128)(2,1)}), bf16[256,32,256]{2,1,0:T(8,128)(2,1)}, u32[]{:S(2)}, u32[]{:S(2)}) %all-to-all-start) | async-done | bytes 4194336 | tf_op jit(solution)/shard_map/all_to_all | solution.py:31
  120.5 5.0 %fusion.3 = (f32[512]{0:T(512)S(1)}, f32[64,32,512,1]{2,1,3,0:T(8,128)S(1)}) fusion(pred[64]{0:T(512)(128)(4,1)S(1)} %compare_bitcast_fusion, bf16[64,4,32,256]{3,2,1,0:T(8,128)(2,1)} %bitcast.11, bf16[4,640,256]{2,1,0:T(8,128)(2,1)} %gather_fusion.1), kind=kOutput, calls=%fused_computation.15 | convolution fusion | flops 2150628864 | bytes 9439296 | tf_op jit(solution)/shard_map/dot_general | solution.py:63
  125.5 2.0 copy-done.2
  129.4 2.4 collective-permute-start.5
  134.3 6.9 %multiply_convert_fusion = bf16[64,32,4,256]{3,1,2,0:T(8,128)(2,1)} fusion(bf16[4,640,256]{2,1,0:T(8,128)(2,1)} %gather_fusion.1, f32[64,32,512,1]{2,1,3,0:T(8,128)} %copy-done.2, f32[512]{0:T(512)S(1)} %get-tuple-element.14, pred[64]{0:T(512)(128)(4,1)S(1)} %compare_bitcast_fusion), kind=kOutput, calls=%fused_computation.7 | convolution fusion | flops 2156920832 | bytes 9439296 | tf_op jit(solution)/shard_map/dot_general | solution.py:106
  141.2 9.8 %all-to-all-start.1 = ((bf16[256,32,256]{2,1,0:T(8,128)(2,1)}), bf16[256,32,256]{2,1,0:T(8,128)(2,1)}, u32[]{:S(2)}, u32[]{:S(2)}) async-start(bf16[256,32,256]{2,1,0:T(8,128)(2,1)} %bitcast.120), calls=%async_computation.1 | async-start | bytes 8388608 | tf_op jit(solution)/shard_map/all_to_all | solution.py:110
  151.2 3.0 %collective-permute-start.10 = (bf16[128,512]{1,0:T(8,128)(2,1)S(1)}, bf16[128,512]{1,0:T(8,128)(2,1)S(1)}, u32[]{:S(2)}, u32[]{:S(2)}) collective-permute-start(bf16[128,512]{1,0:T(8,128)(2,1)S(1)} %subtract_convert_fusion), channel_id=1, source_target_pairs={{0,2},{1,3},{2,0},{3,1},{4,6},{5,7},{6,4},{7,5},{8,10},{9,11},{10,... | collective-permute-start | bytes 393224 | tf_op jit(solution)/shard_map/ppermute | solution.py:11
  154.5 2.4 collective-permute-start.11
  156.9 1.4 fusion.16
  158.3 5.9 %fusion.5 = f32[512,4,256]{2,0,1:T(8,128)S(1)} fusion(f32[512,4,256]{2,0,1:T(8,128)S(1)} %fusion.16, bf16[64,4,32,256]{3,2,1,0:T(8,128)(2,1)} %bitcast.11, f32[64,32,512,1]{2,1,3,0:T(8,128)} %copy-done.2, f32[512]{0:T(512)S(1)} %get-tuple-element.14, pred[64]{0:T(512)(128)(4,1)S(1)} %compare_bitcast_fusion), kind=kOutput, calls=%fused_computation.18 | convolution fusion | flops 2153775104 | bytes 12585024 | tf_op jit(solution)/shard_map/dot_general | solution.py:91
  164.2 1.4 dynamic-slice_bitcast_fusion.3
  167.2 2.3 collective-permute-done.9
  171.3 6.0 %scatter_custom_fusion = f32[4096,256]{1,0:T(8,128)} fusion(s32[512]{0:T(512)S(1)} %compare_select_fusion, f32[512,256]{1,0:T(8,128)} %convolution_multiply_fusion, f32[]{:T(128)} %constant.103.clone.1), kind=kCustom, calls=%fused_computation.20 | custom fusion | flops 131072 | bytes 4194816 | tf_op jit(solution)/shard_map/scatter-add | solution.py:123
  177.3 11.3 %collective-permute-done.8 = f32[512,256]{1,0:T(8,128)} collective-permute-done((f32[512,256]{1,0:T(8,128)}, f32[512,256]{1,0:T(8,128)}, u32[]{:S(2)}, u32[]{:S(2)}) %collective-permute-start.8) | collective-permute-done | bytes 524320 | tf_op jit(solution)/shard_map/ppermute | solution.py:11
  189.3 20.9 %collective-permute-done.6 = f32[512,256]{1,0:T(8,128)} collective-permute-done((f32[512,256]{1,0:T(8,128)}, f32[512,256]{1,0:T(8,128)}, u32[]{:S(2)}, u32[]{:S(2)}) %collective-permute-start.6) | collective-permute-done | bytes 524320 | tf_op jit(solution)/shard_map/ppermute | solution.py:11
  210.2 2.9 %pad_maximum_fusion = f32[4,512,256]{2,1,0:T(8,128)} fusion(f32[1,512,256]{2,1,0:T(8,128)} %bitcast.33, f32[1,512,256]{2,1,0:T(8,128)} %bitcast.31, f32[1,512,256]{2,1,0:T(8,128)} %bitcast.29, f32[1,512,256]{2,1,0:T(8,128)S(1)} %copy-done.3), kind=kLoop, calls=%fused_computation.19 | loop fusion | flops 1572864 | bytes 4194304 | tf_op jit(solution)/shard_map/stack | solution.py:14
  213.2 3.6 %gather_fusion.4 = f32[4,512,256]{2,1,0:T(8,128)} fusion(f32[4,512,256]{2,1,0:T(8,128)} %pad_maximum_fusion, s32[1024]{0:T(1024)S(1)} %pad_clamp_fusion.1), kind=kCustom, calls=%fused_computation.4 | custom fusion | bytes 4194320 | tf_op jit(solution)/shard_map/jit(_take)/gather | solution.py:14
  216.7 2.6 reduce_sum.59
  219.3 30.5 %all-to-all-done.1 = bf16[256,32,256]{2,1,0:T(8,128)(2,1)} async-done(((bf16[256,32,256]{2,1,0:T(8,128)(2,1)}), bf16[256,32,256]{2,1,0:T(8,128)(2,1)}, u32[]{:S(2)}, u32[]{:S(2)}) %all-to-all-start.1) | async-done | bytes 4194336 | tf_op jit(solution)/shard_map/all_to_all | solution.py:110
  249.8 5.2 %fusion.1 = f32[32,128,256]{2,0,1:T(8,128)S(1)} fusion(bf16[64,128,256]{2,1,0:T(8,128)(2,1)} %bitcast.39, s32[64]{0:T(128)S(1)} %get-tuple-element.9), kind=kOutput, calls=%fused_computation.11 | convolution fusion | flops 134219776 | bytes 8388864 | tf_op jit(solution)/shard_map/kr,rpd->kpd/dot_general | solution.py:129
  255.0 2.4 copy.26
  257.4 2.8 %bitcast_add_fusion = f32[4096,256]{1,0:T(8,128)} fusion(f32[4096,256]{1,0:T(8,128)S(1)} %copy-done.1, f32[32,128,256]{2,1,0:T(8,128)S(1)} %copy.26), kind=kLoop, calls=%fused_computation.8 | loop fusion | flops 1048576 | bytes 12582912 | tf_op jit(solution)/shard_map/add | solution.py:130
  (54 shorter events, 13.3 us)
Async XLA Ops:
  0.6 1.6 copy-start
  5.1 16.7 %copy-start.7 = (s32[512]{0:T(512)S(1)}, s32[512]{0:T(512)}, u32[]{:S(2)}) copy-start(s32[512]{0:T(512)} %param.6) | copy-start | bytes 6148
  5.1 18.8 %copy-start.4 = (bf16[512,256]{1,0:T(8,128)(2,1)S(1)}, bf16[512,256]{1,0:T(8,128)(2,1)}, u32[]{:S(2)}) copy-start(bf16[512,256]{1,0:T(8,128)(2,1)} %param.4) | copy-start | bytes 786436
  5.1 115.4 %all-to-all-start = ((bf16[256,32,256]{2,1,0:T(8,128)(2,1)}), bf16[256,32,256]{2,1,0:T(8,128)(2,1)}, u32[]{:S(2)}, u32[]{:S(2)}) async-start(bf16[256,32,256]{2,1,0:T(8,128)(2,1)} %bitcast.119), calls=%async_computation | async-start | bytes 8388608 | tf_op jit(solution)/shard_map/all_to_all | solution.py:31
  24.8 17.3 %collective-permute-start = (bf16[640,256]{1,0:T(8,128)(2,1)}, bf16[640,256]{1,0:T(8,128)(2,1)S(1)}, u32[]{:S(2)}, u32[]{:S(2)}) collective-permute-start(bf16[640,256]{1,0:T(8,128)(2,1)} %get-tuple-element.20), channel_id=1, source_target_pairs={{0,1},{1,2},{2,3},{3,0},{4,5},{5,6},{6,7},{7,4},{8,9},{9,10},{10,1... | collective-permute-start | bytes 983048 | tf_op jit(solution)/shard_map/ppermute | solution.py:11
  26.2 29.5 %collective-permute-start.1 = (bf16[640,256]{1,0:T(8,128)(2,1)S(1)}, bf16[640,256]{1,0:T(8,128)(2,1)}, u32[]{:S(2)}, u32[]{:S(2)}) collective-permute-start(bf16[640,256]{1,0:T(8,128)(2,1)S(1)} %get-tuple-element.21), channel_id=1, source_target_pairs={{0,2},{1,3},{2,0},{3,1},{4,6},{5,7},{6,4},{7,5},{8,10},{9,11},{10,... | collective-permute-start | bytes 983048 | tf_op jit(solution)/shard_map/ppermute | solution.py:11
  28.6 27.1 %collective-permute-start.2 = (bf16[640,256]{1,0:T(8,128)(2,1)S(1)}, bf16[640,256]{1,0:T(8,128)(2,1)}, u32[]{:S(2)}, u32[]{:S(2)}) collective-permute-start(bf16[640,256]{1,0:T(8,128)(2,1)S(1)} %get-tuple-element.22), channel_id=1, source_target_pairs={{0,3},{1,0},{2,1},{3,2},{4,7},{5,4},{6,5},{7,6},{8,11},{9,8},{10,9... | collective-permute-start | bytes 983048 | tf_op jit(solution)/shard_map/ppermute | solution.py:11
  42.1 13.6 %copy-start.6 = (bf16[640,256]{1,0:T(8,128)(2,1)}, bf16[640,256]{1,0:T(8,128)(2,1)S(1)}, u32[]{:S(2)}) copy-start(bf16[640,256]{1,0:T(8,128)(2,1)S(1)} %collective-permute-done) | copy-start | bytes 983044
  125.5 2.0 copy-start.2
  128.9 4.1 %collective-permute-start.4 = (f32[3,512]{1,0:T(4,128)S(1)}, f32[3,512]{1,0:T(4,128)S(1)}, u32[]{:S(2)}, u32[]{:S(2)}) collective-permute-start(f32[3,512]{1,0:T(4,128)S(1)} %get-tuple-element.32), channel_id=1, source_target_pairs={{0,2},{1,3},{2,0},{3,1},{4,6},{5,7},{6,4},{7,5},{8,10},{9,11},{10,... | collective-permute-start | bytes 18440 | tf_op jit(solution)/shard_map/ppermute | solution.py:11
  129.0 4.0 %collective-permute-start.3 = (f32[3,512]{1,0:T(4,128)S(1)}, f32[3,512]{1,0:T(4,128)S(1)}, u32[]{:S(2)}, u32[]{:S(2)}) collective-permute-start(f32[3,512]{1,0:T(4,128)S(1)} %get-tuple-element.32), channel_id=1, source_target_pairs={{0,1},{1,2},{2,3},{3,0},{4,5},{5,6},{6,7},{7,4},{8,9},{9,10},{10,1... | collective-permute-start | bytes 18440 | tf_op jit(solution)/shard_map/ppermute | solution.py:11
  129.4 3.6 %collective-permute-start.5 = (f32[3,512]{1,0:T(4,128)S(1)}, f32[3,512]{1,0:T(4,128)S(1)}, u32[]{:S(2)}, u32[]{:S(2)}) collective-permute-start(f32[3,512]{1,0:T(4,128)S(1)} %get-tuple-element.32), channel_id=1, source_target_pairs={{0,3},{1,0},{2,1},{3,2},{4,7},{5,4},{6,5},{7,6},{8,11},{9,8},{10,9... | collective-permute-start | bytes 18440 | tf_op jit(solution)/shard_map/ppermute | solution.py:11
  141.2 108.6 %all-to-all-start.1 = ((bf16[256,32,256]{2,1,0:T(8,128)(2,1)}), bf16[256,32,256]{2,1,0:T(8,128)(2,1)}, u32[]{:S(2)}, u32[]{:S(2)}) async-start(bf16[256,32,256]{2,1,0:T(8,128)(2,1)} %bitcast.120), calls=%async_computation.1 | async-start | bytes 8388608 | tf_op jit(solution)/shard_map/all_to_all | solution.py:110
  151.2 15.2 %collective-permute-start.10 = (bf16[128,512]{1,0:T(8,128)(2,1)S(1)}, bf16[128,512]{1,0:T(8,128)(2,1)S(1)}, u32[]{:S(2)}, u32[]{:S(2)}) collective-permute-start(bf16[128,512]{1,0:T(8,128)(2,1)S(1)} %subtract_convert_fusion), channel_id=1, source_target_pairs={{0,2},{1,3},{2,0},{3,1},{4,6},{5,7},{6,4},{7,5},{8,10},{9,11},{10,... | collective-permute-start | bytes 393224 | tf_op jit(solution)/shard_map/ppermute | solution.py:11
  154.2 15.3 %collective-permute-start.9 = (bf16[128,512]{1,0:T(8,128)(2,1)S(1)}, bf16[128,512]{1,0:T(8,128)(2,1)S(1)}, u32[]{:S(2)}, u32[]{:S(2)}) collective-permute-start(bf16[128,512]{1,0:T(8,128)(2,1)S(1)} %subtract_convert_fusion), channel_id=1, source_target_pairs={{0,1},{1,2},{2,3},{3,0},{4,5},{5,6},{6,7},{7,4},{8,9},{9,10},{10,1... | collective-permute-start | bytes 393224 | tf_op jit(solution)/shard_map/ppermute | solution.py:11
  154.5 15.0 %collective-permute-start.11 = (bf16[128,512]{1,0:T(8,128)(2,1)S(1)}, bf16[128,512]{1,0:T(8,128)(2,1)S(1)}, u32[]{:S(2)}, u32[]{:S(2)}) collective-permute-start(bf16[128,512]{1,0:T(8,128)(2,1)S(1)} %subtract_convert_fusion), channel_id=1, source_target_pairs={{0,3},{1,0},{2,1},{3,2},{4,7},{5,4},{6,5},{7,6},{8,11},{9,8},{10,9... | collective-permute-start | bytes 393224 | tf_op jit(solution)/shard_map/ppermute | solution.py:11
  164.2 6.0 %copy-start.5 = (bf16[512,256]{1,0:T(8,128)(2,1)S(1)}, bf16[512,256]{1,0:T(8,128)(2,1)}, u32[]{:S(2)}) copy-start(bf16[512,256]{1,0:T(8,128)(2,1)} %param.4) | copy-start | bytes 786436
  165.6 23.0 %collective-permute-start.8 = (f32[512,256]{1,0:T(8,128)}, f32[512,256]{1,0:T(8,128)}, u32[]{:S(2)}, u32[]{:S(2)}) collective-permute-start(f32[512,256]{1,0:T(8,128)} %get-tuple-element.16), channel_id=1, source_target_pairs={{0,3},{1,0},{2,1},{3,2},{4,7},{5,4},{6,5},{7,6},{8,11},{9,8},{10,9... | collective-permute-start | bytes 1572872 | tf_op jit(solution)/shard_map/ppermute | solution.py:11
  165.6 23.7 %collective-permute-start.7 = (f32[512,256]{1,0:T(8,128)}, f32[512,256]{1,0:T(8,128)}, u32[]{:S(2)}, u32[]{:S(2)}) collective-permute-start(f32[512,256]{1,0:T(8,128)} %get-tuple-element.17), channel_id=1, source_target_pairs={{0,2},{1,3},{2,0},{3,1},{4,6},{5,7},{6,4},{7,5},{8,10},{9,11},{10,... | collective-permute-start | bytes 1572872 | tf_op jit(solution)/shard_map/ppermute | solution.py:11
  166.4 43.8 %collective-permute-start.6 = (f32[512,256]{1,0:T(8,128)}, f32[512,256]{1,0:T(8,128)}, u32[]{:S(2)}, u32[]{:S(2)}) collective-permute-start(f32[512,256]{1,0:T(8,128)} %get-tuple-element.18), channel_id=1, source_target_pairs={{0,1},{1,2},{2,3},{3,0},{4,5},{5,6},{6,7},{7,4},{8,9},{9,10},{10,1... | collective-permute-start | bytes 1572872 | tf_op jit(solution)/shard_map/ppermute | solution.py:11
  170.1 40.1 %copy-start.3 = (f32[1,512,256]{2,1,0:T(8,128)S(1)}, f32[1,512,256]{2,1,0:T(8,128)}, u32[]{:S(2)}) copy-start(f32[1,512,256]{2,1,0:T(8,128)} %get-tuple-element.15) | copy-start | bytes 1572868
  255.0 2.4 copy-start.1

commit v10 on v9

--- a/solution.py
+++ b/solution.py
@@ -127,7 +127,9 @@
         jnp.bfloat16
     )
     block_grad = jnp.einsum("kr,rpd->kpd", selector, returned, preferred_element_type=jnp.float32)
-    passage_grad = block_grad.reshape(block_count * PBS, shard_width) + pos_part
+    passage_grad = (block_grad + pos_part.reshape(block_count, PBS, shard_width)).reshape(
+        block_count * PBS, shard_width
+    )
     return (losses, query_grad, passage_grad)
 
 

time: 261 us -> 263 us (level)
  matrix products: 27.3 us -> 30.8 us
  other arithmetic: 20.9 us -> 18.1 us
    add x0 -> x1, local copies, waits for them, and re-layouts: none -> 4.44 us  [body(): block_grad + pos_part.reshape(block_count, PBS, shard_width)]
    dot_general x1, matrix products: 5.21 us -> 8.7 us  [body(): jnp.einsum('kr,rpd->kpd', selector, returned, preferred_element_type=jnp....]
    add x1 -> x0, other arithmetic: 2.82 us -> none  [body(): passage_grad = block_grad.reshape(block_count * PBS, shard_width) + pos_part]
where the time goes in v10:
time: 263 us
  waiting for transfers between devices  152 us (58%)
  starting transfers between devices  41.4 us (16%)
  matrix products  30.8 us (12%)
  local copies, waits for them, and re-layouts  19.6 us (7%)
  other arithmetic  18.1 us (7%)
    ppermute x12, waiting for transfers between devices, from_sources(): lax.ppermute(payload(k), 'mp', [(i, (i + k) % n) for i in range(n)])  61.7 us
    all_to_all x1, waiting for transfers between devices, body(): lax.all_to_all(outgoing.reshape(dp_count * mp_count, quarter, shard_width...  59.8 us
    all_to_all x1, waiting for transfers between devices, body(): lax.all_to_all(sending.reshape(dp_count * mp_count, quarter, shard_width)...  30.5 us
    all_to_all x1, starting transfers between devices, body(): lax.all_to_all(outgoing.reshape(dp_count * mp_count, quarter, shard_width...  16.7 us
    ppermute x12, starting transfers between devices, from_sources(): lax.ppermute(payload(k), 'mp', [(i, (i + k) % n) for i in range(n)])  14.9 us
    all_to_all x1, starting transfers between devices, body(): lax.all_to_all(sending.reshape(dp_count * mp_count, quarter, shard_width)...  9.85 us
    dot_general x1, matrix products, body(): jnp.einsum('kr,rpd->kpd', selector, returned, preferred_element_type=jnp....  8.7 us
    dot_general x1, matrix products, body(): lax.dot_general(neg_grads, q4, (((2,), (0,)), ((), ())), preferred_elemen...  6.93 us
  transfers between devices with their start and end apart: 14, of which 9 were waited for; matrix products, arithmetic and copies ran while one was open for 13% of the time, Pallas kernels for 0%

profile of v10, /device:TPU:1, one launch (start us, length us, event | category | flops | bytes accessed | tf_op | source)
XLA Modules:
  0.0 262.9 jit_solution(7263010753045148914)
XLA Ops:
  2.2 2.8 %gather_fusion.2 = bf16[64,128,256]{2,1,0:T(8,128)(2,1)} fusion(bf16[32,128,256]{2,1,0:T(8,128)(2,1)S(1)} %bitcast.118, s32[1024]{0:T(1024)S(1)} %pad_clamp_fusion), kind=kCustom, calls=%fused_computation.2 | custom fusion | bytes 8388864 | tf_op jit(solution)/shard_map/jit(_take)/gather | solution.py:30
  5.1 16.7 %all-to-all-start = ((bf16[256,32,256]{2,1,0:T(8,128)(2,1)}), bf16[256,32,256]{2,1,0:T(8,128)(2,1)}, u32[]{:S(2)}, u32[]{:S(2)}) async-start(bf16[256,32,256]{2,1,0:T(8,128)(2,1)} %bitcast.119), calls=%async_computation | async-start | bytes 8388608 | tf_op jit(solution)/shard_map/all_to_all | solution.py:31
  21.8 2.0 gather_fusion
  24.8 1.4 collective-permute-start
  26.2 2.4 collective-permute-start.1
  30.5 11.6 %collective-permute-done = bf16[640,256]{1,0:T(8,128)(2,1)S(1)} collective-permute-done((bf16[640,256]{1,0:T(8,128)(2,1)}, bf16[640,256]{1,0:T(8,128)(2,1)S(1)}, u32[]{:S(2)}, u32[]{:S(2)}) %collective-permute-start) | collective-permute-done | bytes 327712 | tf_op jit(solution)/shard_map/ppermute | solution.py:11
  42.1 13.6 %collective-permute-done.1 = bf16[640,256]{1,0:T(8,128)(2,1)} collective-permute-done((bf16[640,256]{1,0:T(8,128)(2,1)S(1)}, bf16[640,256]{1,0:T(8,128)(2,1)}, u32[]{:S(2)}, u32[]{:S(2)}) %collective-permute-start.1) | collective-permute-done | bytes 327712 | tf_op jit(solution)/shard_map/ppermute | solution.py:11
  55.7 1.4 pad_maximum_fusion.1
  57.1 1.8 gather_fusion.1
  58.9 1.8 fusion.34
  60.7 59.8 %all-to-all-done = bf16[256,32,256]{2,1,0:T(8,128)(2,1)} async-done(((bf16[256,32,256]{2,1,0:T(8,128)(2,1)}), bf16[256,32,256]{2,1,0:T(8,128)(2,1)}, u32[]{:S(2)}, u32[]{:S(2)}) %all-to-all-start) | async-done | bytes 4194336 | tf_op jit(solution)/shard_map/all_to_all | solution.py:31
  120.5 5.0 %fusion.3 = (f32[512]{0:T(512)S(1)}, f32[64,32,512,1]{2,1,3,0:T(8,128)S(1)}) fusion(pred[64]{0:T(512)(128)(4,1)S(1)} %compare_bitcast_fusion, bf16[64,4,32,256]{3,2,1,0:T(8,128)(2,1)} %bitcast.11, bf16[4,640,256]{2,1,0:T(8,128)(2,1)} %gather_fusion.1), kind=kOutput, calls=%fused_computation.15 | convolution fusion | flops 2150628864 | bytes 9439296 | tf_op jit(solution)/shard_map/dot_general | solution.py:63
  125.5 2.0 copy-done.1
  127.5 1.3 select_reduce_fusion
  129.4 2.4 collective-permute-start.5
  134.3 6.9 %multiply_convert_fusion = bf16[64,32,4,256]{3,1,2,0:T(8,128)(2,1)} fusion(bf16[4,640,256]{2,1,0:T(8,128)(2,1)} %gather_fusion.1, f32[64,32,512,1]{2,1,3,0:T(8,128)} %copy-done.1, f32[512]{0:T(512)S(1)} %get-tuple-element.14, pred[64]{0:T(512)(128)(4,1)S(1)} %compare_bitcast_fusion), kind=kOutput, calls=%fused_computation.7 | convolution fusion | flops 2156920832 | bytes 9439296 | tf_op jit(solution)/shard_map/dot_general | solution.py:106
  141.2 9.8 %all-to-all-start.1 = ((bf16[256,32,256]{2,1,0:T(8,128)(2,1)}), bf16[256,32,256]{2,1,0:T(8,128)(2,1)}, u32[]{:S(2)}, u32[]{:S(2)}) async-start(bf16[256,32,256]{2,1,0:T(8,128)(2,1)} %bitcast.121), calls=%async_computation.1 | async-start | bytes 8388608 | tf_op jit(solution)/shard_map/all_to_all | solution.py:110
  151.2 3.0 %collective-permute-start.10 = (bf16[128,512]{1,0:T(8,128)(2,1)S(1)}, bf16[128,512]{1,0:T(8,128)(2,1)S(1)}, u32[]{:S(2)}, u32[]{:S(2)}) collective-permute-start(bf16[128,512]{1,0:T(8,128)(2,1)S(1)} %subtract_convert_fusion), channel_id=1, source_target_pairs={{0,2},{1,3},{2,0},{3,1},{4,6},{5,7},{6,4},{7,5},{8,10},{9,11},{10,... | collective-permute-start | bytes 393224 | tf_op jit(solution)/shard_map/ppermute | solution.py:11
  154.5 2.4 collective-permute-start.11
  156.9 1.4 fusion.18
  158.3 5.9 %fusion.7 = f32[512,4,256]{2,0,1:T(8,128)S(1)} fusion(f32[512,4,256]{2,0,1:T(8,128)S(1)} %fusion.18, bf16[64,4,32,256]{3,2,1,0:T(8,128)(2,1)} %bitcast.11, f32[64,32,512,1]{2,1,3,0:T(8,128)} %copy-done.1, f32[512]{0:T(512)S(1)} %get-tuple-element.14, pred[64]{0:T(512)(128)(4,1)S(1)} %compare_bitcast_fusion), kind=kOutput, calls=%fused_computation.18 | convolution fusion | flops 2153775104 | bytes 12585024 | tf_op jit(solution)/shard_map/dot_general | solution.py:91
  164.2 1.4 dynamic-slice_bitcast_fusion.3
  167.2 2.3 collective-permute-done.9
  171.3 6.0 %scatter_custom_fusion = f32[4096,256]{1,0:T(8,128)} fusion(s32[512]{0:T(512)S(1)} %compare_select_fusion, f32[512,256]{1,0:T(8,128)} %convolution_multiply_fusion, f32[]{:T(128)} %constant.103.clone.1), kind=kCustom, calls=%fused_computation.20 | custom fusion | flops 131072 | bytes 4194816 | tf_op jit(solution)/shard_map/scatter-add | solution.py:123
  177.3 11.3 %collective-permute-done.8 = f32[512,256]{1,0:T(8,128)} collective-permute-done((f32[512,256]{1,0:T(8,128)}, f32[512,256]{1,0:T(8,128)}, u32[]{:S(2)}, u32[]{:S(2)}) %collective-permute-start.8) | collective-permute-done | bytes 524320 | tf_op jit(solution)/shard_map/ppermute | solution.py:11
  189.3 20.9 %collective-permute-done.6 = f32[512,256]{1,0:T(8,128)} collective-permute-done((f32[512,256]{1,0:T(8,128)}, f32[512,256]{1,0:T(8,128)}, u32[]{:S(2)}, u32[]{:S(2)}) %collective-permute-start.6) | collective-permute-done | bytes 524320 | tf_op jit(solution)/shard_map/ppermute | solution.py:11
  210.2 2.9 %pad_maximum_fusion = f32[4,512,256]{2,1,0:T(8,128)} fusion(f32[1,512,256]{2,1,0:T(8,128)} %bitcast.33, f32[1,512,256]{2,1,0:T(8,128)} %bitcast.31, f32[1,512,256]{2,1,0:T(8,128)} %bitcast.29, f32[1,512,256]{2,1,0:T(8,128)S(1)} %copy-done.2), kind=kLoop, calls=%fused_computation.19 | loop fusion | flops 1572864 | bytes 4194304 | tf_op jit(solution)/shard_map/stack | solution.py:14
  213.2 3.6 %gather_fusion.4 = f32[4,512,256]{2,1,0:T(8,128)} fusion(f32[4,512,256]{2,1,0:T(8,128)} %pad_maximum_fusion, s32[1024]{0:T(1024)S(1)} %pad_clamp_fusion.1), kind=kCustom, calls=%fused_computation.4 | custom fusion | bytes 4194320 | tf_op jit(solution)/shard_map/jit(_take)/gather | solution.py:14
  216.7 2.6 reduce_sum.59
  219.3 30.5 %all-to-all-done.1 = bf16[256,32,256]{2,1,0:T(8,128)(2,1)} async-done(((bf16[256,32,256]{2,1,0:T(8,128)(2,1)}), bf16[256,32,256]{2,1,0:T(8,128)(2,1)}, u32[]{:S(2)}, u32[]{:S(2)}) %all-to-all-start.1) | async-done | bytes 4194336 | tf_op jit(solution)/shard_map/all_to_all | solution.py:110
  249.8 8.7 %copy_add_fusion = f32[32,128,256]{2,0,1:T(8,128)S(1)} fusion(f32[32,128,256]{2,1,0:T(8,128)} %bitcast.120, bf16[64,128,256]{2,1,0:T(8,128)(2,1)} %bitcast.39, s32[64]{0:T(128)S(1)} %get-tuple-element.9), kind=kOutput, calls=%fused_computation.10 | convolution fusion | flops 135268352 | bytes 12583168 | tf_op jit(solution)/shard_map/kr,rpd->kpd/dot_general | solution.py:129
  258.5 4.4 %copy.29 = f32[32,128,256]{2,1,0:T(8,128)} copy(f32[32,128,256]{2,0,1:T(8,128)S(1)} %copy_add_fusion) | data formatting | bytes 8388608 | tf_op jit(solution)/shard_map/add | solution.py:130
  (51 shorter events, 12.0 us)
Async XLA Ops:
  0.6 1.6 copy-start
  5.1 16.7 %copy-start.6 = (s32[512]{0:T(512)S(1)}, s32[512]{0:T(512)}, u32[]{:S(2)}) copy-start(s32[512]{0:T(512)} %param.6) | copy-start | bytes 6148
  5.1 18.8 %copy-start.3 = (bf16[512,256]{1,0:T(8,128)(2,1)S(1)}, bf16[512,256]{1,0:T(8,128)(2,1)}, u32[]{:S(2)}) copy-start(bf16[512,256]{1,0:T(8,128)(2,1)} %param.4) | copy-start | bytes 786436
  5.1 115.4 %all-to-all-start = ((bf16[256,32,256]{2,1,0:T(8,128)(2,1)}), bf16[256,32,256]{2,1,0:T(8,128)(2,1)}, u32[]{:S(2)}, u32[]{:S(2)}) async-start(bf16[256,32,256]{2,1,0:T(8,128)(2,1)} %bitcast.119), calls=%async_computation | async-start | bytes 8388608 | tf_op jit(solution)/shard_map/all_to_all | solution.py:31
  24.8 17.3 %collective-permute-start = (bf16[640,256]{1,0:T(8,128)(2,1)}, bf16[640,256]{1,0:T(8,128)(2,1)S(1)}, u32[]{:S(2)}, u32[]{:S(2)}) collective-permute-start(bf16[640,256]{1,0:T(8,128)(2,1)} %get-tuple-element.20), channel_id=1, source_target_pairs={{0,1},{1,2},{2,3},{3,0},{4,5},{5,6},{6,7},{7,4},{8,9},{9,10},{10,1... | collective-permute-start | bytes 983048 | tf_op jit(solution)/shard_map/ppermute | solution.py:11
  26.2 29.5 %collective-permute-start.1 = (bf16[640,256]{1,0:T(8,128)(2,1)S(1)}, bf16[640,256]{1,0:T(8,128)(2,1)}, u32[]{:S(2)}, u32[]{:S(2)}) collective-permute-start(bf16[640,256]{1,0:T(8,128)(2,1)S(1)} %get-tuple-element.21), channel_id=1, source_target_pairs={{0,2},{1,3},{2,0},{3,1},{4,6},{5,7},{6,4},{7,5},{8,10},{9,11},{10,... | collective-permute-start | bytes 983048 | tf_op jit(solution)/shard_map/ppermute | solution.py:11
  28.6 27.1 %collective-permute-start.2 = (bf16[640,256]{1,0:T(8,128)(2,1)S(1)}, bf16[640,256]{1,0:T(8,128)(2,1)}, u32[]{:S(2)}, u32[]{:S(2)}) collective-permute-start(bf16[640,256]{1,0:T(8,128)(2,1)S(1)} %get-tuple-element.22), channel_id=1, source_target_pairs={{0,3},{1,0},{2,1},{3,2},{4,7},{5,4},{6,5},{7,6},{8,11},{9,8},{10,9... | collective-permute-start | bytes 983048 | tf_op jit(solution)/shard_map/ppermute | solution.py:11
  42.1 13.6 %copy-start.5 = (bf16[640,256]{1,0:T(8,128)(2,1)}, bf16[640,256]{1,0:T(8,128)(2,1)S(1)}, u32[]{:S(2)}) copy-start(bf16[640,256]{1,0:T(8,128)(2,1)S(1)} %collective-permute-done) | copy-start | bytes 983044
  125.5 2.0 copy-start.1
  128.9 4.1 %collective-permute-start.4 = (f32[3,512]{1,0:T(4,128)S(1)}, f32[3,512]{1,0:T(4,128)S(1)}, u32[]{:S(2)}, u32[]{:S(2)}) collective-permute-start(f32[3,512]{1,0:T(4,128)S(1)} %get-tuple-element.32), channel_id=1, source_target_pairs={{0,2},{1,3},{2,0},{3,1},{4,6},{5,7},{6,4},{7,5},{8,10},{9,11},{10,... | collective-permute-start | bytes 18440 | tf_op jit(solution)/shard_map/ppermute | solution.py:11
  129.0 4.0 %collective-permute-start.3 = (f32[3,512]{1,0:T(4,128)S(1)}, f32[3,512]{1,0:T(4,128)S(1)}, u32[]{:S(2)}, u32[]{:S(2)}) collective-permute-start(f32[3,512]{1,0:T(4,128)S(1)} %get-tuple-element.32), channel_id=1, source_target_pairs={{0,1},{1,2},{2,3},{3,0},{4,5},{5,6},{6,7},{7,4},{8,9},{9,10},{10,1... | collective-permute-start | bytes 18440 | tf_op jit(solution)/shard_map/ppermute | solution.py:11
  129.4 3.6 %collective-permute-start.5 = (f32[3,512]{1,0:T(4,128)S(1)}, f32[3,512]{1,0:T(4,128)S(1)}, u32[]{:S(2)}, u32[]{:S(2)}) collective-permute-start(f32[3,512]{1,0:T(4,128)S(1)} %get-tuple-element.32), channel_id=1, source_target_pairs={{0,3},{1,0},{2,1},{3,2},{4,7},{5,4},{6,5},{7,6},{8,11},{9,8},{10,9... | collective-permute-start | bytes 18440 | tf_op jit(solution)/shard_map/ppermute | solution.py:11
  141.2 108.6 %all-to-all-start.1 = ((bf16[256,32,256]{2,1,0:T(8,128)(2,1)}), bf16[256,32,256]{2,1,0:T(8,128)(2,1)}, u32[]{:S(2)}, u32[]{:S(2)}) async-start(bf16[256,32,256]{2,1,0:T(8,128)(2,1)} %bitcast.121), calls=%async_computation.1 | async-start | bytes 8388608 | tf_op jit(solution)/shard_map/all_to_all | solution.py:110
  151.2 15.2 %collective-permute-start.10 = (bf16[128,512]{1,0:T(8,128)(2,1)S(1)}, bf16[128,512]{1,0:T(8,128)(2,1)S(1)}, u32[]{:S(2)}, u32[]{:S(2)}) collective-permute-start(bf16[128,512]{1,0:T(8,128)(2,1)S(1)} %subtract_convert_fusion), channel_id=1, source_target_pairs={{0,2},{1,3},{2,0},{3,1},{4,6},{5,7},{6,4},{7,5},{8,10},{9,11},{10,... | collective-permute-start | bytes 393224 | tf_op jit(solution)/shard_map/ppermute | solution.py:11
  154.2 15.3 %collective-permute-start.9 = (bf16[128,512]{1,0:T(8,128)(2,1)S(1)}, bf16[128,512]{1,0:T(8,128)(2,1)S(1)}, u32[]{:S(2)}, u32[]{:S(2)}) collective-permute-start(bf16[128,512]{1,0:T(8,128)(2,1)S(1)} %subtract_convert_fusion), channel_id=1, source_target_pairs={{0,1},{1,2},{2,3},{3,0},{4,5},{5,6},{6,7},{7,4},{8,9},{9,10},{10,1... | collective-permute-start | bytes 393224 | tf_op jit(solution)/shard_map/ppermute | solution.py:11
  154.5 15.0 %collective-permute-start.11 = (bf16[128,512]{1,0:T(8,128)(2,1)S(1)}, bf16[128,512]{1,0:T(8,128)(2,1)S(1)}, u32[]{:S(2)}, u32[]{:S(2)}) collective-permute-start(bf16[128,512]{1,0:T(8,128)(2,1)S(1)} %subtract_convert_fusion), channel_id=1, source_target_pairs={{0,3},{1,0},{2,1},{3,2},{4,7},{5,4},{6,5},{7,6},{8,11},{9,8},{10,9... | collective-permute-start | bytes 393224 | tf_op jit(solution)/shard_map/ppermute | solution.py:11
  164.2 6.0 %copy-start.4 = (bf16[512,256]{1,0:T(8,128)(2,1)S(1)}, bf16[512,256]{1,0:T(8,128)(2,1)}, u32[]{:S(2)}) copy-start(bf16[512,256]{1,0:T(8,128)(2,1)} %param.4) | copy-start | bytes 786436
  165.6 23.0 %collective-permute-start.8 = (f32[512,256]{1,0:T(8,128)}, f32[512,256]{1,0:T(8,128)}, u32[]{:S(2)}, u32[]{:S(2)}) collective-permute-start(f32[512,256]{1,0:T(8,128)} %get-tuple-element.16), channel_id=1, source_target_pairs={{0,3},{1,0},{2,1},{3,2},{4,7},{5,4},{6,5},{7,6},{8,11},{9,8},{10,9... | collective-permute-start | bytes 1572872 | tf_op jit(solution)/shard_map/ppermute | solution.py:11
  165.6 23.7 %collective-permute-start.7 = (f32[512,256]{1,0:T(8,128)}, f32[512,256]{1,0:T(8,128)}, u32[]{:S(2)}, u32[]{:S(2)}) collective-permute-start(f32[512,256]{1,0:T(8,128)} %get-tuple-element.17), channel_id=1, source_target_pairs={{0,2},{1,3},{2,0},{3,1},{4,6},{5,7},{6,4},{7,5},{8,10},{9,11},{10,... | collective-permute-start | bytes 1572872 | tf_op jit(solution)/shard_map/ppermute | solution.py:11
  166.4 43.8 %collective-permute-start.6 = (f32[512,256]{1,0:T(8,128)}, f32[512,256]{1,0:T(8,128)}, u32[]{:S(2)}, u32[]{:S(2)}) collective-permute-start(f32[512,256]{1,0:T(8,128)} %get-tuple-element.18), channel_id=1, source_target_pairs={{0,1},{1,2},{2,3},{3,0},{4,5},{5,6},{6,7},{7,4},{8,9},{9,10},{10,1... | collective-permute-start | bytes 1572872 | tf_op jit(solution)/shard_map/ppermute | solution.py:11
  170.1 40.1 %copy-start.2 = (f32[1,512,256]{2,1,0:T(8,128)S(1)}, f32[1,512,256]{2,1,0:T(8,128)}, u32[]{:S(2)}) copy-start(f32[1,512,256]{2,1,0:T(8,128)} %get-tuple-element.15) | copy-start | bytes 1572868

commit v11 on v9

--- a/solution.py
+++ b/solution.py
@@ -1,9 +1,47 @@
 import jax
 import jax.numpy as jnp
 from jax import lax
+from jax.experimental import pallas as pl
+from jax.experimental.pallas import tpu as pltpu
 from jax.sharding import PartitionSpec as P
 
 PBS = 128
+PER = 8
+
+def _segment_kernel(asked_ref, ret_ref, pos_ref, out_ref):
+    step = pl.program_id(0)
+
+    @pl.when(step == 0)
+    def _():
+        out_ref[...] = pos_ref[...]
+
+    for t in range(PER):
+        k = asked_ref[step * PER + t]
+
+        @pl.when(k >= 0)
+        def _():
+            out_ref[k] = out_ref[k] + ret_ref[t].astype(jnp.float32)
+
+
+def segment_add(asked, returned, pos_blocks):
+    n, rows, width = returned.shape
+    blocks = pos_blocks.shape[0]
+    return pl.pallas_call(
+        _segment_kernel,
+        grid_spec=pltpu.PrefetchScalarGridSpec(
+            num_scalar_prefetch=1,
+            grid=(n // PER,),
+            in_specs=[
+                pl.BlockSpec((PER, rows, width), lambda i, a: (i, 0, 0)),
+                pl.BlockSpec((blocks, rows, width), lambda i, a: (0, 0, 0)),
+            ],
+            out_specs=pl.BlockSpec((blocks, rows, width), lambda i, a: (0, 0, 0)),
+        ),
+        out_shape=jax.ShapeDtypeStruct(pos_blocks.shape, jnp.float32),
+        compiler_params=pltpu.CompilerParams(dimension_semantics=("arbitrary",)),
+        cost_estimate=pl.CostEstimate(flops=n * rows * width, transcendentals=0,
+                                      bytes_accessed=returned.size * 2 + pos_blocks.size * 8),
+    )(asked, returned, pos_blocks)
 
 
 def from_sources(payload, me, n):
@@ -123,11 +161,9 @@
     pos_part = jnp.zeros((block_count * PBS, shard_width), jnp.float32).at[positives].add(pos_back)
     returned, pos_part = lax.optimization_barrier((returned, pos_part))
 
-    selector = (asked[None, :] == jnp.arange(block_count, dtype=jnp.int32)[:, None]).astype(
-        jnp.bfloat16
-    )
-    block_grad = jnp.einsum("kr,rpd->kpd", selector, returned, preferred_element_type=jnp.float32)
-    passage_grad = block_grad.reshape(block_count * PBS, shard_width) + pos_part
+    passage_grad = segment_add(
+        asked, returned, pos_part.reshape(block_count, PBS, shard_width)
+    ).reshape(block_count * PBS, shard_width)
     return (losses, query_grad, passage_grad)
 
 

time: 261 us -> 260 us (level)
  Pallas kernels: 0 us -> 9.21 us
  matrix products: 27.3 us -> 22.1 us
  local copies, waits for them, and re-layouts: 17.6 us -> 14.8 us
    pallas_call x0 -> x1, Pallas kernels: none -> 9.21 us  [segment_add(): pl.pallas_call(_segment_kernel, grid_spec=pltpu.PrefetchScalarGridSpec(nu...]
    dot_general x1 -> x0, matrix products: 5.21 us -> none  [body(): jnp.einsum('kr,rpd->kpd', selector, returned, preferred_element_type=jnp....]
    add x1 -> x0, other arithmetic: 2.82 us -> none  [body(): passage_grad = block_grad.reshape(block_count * PBS, shard_width) + pos_part]
where the time goes in v11:
time: 260 us; the launch traced here: 259 us
  waiting for transfers between devices  152 us (58%)
  starting transfers between devices  41.4 us (16%)
  matrix products  22.1 us (8%)
  other arithmetic  18.5 us (7%)
  local copies, waits for them, and re-layouts  14.8 us (6%)
  Pallas kernels  9.21 us (4%)
    ppermute x12, waiting for transfers between devices, from_sources(): lax.ppermute(payload(k), 'mp', [(i, (i + k) % n) for i in range(n)])  61.7 us
    all_to_all x1, waiting for transfers between devices, body(): lax.all_to_all(outgoing.reshape(dp_count * mp_count, quarter, shard_width...  59.8 us
    all_to_all x1, waiting for transfers between devices, body(): lax.all_to_all(sending.reshape(dp_count * mp_count, quarter, shard_width)...  30.5 us
    all_to_all x1, starting transfers between devices, body(): lax.all_to_all(outgoing.reshape(dp_count * mp_count, quarter, shard_width...  16.7 us
    ppermute x12, starting transfers between devices, from_sources(): lax.ppermute(payload(k), 'mp', [(i, (i + k) % n) for i in range(n)])  14.9 us
    all_to_all x1, starting transfers between devices, body(): lax.all_to_all(sending.reshape(dp_count * mp_count, quarter, shard_width)...  9.84 us
    pallas_call x1, Pallas kernels, segment_add(): pl.pallas_call(_segment_kernel, grid_spec=pltpu.PrefetchScalarGridSpec(nu...  9.21 us
    dot_general x1, matrix products, body(): lax.dot_general(neg_grads, q4, (((2,), (0,)), ((), ())), preferred_elemen...  6.93 us
  transfers between devices with their start and end apart: 14, of which 9 were waited for; matrix products, arithmetic and copies ran while one was open for 13% of the time, Pallas kernels for 0%

profile of v11, /device:TPU:1, one launch (start us, length us, event | category | flops | bytes accessed | tf_op | source)
XLA Modules:
  0.0 259.0 jit_solution(18045288949328582812)
XLA Ops:
  0.7 1.6 dynamic-slice_reduce_fusion
  2.3 2.8 %gather_fusion.2 = bf16[64,128,256]{2,1,0:T(8,128)(2,1)} fusion(bf16[32,128,256]{2,1,0:T(8,128)(2,1)S(1)} %bitcast.115, s32[1024]{0:T(1024)S(1)} %pad_clamp_fusion), kind=kCustom, calls=%fused_computation.2 | custom fusion | bytes 8388864 | tf_op jit(solution)/shard_map/jit(_take)/gather | solution.py:68
  5.1 16.7 %all-to-all-start = ((bf16[256,32,256]{2,1,0:T(8,128)(2,1)}), bf16[256,32,256]{2,1,0:T(8,128)(2,1)}, u32[]{:S(2)}, u32[]{:S(2)}) async-start(bf16[256,32,256]{2,1,0:T(8,128)(2,1)} %bitcast.116), calls=%async_computation | async-start | bytes 8388608 | tf_op jit(solution)/shard_map/all_to_all | solution.py:69
  21.9 2.0 gather_fusion
  24.8 1.4 collective-permute-start
  26.2 2.4 collective-permute-start.1
  30.5 11.6 %collective-permute-done = bf16[640,256]{1,0:T(8,128)(2,1)S(1)} collective-permute-done((bf16[640,256]{1,0:T(8,128)(2,1)}, bf16[640,256]{1,0:T(8,128)(2,1)S(1)}, u32[]{:S(2)}, u32[]{:S(2)}) %collective-permute-start) | collective-permute-done | bytes 327712 | tf_op jit(solution)/shard_map/ppermute | solution.py:49
  42.1 13.6 %collective-permute-done.1 = bf16[640,256]{1,0:T(8,128)(2,1)} collective-permute-done((bf16[640,256]{1,0:T(8,128)(2,1)S(1)}, bf16[640,256]{1,0:T(8,128)(2,1)}, u32[]{:S(2)}, u32[]{:S(2)}) %collective-permute-start.1) | collective-permute-done | bytes 327712 | tf_op jit(solution)/shard_map/ppermute | solution.py:49
  55.7 1.4 pad_maximum_fusion.1
  57.1 1.8 gather_fusion.1
  58.9 1.8 fusion.27
  60.7 59.8 %all-to-all-done = bf16[256,32,256]{2,1,0:T(8,128)(2,1)} async-done(((bf16[256,32,256]{2,1,0:T(8,128)(2,1)}), bf16[256,32,256]{2,1,0:T(8,128)(2,1)}, u32[]{:S(2)}, u32[]{:S(2)}) %all-to-all-start) | async-done | bytes 4194336 | tf_op jit(solution)/shard_map/all_to_all | solution.py:69
  120.5 5.0 %fusion.1 = (f32[512]{0:T(512)S(1)}, f32[64,32,512,1]{2,1,3,0:T(8,128)S(1)}) fusion(pred[64]{0:T(512)(128)(4,1)S(1)} %compare_bitcast_fusion, bf16[64,4,32,256]{3,2,1,0:T(8,128)(2,1)} %bitcast.11, bf16[4,640,256]{2,1,0:T(8,128)(2,1)} %gather_fusion.1), kind=kOutput, calls=%fused_computation.12 | convolution fusion | flops 2150628864 | bytes 9439296 | tf_op jit(solution)/shard_map/dot_general | solution.py:101
  125.5 2.0 copy-done.1
  127.5 1.3 select_reduce_fusion
  129.4 2.4 collective-permute-start.5
  134.3 6.9 %multiply_convert_fusion = bf16[64,32,4,256]{3,1,2,0:T(8,128)(2,1)} fusion(bf16[4,640,256]{2,1,0:T(8,128)(2,1)} %gather_fusion.1, f32[64,32,512,1]{2,1,3,0:T(8,128)} %copy-done.1, f32[512]{0:T(512)S(1)} %get-tuple-element.14, pred[64]{0:T(512)(128)(4,1)S(1)} %compare_bitcast_fusion), kind=kOutput, calls=%fused_computation.7 | convolution fusion | flops 2156920832 | bytes 9439296 | tf_op jit(solution)/shard_map/dot_general | solution.py:144
  141.2 9.8 %all-to-all-start.1 = ((bf16[256,32,256]{2,1,0:T(8,128)(2,1)}), bf16[256,32,256]{2,1,0:T(8,128)(2,1)}, u32[]{:S(2)}, u32[]{:S(2)}) async-start(bf16[256,32,256]{2,1,0:T(8,128)(2,1)} %bitcast.118), calls=%async_computation.1 | async-start | bytes 8388608 | tf_op jit(solution)/shard_map/all_to_all | solution.py:148
  151.3 3.0 %collective-permute-start.10 = (bf16[128,512]{1,0:T(8,128)(2,1)S(1)}, bf16[128,512]{1,0:T(8,128)(2,1)S(1)}, u32[]{:S(2)}, u32[]{:S(2)}) collective-permute-start(bf16[128,512]{1,0:T(8,128)(2,1)S(1)} %subtract_convert_fusion), channel_id=1, source_target_pairs={{0,2},{1,3},{2,0},{3,1},{4,6},{5,7},{6,4},{7,5},{8,10},{9,11},{10,... | collective-permute-start | bytes 393224 | tf_op jit(solution)/shard_map/ppermute | solution.py:49
  154.5 2.4 collective-permute-start.11
  156.9 1.4 fusion.14
  158.3 5.9 %fusion.3 = f32[512,4,256]{2,0,1:T(8,128)S(1)} fusion(f32[512,4,256]{2,0,1:T(8,128)S(1)} %fusion.14, bf16[64,4,32,256]{3,2,1,0:T(8,128)(2,1)} %bitcast.11, f32[64,32,512,1]{2,1,3,0:T(8,128)} %copy-done.1, f32[512]{0:T(512)S(1)} %get-tuple-element.14, pred[64]{0:T(512)(128)(4,1)S(1)} %compare_bitcast_fusion), kind=kOutput, calls=%fused_computation.15 | convolution fusion | flops 2153775104 | bytes 12585024 | tf_op jit(solution)/shard_map/dot_general | solution.py:129
  164.3 1.4 dynamic-slice_bitcast_fusion.3
  167.2 2.3 collective-permute-done.9
  171.3 6.0 %scatter_custom_fusion = f32[4096,256]{1,0:T(8,128)} fusion(s32[512]{0:T(512)S(1)} %compare_select_fusion, f32[512,256]{1,0:T(8,128)} %convolution_multiply_fusion, f32[]{:T(128)} %constant.103.clone.1), kind=kCustom, calls=%fused_computation.17 | custom fusion | flops 131072 | bytes 4194816 | tf_op jit(solution)/shard_map/scatter-add | solution.py:161
  177.3 11.3 %collective-permute-done.8 = f32[512,256]{1,0:T(8,128)} collective-permute-done((f32[512,256]{1,0:T(8,128)}, f32[512,256]{1,0:T(8,128)}, u32[]{:S(2)}, u32[]{:S(2)}) %collective-permute-start.8) | collective-permute-done | bytes 524320 | tf_op jit(solution)/shard_map/ppermute | solution.py:49
  189.2 21.1 %collective-permute-done.6 = f32[512,256]{1,0:T(8,128)} collective-permute-done((f32[512,256]{1,0:T(8,128)}, f32[512,256]{1,0:T(8,128)}, u32[]{:S(2)}, u32[]{:S(2)}) %collective-permute-start.6) | collective-permute-done | bytes 524320 | tf_op jit(solution)/shard_map/ppermute | solution.py:49
  210.3 2.8 %pad_maximum_fusion = f32[4,512,256]{2,1,0:T(8,128)} fusion(f32[1,512,256]{2,1,0:T(8,128)} %bitcast.33, f32[1,512,256]{2,1,0:T(8,128)} %bitcast.31, f32[1,512,256]{2,1,0:T(8,128)} %bitcast.29, f32[1,512,256]{2,1,0:T(8,128)S(1)} %copy-done.2), kind=kLoop, calls=%fused_computation.16 | loop fusion | flops 1572864 | bytes 4194304 | tf_op jit(solution)/shard_map/stack | solution.py:52
  213.1 3.6 %gather_fusion.4 = f32[4,512,256]{2,1,0:T(8,128)} fusion(f32[4,512,256]{2,1,0:T(8,128)} %pad_maximum_fusion, s32[1024]{0:T(1024)S(1)} %pad_clamp_fusion.1), kind=kCustom, calls=%fused_computation.4 | custom fusion | bytes 4194320 | tf_op jit(solution)/shard_map/jit(_take)/gather | solution.py:52
  216.8 2.6 reduce_sum.59
  219.3 30.5 %all-to-all-done.1 = bf16[256,32,256]{2,1,0:T(8,128)(2,1)} async-done(((bf16[256,32,256]{2,1,0:T(8,128)(2,1)}), bf16[256,32,256]{2,1,0:T(8,128)(2,1)}, u32[]{:S(2)}, u32[]{:S(2)}) %all-to-all-start.1) | async-done | bytes 4194336 | tf_op jit(solution)/shard_map/all_to_all | solution.py:148
  249.8 9.2 %shard_map.67 = f32[32,128,256]{2,1,0:T(8,128)} custom-call(s32[64]{0:T(128)} %get-tuple-element.9.asked_ref, bf16[64,128,256]{2,1,0:T(8,128)(2,1)} %bitcast.38.ret_ref, f32[32,128,256]{2,1,0:T(8,128)} %bitcast.117), custom_call_target="tpu_custom_call" | custom-call | flops 2097152 | bytes 12582912 | tf_op jit(solution)/shard_map/pallas_call | solution.py:29
  (50 shorter events, 10.2 us)
Async XLA Ops:
  0.6 1.7 copy-start
  5.1 16.7 %copy-start.6 = (s32[512]{0:T(512)S(1)}, s32[512]{0:T(512)}, u32[]{:S(2)}) copy-start(s32[512]{0:T(512)} %param.6) | copy-start | bytes 6148
  5.1 18.8 %copy-start.3 = (bf16[512,256]{1,0:T(8,128)(2,1)S(1)}, bf16[512,256]{1,0:T(8,128)(2,1)}, u32[]{:S(2)}) copy-start(bf16[512,256]{1,0:T(8,128)(2,1)} %param.4) | copy-start | bytes 786436
  5.1 115.4 %all-to-all-start = ((bf16[256,32,256]{2,1,0:T(8,128)(2,1)}), bf16[256,32,256]{2,1,0:T(8,128)(2,1)}, u32[]{:S(2)}, u32[]{:S(2)}) async-start(bf16[256,32,256]{2,1,0:T(8,128)(2,1)} %bitcast.116), calls=%async_computation | async-start | bytes 8388608 | tf_op jit(solution)/shard_map/all_to_all | solution.py:69
  24.8 17.3 %collective-permute-start = (bf16[640,256]{1,0:T(8,128)(2,1)}, bf16[640,256]{1,0:T(8,128)(2,1)S(1)}, u32[]{:S(2)}, u32[]{:S(2)}) collective-permute-start(bf16[640,256]{1,0:T(8,128)(2,1)} %get-tuple-element.20), channel_id=1, source_target_pairs={{0,1},{1,2},{2,3},{3,0},{4,5},{5,6},{6,7},{7,4},{8,9},{9,10},{10,1... | collective-permute-start | bytes 983048 | tf_op jit(solution)/shard_map/ppermute | solution.py:49
  26.2 29.5 %collective-permute-start.1 = (bf16[640,256]{1,0:T(8,128)(2,1)S(1)}, bf16[640,256]{1,0:T(8,128)(2,1)}, u32[]{:S(2)}, u32[]{:S(2)}) collective-permute-start(bf16[640,256]{1,0:T(8,128)(2,1)S(1)} %get-tuple-element.21), channel_id=1, source_target_pairs={{0,2},{1,3},{2,0},{3,1},{4,6},{5,7},{6,4},{7,5},{8,10},{9,11},{10,... | collective-permute-start | bytes 983048 | tf_op jit(solution)/shard_map/ppermute | solution.py:49
  28.6 27.1 %collective-permute-start.2 = (bf16[640,256]{1,0:T(8,128)(2,1)S(1)}, bf16[640,256]{1,0:T(8,128)(2,1)}, u32[]{:S(2)}, u32[]{:S(2)}) collective-permute-start(bf16[640,256]{1,0:T(8,128)(2,1)S(1)} %get-tuple-element.22), channel_id=1, source_target_pairs={{0,3},{1,0},{2,1},{3,2},{4,7},{5,4},{6,5},{7,6},{8,11},{9,8},{10,9... | collective-permute-start | bytes 983048 | tf_op jit(solution)/shard_map/ppermute | solution.py:49
  42.1 13.6 %copy-start.5 = (bf16[640,256]{1,0:T(8,128)(2,1)}, bf16[640,256]{1,0:T(8,128)(2,1)S(1)}, u32[]{:S(2)}) copy-start(bf16[640,256]{1,0:T(8,128)(2,1)S(1)} %collective-permute-done) | copy-start | bytes 983044
  125.5 2.0 copy-start.1
  129.0 4.1 %collective-permute-start.4 = (f32[3,512]{1,0:T(4,128)S(1)}, f32[3,512]{1,0:T(4,128)S(1)}, u32[]{:S(2)}, u32[]{:S(2)}) collective-permute-start(f32[3,512]{1,0:T(4,128)S(1)} %get-tuple-element.32), channel_id=1, source_target_pairs={{0,2},{1,3},{2,0},{3,1},{4,6},{5,7},{6,4},{7,5},{8,10},{9,11},{10,... | collective-permute-start | bytes 18440 | tf_op jit(solution)/shard_map/ppermute | solution.py:49
  129.1 4.0 %collective-permute-start.3 = (f32[3,512]{1,0:T(4,128)S(1)}, f32[3,512]{1,0:T(4,128)S(1)}, u32[]{:S(2)}, u32[]{:S(2)}) collective-permute-start(f32[3,512]{1,0:T(4,128)S(1)} %get-tuple-element.32), channel_id=1, source_target_pairs={{0,1},{1,2},{2,3},{3,0},{4,5},{5,6},{6,7},{7,4},{8,9},{9,10},{10,1... | collective-permute-start | bytes 18440 | tf_op jit(solution)/shard_map/ppermute | solution.py:49
  129.4 3.6 %collective-permute-start.5 = (f32[3,512]{1,0:T(4,128)S(1)}, f32[3,512]{1,0:T(4,128)S(1)}, u32[]{:S(2)}, u32[]{:S(2)}) collective-permute-start(f32[3,512]{1,0:T(4,128)S(1)} %get-tuple-element.32), channel_id=1, source_target_pairs={{0,3},{1,0},{2,1},{3,2},{4,7},{5,4},{6,5},{7,6},{8,11},{9,8},{10,9... | collective-permute-start | bytes 18440 | tf_op jit(solution)/shard_map/ppermute | solution.py:49
  141.2 108.6 %all-to-all-start.1 = ((bf16[256,32,256]{2,1,0:T(8,128)(2,1)}), bf16[256,32,256]{2,1,0:T(8,128)(2,1)}, u32[]{:S(2)}, u32[]{:S(2)}) async-start(bf16[256,32,256]{2,1,0:T(8,128)(2,1)} %bitcast.118), calls=%async_computation.1 | async-start | bytes 8388608 | tf_op jit(solution)/shard_map/all_to_all | solution.py:148
  151.3 15.3 %collective-permute-start.10 = (bf16[128,512]{1,0:T(8,128)(2,1)S(1)}, bf16[128,512]{1,0:T(8,128)(2,1)S(1)}, u32[]{:S(2)}, u32[]{:S(2)}) collective-permute-start(bf16[128,512]{1,0:T(8,128)(2,1)S(1)} %subtract_convert_fusion), channel_id=1, source_target_pairs={{0,2},{1,3},{2,0},{3,1},{4,6},{5,7},{6,4},{7,5},{8,10},{9,11},{10,... | collective-permute-start | bytes 393224 | tf_op jit(solution)/shard_map/ppermute | solution.py:49
  154.2 15.3 %collective-permute-start.9 = (bf16[128,512]{1,0:T(8,128)(2,1)S(1)}, bf16[128,512]{1,0:T(8,128)(2,1)S(1)}, u32[]{:S(2)}, u32[]{:S(2)}) collective-permute-start(bf16[128,512]{1,0:T(8,128)(2,1)S(1)} %subtract_convert_fusion), channel_id=1, source_target_pairs={{0,1},{1,2},{2,3},{3,0},{4,5},{5,6},{6,7},{7,4},{8,9},{9,10},{10,1... | collective-permute-start | bytes 393224 | tf_op jit(solution)/shard_map/ppermute | solution.py:49
  154.5 15.0 %collective-permute-start.11 = (bf16[128,512]{1,0:T(8,128)(2,1)S(1)}, bf16[128,512]{1,0:T(8,128)(2,1)S(1)}, u32[]{:S(2)}, u32[]{:S(2)}) collective-permute-start(bf16[128,512]{1,0:T(8,128)(2,1)S(1)} %subtract_convert_fusion), channel_id=1, source_target_pairs={{0,3},{1,0},{2,1},{3,2},{4,7},{5,4},{6,5},{7,6},{8,11},{9,8},{10,9... | collective-permute-start | bytes 393224 | tf_op jit(solution)/shard_map/ppermute | solution.py:49
  164.2 6.0 %copy-start.4 = (bf16[512,256]{1,0:T(8,128)(2,1)S(1)}, bf16[512,256]{1,0:T(8,128)(2,1)}, u32[]{:S(2)}) copy-start(bf16[512,256]{1,0:T(8,128)(2,1)} %param.4) | copy-start | bytes 786436
  165.7 23.0 %collective-permute-start.8 = (f32[512,256]{1,0:T(8,128)}, f32[512,256]{1,0:T(8,128)}, u32[]{:S(2)}, u32[]{:S(2)}) collective-permute-start(f32[512,256]{1,0:T(8,128)} %get-tuple-element.16), channel_id=1, source_target_pairs={{0,3},{1,0},{2,1},{3,2},{4,7},{5,4},{6,5},{7,6},{8,11},{9,8},{10,9... | collective-permute-start | bytes 1572872 | tf_op jit(solution)/shard_map/ppermute | solution.py:49
  165.7 23.5 %collective-permute-start.7 = (f32[512,256]{1,0:T(8,128)}, f32[512,256]{1,0:T(8,128)}, u32[]{:S(2)}, u32[]{:S(2)}) collective-permute-start(f32[512,256]{1,0:T(8,128)} %get-tuple-element.17), channel_id=1, source_target_pairs={{0,2},{1,3},{2,0},{3,1},{4,6},{5,7},{6,4},{7,5},{8,10},{9,11},{10,... | collective-permute-start | bytes 1572872 | tf_op jit(solution)/shard_map/ppermute | solution.py:49
  166.5 43.7 %collective-permute-start.6 = (f32[512,256]{1,0:T(8,128)}, f32[512,256]{1,0:T(8,128)}, u32[]{:S(2)}, u32[]{:S(2)}) collective-permute-start(f32[512,256]{1,0:T(8,128)} %get-tuple-element.18), channel_id=1, source_target_pairs={{0,1},{1,2},{2,3},{3,0},{4,5},{5,6},{6,7},{7,4},{8,9},{9,10},{10,1... | collective-permute-start | bytes 1572872 | tf_op jit(solution)/shard_map/ppermute | solution.py:49
  170.2 40.1 %copy-start.2 = (f32[1,512,256]{2,1,0:T(8,128)S(1)}, f32[1,512,256]{2,1,0:T(8,128)}, u32[]{:S(2)}) copy-start(f32[1,512,256]{2,1,0:T(8,128)} %get-tuple-element.15) | copy-start | bytes 1572868

commit v12 on v11

--- a/solution.py
+++ b/solution.py
@@ -6,10 +6,10 @@
 from jax.sharding import PartitionSpec as P
 
 PBS = 128
-PER = 8
+PER = 16
 
 def _segment_kernel(asked_ref, ret_ref, pos_ref, out_ref):
-    step = pl.program_id(0)
+    step = pl.program_id(1)
 
     @pl.when(step == 0)
     def _():
@@ -30,15 +30,15 @@
         _segment_kernel,
         grid_spec=pltpu.PrefetchScalarGridSpec(
             num_scalar_prefetch=1,
-            grid=(n // PER,),
+            grid=(2, n // PER),
             in_specs=[
-                pl.BlockSpec((PER, rows, width), lambda i, a: (i, 0, 0)),
-                pl.BlockSpec((blocks, rows, width), lambda i, a: (0, 0, 0)),
+                pl.BlockSpec((PER, rows // 2, width), lambda h, i, a: (i, h, 0)),
+                pl.BlockSpec((blocks, rows // 2, width), lambda h, i, a: (0, h, 0)),
             ],
-            out_specs=pl.BlockSpec((blocks, rows, width), lambda i, a: (0, 0, 0)),
+            out_specs=pl.BlockSpec((blocks, rows // 2, width), lambda h, i, a: (0, h, 0)),
         ),
         out_shape=jax.ShapeDtypeStruct(pos_blocks.shape, jnp.float32),
-        compiler_params=pltpu.CompilerParams(dimension_semantics=("arbitrary",)),
+        compiler_params=pltpu.CompilerParams(dimension_semantics=("arbitrary", "arbitrary")),
         cost_estimate=pl.CostEstimate(flops=n * rows * width, transcendentals=0,
                                       bytes_accessed=returned.size * 2 + pos_blocks.size * 8),
     )(asked, returned, pos_blocks)

time: 260 us -> 260 us (level)
  no operation moved by 1% of the time
where the time goes in v12:
time: 260 us
  waiting for transfers between devices  152 us (58%)
  starting transfers between devices  41.4 us (16%)
  matrix products  22.1 us (8%)
  other arithmetic  18.5 us (7%)
  local copies, waits for them, and re-layouts  14.8 us (6%)
  Pallas kernels  9.72 us (4%)
    ppermute x12, waiting for transfers between devices, from_sources(): lax.ppermute(payload(k), 'mp', [(i, (i + k) % n) for i in range(n)])  61.7 us
    all_to_all x1, waiting for transfers between devices, body(): lax.all_to_all(outgoing.reshape(dp_count * mp_count, quarter, shard_width...  59.8 us
    all_to_all x1, waiting for transfers between devices, body(): lax.all_to_all(sending.reshape(dp_count * mp_count, quarter, shard_width)...  30.5 us
    all_to_all x1, starting transfers between devices, body(): lax.all_to_all(outgoing.reshape(dp_count * mp_count, quarter, shard_width...  16.7 us
    ppermute x12, starting transfers between devices, from_sources(): lax.ppermute(payload(k), 'mp', [(i, (i + k) % n) for i in range(n)])  14.9 us
    all_to_all x1, starting transfers between devices, body(): lax.all_to_all(sending.reshape(dp_count * mp_count, quarter, shard_width)...  9.84 us
    pallas_call x1, Pallas kernels, segment_add(): pl.pallas_call(_segment_kernel, grid_spec=pltpu.PrefetchScalarGridSpec(nu...  9.72 us
    dot_general x1, matrix products, body(): lax.dot_general(neg_grads, q4, (((2,), (0,)), ((), ())), preferred_elemen...  6.93 us
  transfers between devices with their start and end apart: 14, of which 9 were waited for; matrix products, arithmetic and copies ran while one was open for 13% of the time, Pallas kernels for 0%

profile of v12, /device:TPU:1, one launch (start us, length us, event | category | flops | bytes accessed | tf_op | source)
XLA Modules:
  0.0 259.6 jit_solution(14062560144493155102)
XLA Ops:
  0.7 1.6 dynamic-slice_reduce_fusion
  2.3 2.8 %gather_fusion.2 = bf16[64,128,256]{2,1,0:T(8,128)(2,1)} fusion(bf16[32,128,256]{2,1,0:T(8,128)(2,1)S(1)} %bitcast.115, s32[1024]{0:T(1024)S(1)} %pad_clamp_fusion), kind=kCustom, calls=%fused_computation.2 | custom fusion | bytes 8388864 | tf_op jit(solution)/shard_map/jit(_take)/gather | solution.py:68
  5.1 16.7 %all-to-all-start = ((bf16[256,32,256]{2,1,0:T(8,128)(2,1)}), bf16[256,32,256]{2,1,0:T(8,128)(2,1)}, u32[]{:S(2)}, u32[]{:S(2)}) async-start(bf16[256,32,256]{2,1,0:T(8,128)(2,1)} %bitcast.116), calls=%async_computation | async-start | bytes 8388608 | tf_op jit(solution)/shard_map/all_to_all | solution.py:69
  21.9 2.0 gather_fusion
  24.8 1.4 collective-permute-start
  26.2 2.4 collective-permute-start.1
  30.5 11.6 %collective-permute-done = bf16[640,256]{1,0:T(8,128)(2,1)S(1)} collective-permute-done((bf16[640,256]{1,0:T(8,128)(2,1)}, bf16[640,256]{1,0:T(8,128)(2,1)S(1)}, u32[]{:S(2)}, u32[]{:S(2)}) %collective-permute-start) | collective-permute-done | bytes 327712 | tf_op jit(solution)/shard_map/ppermute | solution.py:49
  42.1 13.6 %collective-permute-done.1 = bf16[640,256]{1,0:T(8,128)(2,1)} collective-permute-done((bf16[640,256]{1,0:T(8,128)(2,1)S(1)}, bf16[640,256]{1,0:T(8,128)(2,1)}, u32[]{:S(2)}, u32[]{:S(2)}) %collective-permute-start.1) | collective-permute-done | bytes 327712 | tf_op jit(solution)/shard_map/ppermute | solution.py:49
  55.7 1.4 pad_maximum_fusion.1
  57.1 1.8 gather_fusion.1
  58.9 1.8 fusion.27
  60.7 59.8 %all-to-all-done = bf16[256,32,256]{2,1,0:T(8,128)(2,1)} async-done(((bf16[256,32,256]{2,1,0:T(8,128)(2,1)}), bf16[256,32,256]{2,1,0:T(8,128)(2,1)}, u32[]{:S(2)}, u32[]{:S(2)}) %all-to-all-start) | async-done | bytes 4194336 | tf_op jit(solution)/shard_map/all_to_all | solution.py:69
  120.5 5.0 %fusion.1 = (f32[512]{0:T(512)S(1)}, f32[64,32,512,1]{2,1,3,0:T(8,128)S(1)}) fusion(pred[64]{0:T(512)(128)(4,1)S(1)} %compare_bitcast_fusion, bf16[64,4,32,256]{3,2,1,0:T(8,128)(2,1)} %bitcast.11, bf16[4,640,256]{2,1,0:T(8,128)(2,1)} %gather_fusion.1), kind=kOutput, calls=%fused_computation.12 | convolution fusion | flops 2150628864 | bytes 9439296 | tf_op jit(solution)/shard_map/dot_general | solution.py:101
  125.5 2.0 copy-done.1
  127.5 1.3 select_reduce_fusion
  129.4 2.4 collective-permute-start.5
  134.3 6.9 %multiply_convert_fusion = bf16[64,32,4,256]{3,1,2,0:T(8,128)(2,1)} fusion(bf16[4,640,256]{2,1,0:T(8,128)(2,1)} %gather_fusion.1, f32[64,32,512,1]{2,1,3,0:T(8,128)} %copy-done.1, f32[512]{0:T(512)S(1)} %get-tuple-element.14, pred[64]{0:T(512)(128)(4,1)S(1)} %compare_bitcast_fusion), kind=kOutput, calls=%fused_computation.7 | convolution fusion | flops 2156920832 | bytes 9439296 | tf_op jit(solution)/shard_map/dot_general | solution.py:144
  141.2 9.8 %all-to-all-start.1 = ((bf16[256,32,256]{2,1,0:T(8,128)(2,1)}), bf16[256,32,256]{2,1,0:T(8,128)(2,1)}, u32[]{:S(2)}, u32[]{:S(2)}) async-start(bf16[256,32,256]{2,1,0:T(8,128)(2,1)} %bitcast.118), calls=%async_computation.1 | async-start | bytes 8388608 | tf_op jit(solution)/shard_map/all_to_all | solution.py:148
  151.3 3.0 %collective-permute-start.10 = (bf16[128,512]{1,0:T(8,128)(2,1)S(1)}, bf16[128,512]{1,0:T(8,128)(2,1)S(1)}, u32[]{:S(2)}, u32[]{:S(2)}) collective-permute-start(bf16[128,512]{1,0:T(8,128)(2,1)S(1)} %subtract_convert_fusion), channel_id=1, source_target_pairs={{0,2},{1,3},{2,0},{3,1},{4,6},{5,7},{6,4},{7,5},{8,10},{9,11},{10,... | collective-permute-start | bytes 393224 | tf_op jit(solution)/shard_map/ppermute | solution.py:49
  154.5 2.4 collective-permute-start.11
  156.9 1.4 fusion.14
  158.3 5.9 %fusion.3 = f32[512,4,256]{2,0,1:T(8,128)S(1)} fusion(f32[512,4,256]{2,0,1:T(8,128)S(1)} %fusion.14, bf16[64,4,32,256]{3,2,1,0:T(8,128)(2,1)} %bitcast.11, f32[64,32,512,1]{2,1,3,0:T(8,128)} %copy-done.1, f32[512]{0:T(512)S(1)} %get-tuple-element.14, pred[64]{0:T(512)(128)(4,1)S(1)} %compare_bitcast_fusion), kind=kOutput, calls=%fused_computation.15 | convolution fusion | flops 2153775104 | bytes 12585024 | tf_op jit(solution)/shard_map/dot_general | solution.py:129
  164.3 1.4 dynamic-slice_bitcast_fusion.3
  167.2 2.3 collective-permute-done.9
  171.3 6.0 %scatter_custom_fusion = f32[4096,256]{1,0:T(8,128)} fusion(s32[512]{0:T(512)S(1)} %compare_select_fusion, f32[512,256]{1,0:T(8,128)} %convolution_multiply_fusion, f32[]{:T(128)} %constant.103.clone.1), kind=kCustom, calls=%fused_computation.17 | custom fusion | flops 131072 | bytes 4194816 | tf_op jit(solution)/shard_map/scatter-add | solution.py:161
  177.3 11.3 %collective-permute-done.8 = f32[512,256]{1,0:T(8,128)} collective-permute-done((f32[512,256]{1,0:T(8,128)}, f32[512,256]{1,0:T(8,128)}, u32[]{:S(2)}, u32[]{:S(2)}) %collective-permute-start.8) | collective-permute-done | bytes 524320 | tf_op jit(solution)/shard_map/ppermute | solution.py:49
  189.2 21.1 %collective-permute-done.6 = f32[512,256]{1,0:T(8,128)} collective-permute-done((f32[512,256]{1,0:T(8,128)}, f32[512,256]{1,0:T(8,128)}, u32[]{:S(2)}, u32[]{:S(2)}) %collective-permute-start.6) | collective-permute-done | bytes 524320 | tf_op jit(solution)/shard_map/ppermute | solution.py:49
  210.3 2.8 %pad_maximum_fusion = f32[4,512,256]{2,1,0:T(8,128)} fusion(f32[1,512,256]{2,1,0:T(8,128)} %bitcast.33, f32[1,512,256]{2,1,0:T(8,128)} %bitcast.31, f32[1,512,256]{2,1,0:T(8,128)} %bitcast.29, f32[1,512,256]{2,1,0:T(8,128)S(1)} %copy-done.2), kind=kLoop, calls=%fused_computation.16 | loop fusion | flops 1572864 | bytes 4194304 | tf_op jit(solution)/shard_map/stack | solution.py:52
  213.1 3.6 %gather_fusion.4 = f32[4,512,256]{2,1,0:T(8,128)} fusion(f32[4,512,256]{2,1,0:T(8,128)} %pad_maximum_fusion, s32[1024]{0:T(1024)S(1)} %pad_clamp_fusion.1), kind=kCustom, calls=%fused_computation.4 | custom fusion | bytes 4194320 | tf_op jit(solution)/shard_map/jit(_take)/gather | solution.py:52
  216.8 2.6 reduce_sum.59
  219.3 30.5 %all-to-all-done.1 = bf16[256,32,256]{2,1,0:T(8,128)(2,1)} async-done(((bf16[256,32,256]{2,1,0:T(8,128)(2,1)}), bf16[256,32,256]{2,1,0:T(8,128)(2,1)}, u32[]{:S(2)}, u32[]{:S(2)}) %all-to-all-start.1) | async-done | bytes 4194336 | tf_op jit(solution)/shard_map/all_to_all | solution.py:148
  249.8 9.7 %shard_map.67 = f32[32,128,256]{2,1,0:T(8,128)} custom-call(s32[64]{0:T(128)} %get-tuple-element.9.asked_ref, bf16[64,128,256]{2,1,0:T(8,128)(2,1)} %bitcast.38.ret_ref, f32[32,128,256]{2,1,0:T(8,128)} %bitcast.117), custom_call_target="tpu_custom_call" | custom-call | flops 2097152 | bytes 12582912 | tf_op jit(solution)/shard_map/pallas_call | solution.py:29
  (50 shorter events, 10.2 us)
Async XLA Ops:
  0.6 1.7 copy-start
  5.1 16.7 %copy-start.6 = (s32[512]{0:T(512)S(1)}, s32[512]{0:T(512)}, u32[]{:S(2)}) copy-start(s32[512]{0:T(512)} %param.6) | copy-start | bytes 6148
  5.1 18.8 %copy-start.3 = (bf16[512,256]{1,0:T(8,128)(2,1)S(1)}, bf16[512,256]{1,0:T(8,128)(2,1)}, u32[]{:S(2)}) copy-start(bf16[512,256]{1,0:T(8,128)(2,1)} %param.4) | copy-start | bytes 786436
  5.1 115.4 %all-to-all-start = ((bf16[256,32,256]{2,1,0:T(8,128)(2,1)}), bf16[256,32,256]{2,1,0:T(8,128)(2,1)}, u32[]{:S(2)}, u32[]{:S(2)}) async-start(bf16[256,32,256]{2,1,0:T(8,128)(2,1)} %bitcast.116), calls=%async_computation | async-start | bytes 8388608 | tf_op jit(solution)/shard_map/all_to_all | solution.py:69
  24.8 17.3 %collective-permute-start = (bf16[640,256]{1,0:T(8,128)(2,1)}, bf16[640,256]{1,0:T(8,128)(2,1)S(1)}, u32[]{:S(2)}, u32[]{:S(2)}) collective-permute-start(bf16[640,256]{1,0:T(8,128)(2,1)} %get-tuple-element.20), channel_id=1, source_target_pairs={{0,1},{1,2},{2,3},{3,0},{4,5},{5,6},{6,7},{7,4},{8,9},{9,10},{10,1... | collective-permute-start | bytes 983048 | tf_op jit(solution)/shard_map/ppermute | solution.py:49
  26.2 29.5 %collective-permute-start.1 = (bf16[640,256]{1,0:T(8,128)(2,1)S(1)}, bf16[640,256]{1,0:T(8,128)(2,1)}, u32[]{:S(2)}, u32[]{:S(2)}) collective-permute-start(bf16[640,256]{1,0:T(8,128)(2,1)S(1)} %get-tuple-element.21), channel_id=1, source_target_pairs={{0,2},{1,3},{2,0},{3,1},{4,6},{5,7},{6,4},{7,5},{8,10},{9,11},{10,... | collective-permute-start | bytes 983048 | tf_op jit(solution)/shard_map/ppermute | solution.py:49
  28.6 27.1 %collective-permute-start.2 = (bf16[640,256]{1,0:T(8,128)(2,1)S(1)}, bf16[640,256]{1,0:T(8,128)(2,1)}, u32[]{:S(2)}, u32[]{:S(2)}) collective-permute-start(bf16[640,256]{1,0:T(8,128)(2,1)S(1)} %get-tuple-element.22), channel_id=1, source_target_pairs={{0,3},{1,0},{2,1},{3,2},{4,7},{5,4},{6,5},{7,6},{8,11},{9,8},{10,9... | collective-permute-start | bytes 983048 | tf_op jit(solution)/shard_map/ppermute | solution.py:49
  42.1 13.6 %copy-start.5 = (bf16[640,256]{1,0:T(8,128)(2,1)}, bf16[640,256]{1,0:T(8,128)(2,1)S(1)}, u32[]{:S(2)}) copy-start(bf16[640,256]{1,0:T(8,128)(2,1)S(1)} %collective-permute-done) | copy-start | bytes 983044
  125.5 2.0 copy-start.1
  129.0 4.1 %collective-permute-start.4 = (f32[3,512]{1,0:T(4,128)S(1)}, f32[3,512]{1,0:T(4,128)S(1)}, u32[]{:S(2)}, u32[]{:S(2)}) collective-permute-start(f32[3,512]{1,0:T(4,128)S(1)} %get-tuple-element.32), channel_id=1, source_target_pairs={{0,2},{1,3},{2,0},{3,1},{4,6},{5,7},{6,4},{7,5},{8,10},{9,11},{10,... | collective-permute-start | bytes 18440 | tf_op jit(solution)/shard_map/ppermute | solution.py:49
  129.1 4.0 %collective-permute-start.3 = (f32[3,512]{1,0:T(4,128)S(1)}, f32[3,512]{1,0:T(4,128)S(1)}, u32[]{:S(2)}, u32[]{:S(2)}) collective-permute-start(f32[3,512]{1,0:T(4,128)S(1)} %get-tuple-element.32), channel_id=1, source_target_pairs={{0,1},{1,2},{2,3},{3,0},{4,5},{5,6},{6,7},{7,4},{8,9},{9,10},{10,1... | collective-permute-start | bytes 18440 | tf_op jit(solution)/shard_map/ppermute | solution.py:49
  129.4 3.6 %collective-permute-start.5 = (f32[3,512]{1,0:T(4,128)S(1)}, f32[3,512]{1,0:T(4,128)S(1)}, u32[]{:S(2)}, u32[]{:S(2)}) collective-permute-start(f32[3,512]{1,0:T(4,128)S(1)} %get-tuple-element.32), channel_id=1, source_target_pairs={{0,3},{1,0},{2,1},{3,2},{4,7},{5,4},{6,5},{7,6},{8,11},{9,8},{10,9... | collective-permute-start | bytes 18440 | tf_op jit(solution)/shard_map/ppermute | solution.py:49
  141.2 108.6 %all-to-all-start.1 = ((bf16[256,32,256]{2,1,0:T(8,128)(2,1)}), bf16[256,32,256]{2,1,0:T(8,128)(2,1)}, u32[]{:S(2)}, u32[]{:S(2)}) async-start(bf16[256,32,256]{2,1,0:T(8,128)(2,1)} %bitcast.118), calls=%async_computation.1 | async-start | bytes 8388608 | tf_op jit(solution)/shard_map/all_to_all | solution.py:148
  151.3 15.3 %collective-permute-start.10 = (bf16[128,512]{1,0:T(8,128)(2,1)S(1)}, bf16[128,512]{1,0:T(8,128)(2,1)S(1)}, u32[]{:S(2)}, u32[]{:S(2)}) collective-permute-start(bf16[128,512]{1,0:T(8,128)(2,1)S(1)} %subtract_convert_fusion), channel_id=1, source_target_pairs={{0,2},{1,3},{2,0},{3,1},{4,6},{5,7},{6,4},{7,5},{8,10},{9,11},{10,... | collective-permute-start | bytes 393224 | tf_op jit(solution)/shard_map/ppermute | solution.py:49
  154.2 15.3 %collective-permute-start.9 = (bf16[128,512]{1,0:T(8,128)(2,1)S(1)}, bf16[128,512]{1,0:T(8,128)(2,1)S(1)}, u32[]{:S(2)}, u32[]{:S(2)}) collective-permute-start(bf16[128,512]{1,0:T(8,128)(2,1)S(1)} %subtract_convert_fusion), channel_id=1, source_target_pairs={{0,1},{1,2},{2,3},{3,0},{4,5},{5,6},{6,7},{7,4},{8,9},{9,10},{10,1... | collective-permute-start | bytes 393224 | tf_op jit(solution)/shard_map/ppermute | solution.py:49
  154.5 15.0 %collective-permute-start.11 = (bf16[128,512]{1,0:T(8,128)(2,1)S(1)}, bf16[128,512]{1,0:T(8,128)(2,1)S(1)}, u32[]{:S(2)}, u32[]{:S(2)}) collective-permute-start(bf16[128,512]{1,0:T(8,128)(2,1)S(1)} %subtract_convert_fusion), channel_id=1, source_target_pairs={{0,3},{1,0},{2,1},{3,2},{4,7},{5,4},{6,5},{7,6},{8,11},{9,8},{10,9... | collective-permute-start | bytes 393224 | tf_op jit(solution)/shard_map/ppermute | solution.py:49
  164.2 6.0 %copy-start.4 = (bf16[512,256]{1,0:T(8,128)(2,1)S(1)}, bf16[512,256]{1,0:T(8,128)(2,1)}, u32[]{:S(2)}) copy-start(bf16[512,256]{1,0:T(8,128)(2,1)} %param.4) | copy-start | bytes 786436
  165.7 23.0 %collective-permute-start.8 = (f32[512,256]{1,0:T(8,128)}, f32[512,256]{1,0:T(8,128)}, u32[]{:S(2)}, u32[]{:S(2)}) collective-permute-start(f32[512,256]{1,0:T(8,128)} %get-tuple-element.16), channel_id=1, source_target_pairs={{0,3},{1,0},{2,1},{3,2},{4,7},{5,4},{6,5},{7,6},{8,11},{9,8},{10,9... | collective-permute-start | bytes 1572872 | tf_op jit(solution)/shard_map/ppermute | solution.py:49
  165.7 23.5 %collective-permute-start.7 = (f32[512,256]{1,0:T(8,128)}, f32[512,256]{1,0:T(8,128)}, u32[]{:S(2)}, u32[]{:S(2)}) collective-permute-start(f32[512,256]{1,0:T(8,128)} %get-tuple-element.17), channel_id=1, source_target_pairs={{0,2},{1,3},{2,0},{3,1},{4,6},{5,7},{6,4},{7,5},{8,10},{9,11},{10,... | collective-permute-start | bytes 1572872 | tf_op jit(solution)/shard_map/ppermute | solution.py:49
  166.5 43.7 %collective-permute-start.6 = (f32[512,256]{1,0:T(8,128)}, f32[512,256]{1,0:T(8,128)}, u32[]{:S(2)}, u32[]{:S(2)}) collective-permute-start(f32[512,256]{1,0:T(8,128)} %get-tuple-element.18), channel_id=1, source_target_pairs={{0,1},{1,2},{2,3},{3,0},{4,5},{5,6},{6,7},{7,4},{8,9},{9,10},{10,1... | collective-permute-start | bytes 1572872 | tf_op jit(solution)/shard_map/ppermute | solution.py:49
  170.2 40.1 %copy-start.2 = (f32[1,512,256]{2,1,0:T(8,128)S(1)}, f32[1,512,256]{2,1,0:T(8,128)}, u32[]{:S(2)}) copy-start(f32[1,512,256]{2,1,0:T(8,128)} %get-tuple-element.15) | copy-start | bytes 1572868

commit v13 on v11

--- a/solution.py
+++ b/solution.py
@@ -6,7 +6,7 @@
 from jax.sharding import PartitionSpec as P
 
 PBS = 128
-PER = 8
+PER = 32
 
 def _segment_kernel(asked_ref, ret_ref, pos_ref, out_ref):
     step = pl.program_id(0)

time: 260 us -> 257 us (0.988)
  no operation moved by 1% of the time
where the time goes in v13:
time: 257 us
  waiting for transfers between devices  152 us (59%)
  starting transfers between devices  41.4 us (16%)
  matrix products  22.1 us (9%)
  other arithmetic  18.5 us (7%)
  local copies, waits for them, and re-layouts  14.8 us (6%)
  Pallas kernels  6.67 us (3%)
    ppermute x12, waiting for transfers between devices, from_sources(): lax.ppermute(payload(k), 'mp', [(i, (i + k) % n) for i in range(n)])  61.7 us
    all_to_all x1, waiting for transfers between devices, body(): lax.all_to_all(outgoing.reshape(dp_count * mp_count, quarter, shard_width...  59.8 us
    all_to_all x1, waiting for transfers between devices, body(): lax.all_to_all(sending.reshape(dp_count * mp_count, quarter, shard_width)...  30.5 us
    all_to_all x1, starting transfers between devices, body(): lax.all_to_all(outgoing.reshape(dp_count * mp_count, quarter, shard_width...  16.7 us
    ppermute x12, starting transfers between devices, from_sources(): lax.ppermute(payload(k), 'mp', [(i, (i + k) % n) for i in range(n)])  14.9 us
    all_to_all x1, starting transfers between devices, body(): lax.all_to_all(sending.reshape(dp_count * mp_count, quarter, shard_width)...  9.84 us
    dot_general x1, matrix products, body(): lax.dot_general(neg_grads, q4, (((2,), (0,)), ((), ())), preferred_elemen...  6.93 us
    pallas_call x1, Pallas kernels, segment_add(): pl.pallas_call(_segment_kernel, grid_spec=pltpu.PrefetchScalarGridSpec(nu...  6.67 us
  transfers between devices with their start and end apart: 14, of which 9 were waited for; matrix products, arithmetic and copies ran while one was open for 13% of the time, Pallas kernels for 0%

profile of v13, /device:TPU:1, one launch (start us, length us, event | category | flops | bytes accessed | tf_op | source)
XLA Modules:
  0.0 256.5 jit_solution(3518830197093170508)
XLA Ops:
  0.7 1.6 dynamic-slice_reduce_fusion
  2.3 2.8 %gather_fusion.2 = bf16[64,128,256]{2,1,0:T(8,128)(2,1)} fusion(bf16[32,128,256]{2,1,0:T(8,128)(2,1)S(1)} %bitcast.115, s32[1024]{0:T(1024)S(1)} %pad_clamp_fusion), kind=kCustom, calls=%fused_computation.2 | custom fusion | bytes 8388864 | tf_op jit(solution)/shard_map/jit(_take)/gather | solution.py:68
  5.1 16.7 %all-to-all-start = ((bf16[256,32,256]{2,1,0:T(8,128)(2,1)}), bf16[256,32,256]{2,1,0:T(8,128)(2,1)}, u32[]{:S(2)}, u32[]{:S(2)}) async-start(bf16[256,32,256]{2,1,0:T(8,128)(2,1)} %bitcast.116), calls=%async_computation | async-start | bytes 8388608 | tf_op jit(solution)/shard_map/all_to_all | solution.py:69
  21.9 2.0 gather_fusion
  24.8 1.4 collective-permute-start
  26.2 2.4 collective-permute-start.1
  30.5 11.6 %collective-permute-done = bf16[640,256]{1,0:T(8,128)(2,1)S(1)} collective-permute-done((bf16[640,256]{1,0:T(8,128)(2,1)}, bf16[640,256]{1,0:T(8,128)(2,1)S(1)}, u32[]{:S(2)}, u32[]{:S(2)}) %collective-permute-start) | collective-permute-done | bytes 327712 | tf_op jit(solution)/shard_map/ppermute | solution.py:49
  42.1 13.6 %collective-permute-done.1 = bf16[640,256]{1,0:T(8,128)(2,1)} collective-permute-done((bf16[640,256]{1,0:T(8,128)(2,1)S(1)}, bf16[640,256]{1,0:T(8,128)(2,1)}, u32[]{:S(2)}, u32[]{:S(2)}) %collective-permute-start.1) | collective-permute-done | bytes 327712 | tf_op jit(solution)/shard_map/ppermute | solution.py:49
  55.7 1.4 pad_maximum_fusion.1
  57.1 1.8 gather_fusion.1
  58.9 1.8 fusion.27
  60.7 59.8 %all-to-all-done = bf16[256,32,256]{2,1,0:T(8,128)(2,1)} async-done(((bf16[256,32,256]{2,1,0:T(8,128)(2,1)}), bf16[256,32,256]{2,1,0:T(8,128)(2,1)}, u32[]{:S(2)}, u32[]{:S(2)}) %all-to-all-start) | async-done | bytes 4194336 | tf_op jit(solution)/shard_map/all_to_all | solution.py:69
  120.5 5.0 %fusion.1 = (f32[512]{0:T(512)S(1)}, f32[64,32,512,1]{2,1,3,0:T(8,128)S(1)}) fusion(pred[64]{0:T(512)(128)(4,1)S(1)} %compare_bitcast_fusion, bf16[64,4,32,256]{3,2,1,0:T(8,128)(2,1)} %bitcast.11, bf16[4,640,256]{2,1,0:T(8,128)(2,1)} %gather_fusion.1), kind=kOutput, calls=%fused_computation.12 | convolution fusion | flops 2150628864 | bytes 9439296 | tf_op jit(solution)/shard_map/dot_general | solution.py:101
  125.5 2.0 copy-done.1
  127.5 1.3 select_reduce_fusion
  129.4 2.4 collective-permute-start.5
  134.3 6.9 %multiply_convert_fusion = bf16[64,32,4,256]{3,1,2,0:T(8,128)(2,1)} fusion(bf16[4,640,256]{2,1,0:T(8,128)(2,1)} %gather_fusion.1, f32[64,32,512,1]{2,1,3,0:T(8,128)} %copy-done.1, f32[512]{0:T(512)S(1)} %get-tuple-element.14, pred[64]{0:T(512)(128)(4,1)S(1)} %compare_bitcast_fusion), kind=kOutput, calls=%fused_computation.7 | convolution fusion | flops 2156920832 | bytes 9439296 | tf_op jit(solution)/shard_map/dot_general | solution.py:144
  141.2 9.8 %all-to-all-start.1 = ((bf16[256,32,256]{2,1,0:T(8,128)(2,1)}), bf16[256,32,256]{2,1,0:T(8,128)(2,1)}, u32[]{:S(2)}, u32[]{:S(2)}) async-start(bf16[256,32,256]{2,1,0:T(8,128)(2,1)} %bitcast.118), calls=%async_computation.1 | async-start | bytes 8388608 | tf_op jit(solution)/shard_map/all_to_all | solution.py:148
  151.3 3.0 %collective-permute-start.10 = (bf16[128,512]{1,0:T(8,128)(2,1)S(1)}, bf16[128,512]{1,0:T(8,128)(2,1)S(1)}, u32[]{:S(2)}, u32[]{:S(2)}) collective-permute-start(bf16[128,512]{1,0:T(8,128)(2,1)S(1)} %subtract_convert_fusion), channel_id=1, source_target_pairs={{0,2},{1,3},{2,0},{3,1},{4,6},{5,7},{6,4},{7,5},{8,10},{9,11},{10,... | collective-permute-start | bytes 393224 | tf_op jit(solution)/shard_map/ppermute | solution.py:49
  154.5 2.4 collective-permute-start.11
  156.9 1.4 fusion.14
  158.3 5.9 %fusion.3 = f32[512,4,256]{2,0,1:T(8,128)S(1)} fusion(f32[512,4,256]{2,0,1:T(8,128)S(1)} %fusion.14, bf16[64,4,32,256]{3,2,1,0:T(8,128)(2,1)} %bitcast.11, f32[64,32,512,1]{2,1,3,0:T(8,128)} %copy-done.1, f32[512]{0:T(512)S(1)} %get-tuple-element.14, pred[64]{0:T(512)(128)(4,1)S(1)} %compare_bitcast_fusion), kind=kOutput, calls=%fused_computation.15 | convolution fusion | flops 2153775104 | bytes 12585024 | tf_op jit(solution)/shard_map/dot_general | solution.py:129
  164.3 1.4 dynamic-slice_bitcast_fusion.3
  167.2 2.3 collective-permute-done.9
  171.3 6.0 %scatter_custom_fusion = f32[4096,256]{1,0:T(8,128)} fusion(s32[512]{0:T(512)S(1)} %compare_select_fusion, f32[512,256]{1,0:T(8,128)} %convolution_multiply_fusion, f32[]{:T(128)} %constant.103.clone.1), kind=kCustom, calls=%fused_computation.17 | custom fusion | flops 131072 | bytes 4194816 | tf_op jit(solution)/shard_map/scatter-add | solution.py:161
  177.3 11.3 %collective-permute-done.8 = f32[512,256]{1,0:T(8,128)} collective-permute-done((f32[512,256]{1,0:T(8,128)}, f32[512,256]{1,0:T(8,128)}, u32[]{:S(2)}, u32[]{:S(2)}) %collective-permute-start.8) | collective-permute-done | bytes 524320 | tf_op jit(solution)/shard_map/ppermute | solution.py:49
  189.2 21.1 %collective-permute-done.6 = f32[512,256]{1,0:T(8,128)} collective-permute-done((f32[512,256]{1,0:T(8,128)}, f32[512,256]{1,0:T(8,128)}, u32[]{:S(2)}, u32[]{:S(2)}) %collective-permute-start.6) | collective-permute-done | bytes 524320 | tf_op jit(solution)/shard_map/ppermute | solution.py:49
  210.3 2.8 %pad_maximum_fusion = f32[4,512,256]{2,1,0:T(8,128)} fusion(f32[1,512,256]{2,1,0:T(8,128)} %bitcast.33, f32[1,512,256]{2,1,0:T(8,128)} %bitcast.31, f32[1,512,256]{2,1,0:T(8,128)} %bitcast.29, f32[1,512,256]{2,1,0:T(8,128)S(1)} %copy-done.2), kind=kLoop, calls=%fused_computation.16 | loop fusion | flops 1572864 | bytes 4194304 | tf_op jit(solution)/shard_map/stack | solution.py:52
  213.1 3.6 %gather_fusion.4 = f32[4,512,256]{2,1,0:T(8,128)} fusion(f32[4,512,256]{2,1,0:T(8,128)} %pad_maximum_fusion, s32[1024]{0:T(1024)S(1)} %pad_clamp_fusion.1), kind=kCustom, calls=%fused_computation.4 | custom fusion | bytes 4194320 | tf_op jit(solution)/shard_map/jit(_take)/gather | solution.py:52
  216.8 2.6 %reduce_sum.59 = f32[512,256]{1,0:T(8,128)} reduce(f32[4,512,256]{2,1,0:T(8,128)} %gather_fusion.4, f32[]{:T(128)} %constant.103.clone.1), dimensions={0}, to_apply=%region_8.9 | reduce | flops 393216 | bytes 2621444 | tf_op jit(solution)/shard_map/reduce_sum | solution.py:133
  219.3 30.5 %all-to-all-done.1 = bf16[256,32,256]{2,1,0:T(8,128)(2,1)} async-done(((bf16[256,32,256]{2,1,0:T(8,128)(2,1)}), bf16[256,32,256]{2,1,0:T(8,128)(2,1)}, u32[]{:S(2)}, u32[]{:S(2)}) %all-to-all-start.1) | async-done | bytes 4194336 | tf_op jit(solution)/shard_map/all_to_all | solution.py:148
  249.8 6.7 %shard_map.67 = f32[32,128,256]{2,1,0:T(8,128)} custom-call(s32[64]{0:T(128)} %get-tuple-element.9.asked_ref, bf16[64,128,256]{2,1,0:T(8,128)(2,1)} %bitcast.38.ret_ref, f32[32,128,256]{2,1,0:T(8,128)} %bitcast.117), custom_call_target="tpu_custom_call" | custom-call | flops 2097152 | bytes 12582912 | tf_op jit(solution)/shard_map/pallas_call | solution.py:29
  (50 shorter events, 10.2 us)
Async XLA Ops:
  0.6 1.7 copy-start
  5.1 16.7 %copy-start.6 = (s32[512]{0:T(512)S(1)}, s32[512]{0:T(512)}, u32[]{:S(2)}) copy-start(s32[512]{0:T(512)} %param.6) | copy-start | bytes 6148
  5.1 18.8 %copy-start.3 = (bf16[512,256]{1,0:T(8,128)(2,1)S(1)}, bf16[512,256]{1,0:T(8,128)(2,1)}, u32[]{:S(2)}) copy-start(bf16[512,256]{1,0:T(8,128)(2,1)} %param.4) | copy-start | bytes 786436
  5.1 115.4 %all-to-all-start = ((bf16[256,32,256]{2,1,0:T(8,128)(2,1)}), bf16[256,32,256]{2,1,0:T(8,128)(2,1)}, u32[]{:S(2)}, u32[]{:S(2)}) async-start(bf16[256,32,256]{2,1,0:T(8,128)(2,1)} %bitcast.116), calls=%async_computation | async-start | bytes 8388608 | tf_op jit(solution)/shard_map/all_to_all | solution.py:69
  24.8 17.3 %collective-permute-start = (bf16[640,256]{1,0:T(8,128)(2,1)}, bf16[640,256]{1,0:T(8,128)(2,1)S(1)}, u32[]{:S(2)}, u32[]{:S(2)}) collective-permute-start(bf16[640,256]{1,0:T(8,128)(2,1)} %get-tuple-element.20), channel_id=1, source_target_pairs={{0,1},{1,2},{2,3},{3,0},{4,5},{5,6},{6,7},{7,4},{8,9},{9,10},{10,1... | collective-permute-start | bytes 983048 | tf_op jit(solution)/shard_map/ppermute | solution.py:49
  26.2 29.5 %collective-permute-start.1 = (bf16[640,256]{1,0:T(8,128)(2,1)S(1)}, bf16[640,256]{1,0:T(8,128)(2,1)}, u32[]{:S(2)}, u32[]{:S(2)}) collective-permute-start(bf16[640,256]{1,0:T(8,128)(2,1)S(1)} %get-tuple-element.21), channel_id=1, source_target_pairs={{0,2},{1,3},{2,0},{3,1},{4,6},{5,7},{6,4},{7,5},{8,10},{9,11},{10,... | collective-permute-start | bytes 983048 | tf_op jit(solution)/shard_map/ppermute | solution.py:49
  28.6 27.1 %collective-permute-start.2 = (bf16[640,256]{1,0:T(8,128)(2,1)S(1)}, bf16[640,256]{1,0:T(8,128)(2,1)}, u32[]{:S(2)}, u32[]{:S(2)}) collective-permute-start(bf16[640,256]{1,0:T(8,128)(2,1)S(1)} %get-tuple-element.22), channel_id=1, source_target_pairs={{0,3},{1,0},{2,1},{3,2},{4,7},{5,4},{6,5},{7,6},{8,11},{9,8},{10,9... | collective-permute-start | bytes 983048 | tf_op jit(solution)/shard_map/ppermute | solution.py:49
  42.1 13.6 %copy-start.5 = (bf16[640,256]{1,0:T(8,128)(2,1)}, bf16[640,256]{1,0:T(8,128)(2,1)S(1)}, u32[]{:S(2)}) copy-start(bf16[640,256]{1,0:T(8,128)(2,1)S(1)} %collective-permute-done) | copy-start | bytes 983044
  125.5 2.0 copy-start.1
  129.0 4.1 %collective-permute-start.4 = (f32[3,512]{1,0:T(4,128)S(1)}, f32[3,512]{1,0:T(4,128)S(1)}, u32[]{:S(2)}, u32[]{:S(2)}) collective-permute-start(f32[3,512]{1,0:T(4,128)S(1)} %get-tuple-element.32), channel_id=1, source_target_pairs={{0,2},{1,3},{2,0},{3,1},{4,6},{5,7},{6,4},{7,5},{8,10},{9,11},{10,... | collective-permute-start | bytes 18440 | tf_op jit(solution)/shard_map/ppermute | solution.py:49
  129.1 4.0 %collective-permute-start.3 = (f32[3,512]{1,0:T(4,128)S(1)}, f32[3,512]{1,0:T(4,128)S(1)}, u32[]{:S(2)}, u32[]{:S(2)}) collective-permute-start(f32[3,512]{1,0:T(4,128)S(1)} %get-tuple-element.32), channel_id=1, source_target_pairs={{0,1},{1,2},{2,3},{3,0},{4,5},{5,6},{6,7},{7,4},{8,9},{9,10},{10,1... | collective-permute-start | bytes 18440 | tf_op jit(solution)/shard_map/ppermute | solution.py:49
  129.4 3.6 %collective-permute-start.5 = (f32[3,512]{1,0:T(4,128)S(1)}, f32[3,512]{1,0:T(4,128)S(1)}, u32[]{:S(2)}, u32[]{:S(2)}) collective-permute-start(f32[3,512]{1,0:T(4,128)S(1)} %get-tuple-element.32), channel_id=1, source_target_pairs={{0,3},{1,0},{2,1},{3,2},{4,7},{5,4},{6,5},{7,6},{8,11},{9,8},{10,9... | collective-permute-start | bytes 18440 | tf_op jit(solution)/shard_map/ppermute | solution.py:49
  141.2 108.6 %all-to-all-start.1 = ((bf16[256,32,256]{2,1,0:T(8,128)(2,1)}), bf16[256,32,256]{2,1,0:T(8,128)(2,1)}, u32[]{:S(2)}, u32[]{:S(2)}) async-start(bf16[256,32,256]{2,1,0:T(8,128)(2,1)} %bitcast.118), calls=%async_computation.1 | async-start | bytes 8388608 | tf_op jit(solution)/shard_map/all_to_all | solution.py:148
  151.3 15.3 %collective-permute-start.10 = (bf16[128,512]{1,0:T(8,128)(2,1)S(1)}, bf16[128,512]{1,0:T(8,128)(2,1)S(1)}, u32[]{:S(2)}, u32[]{:S(2)}) collective-permute-start(bf16[128,512]{1,0:T(8,128)(2,1)S(1)} %subtract_convert_fusion), channel_id=1, source_target_pairs={{0,2},{1,3},{2,0},{3,1},{4,6},{5,7},{6,4},{7,5},{8,10},{9,11},{10,... | collective-permute-start | bytes 393224 | tf_op jit(solution)/shard_map/ppermute | solution.py:49
  154.2 15.3 %collective-permute-start.9 = (bf16[128,512]{1,0:T(8,128)(2,1)S(1)}, bf16[128,512]{1,0:T(8,128)(2,1)S(1)}, u32[]{:S(2)}, u32[]{:S(2)}) collective-permute-start(bf16[128,512]{1,0:T(8,128)(2,1)S(1)} %subtract_convert_fusion), channel_id=1, source_target_pairs={{0,1},{1,2},{2,3},{3,0},{4,5},{5,6},{6,7},{7,4},{8,9},{9,10},{10,1... | collective-permute-start | bytes 393224 | tf_op jit(solution)/shard_map/ppermute | solution.py:49
  154.5 15.0 %collective-permute-start.11 = (bf16[128,512]{1,0:T(8,128)(2,1)S(1)}, bf16[128,512]{1,0:T(8,128)(2,1)S(1)}, u32[]{:S(2)}, u32[]{:S(2)}) collective-permute-start(bf16[128,512]{1,0:T(8,128)(2,1)S(1)} %subtract_convert_fusion), channel_id=1, source_target_pairs={{0,3},{1,0},{2,1},{3,2},{4,7},{5,4},{6,5},{7,6},{8,11},{9,8},{10,9... | collective-permute-start | bytes 393224 | tf_op jit(solution)/shard_map/ppermute | solution.py:49
  164.2 6.0 %copy-start.4 = (bf16[512,256]{1,0:T(8,128)(2,1)S(1)}, bf16[512,256]{1,0:T(8,128)(2,1)}, u32[]{:S(2)}) copy-start(bf16[512,256]{1,0:T(8,128)(2,1)} %param.4) | copy-start | bytes 786436
  165.7 23.0 %collective-permute-start.8 = (f32[512,256]{1,0:T(8,128)}, f32[512,256]{1,0:T(8,128)}, u32[]{:S(2)}, u32[]{:S(2)}) collective-permute-start(f32[512,256]{1,0:T(8,128)} %get-tuple-element.16), channel_id=1, source_target_pairs={{0,3},{1,0},{2,1},{3,2},{4,7},{5,4},{6,5},{7,6},{8,11},{9,8},{10,9... | collective-permute-start | bytes 1572872 | tf_op jit(solution)/shard_map/ppermute | solution.py:49
  165.7 23.5 %collective-permute-start.7 = (f32[512,256]{1,0:T(8,128)}, f32[512,256]{1,0:T(8,128)}, u32[]{:S(2)}, u32[]{:S(2)}) collective-permute-start(f32[512,256]{1,0:T(8,128)} %get-tuple-element.17), channel_id=1, source_target_pairs={{0,2},{1,3},{2,0},{3,1},{4,6},{5,7},{6,4},{7,5},{8,10},{9,11},{10,... | collective-permute-start | bytes 1572872 | tf_op jit(solution)/shard_map/ppermute | solution.py:49
  166.5 43.7 %collective-permute-start.6 = (f32[512,256]{1,0:T(8,128)}, f32[512,256]{1,0:T(8,128)}, u32[]{:S(2)}, u32[]{:S(2)}) collective-permute-start(f32[512,256]{1,0:T(8,128)} %get-tuple-element.18), channel_id=1, source_target_pairs={{0,1},{1,2},{2,3},{3,0},{4,5},{5,6},{6,7},{7,4},{8,9},{9,10},{10,1... | collective-permute-start | bytes 1572872 | tf_op jit(solution)/shard_map/ppermute | solution.py:49
  170.2 40.1 %copy-start.2 = (f32[1,512,256]{2,1,0:T(8,128)S(1)}, f32[1,512,256]{2,1,0:T(8,128)}, u32[]{:S(2)}) copy-start(f32[1,512,256]{2,1,0:T(8,128)} %get-tuple-element.15) | copy-start | bytes 1572868
